TPU v7x, 128 devices: a whole 4x4x4 slice. The times are simulated.
128 devices in a mesh: slab: 32 (over z, y, x_hi), head: 4 (over x_lo, core).
Axes of the slice: x: 4 (x_hi: 2, x_lo: 2; x = x_hi * 2 + x_lo), y: 4, z: 4, core: 2. Of those that a mesh axis runs over, the one named last changes fastest.
Arguments:
- tokens: bfloat16 [65536, 384], P(('slab', 'head')), may hold values from -6 to 6
- norm_gain: float32 [384], replicated, may hold values from 0.25 to 1.75
- w_qkv: bfloat16 [3, 384, 384], replicated, may hold values from -0.3125 to 0.3125
- w_out: bfloat16 [384, 384], replicated, may hold values from -0.625 to 0.625
- cotangent: bfloat16 [65536, 384], P(('slab', 'head')), may hold values from -6 to 6
- neighbours: int32 [512, 8], P('slab'), may hold values from 0 to 511, as said below
- counts: int32 [512], P('slab'), may hold values from 2 to 8, as said below
Outputs:
- output: bfloat16 [65536, 384], P(('slab', 'head'))
- d_tokens: bfloat16 [65536, 384], P(('slab', 'head'))
- d_w_qkv: float32 [3, 384, 384], P(None, None, 'head')
- d_w_out: float32 [384, 384], replicated
- d_gain: float32 [384], replicated
Inputs may be any that keep to these rules, and one draw needn't show every extreme that they name: `neighbours`: entry 0 of block b's list is b itself; the entries of a list are distinct and each lies within 16 blocks of b along the periodic block order (modulo 512); every block lists one block at distance exactly 16. Only the first counts[b] slots of block b's list are live; the first block of every slab has all 8 live.
All inputs are finite; a program needn't handle non-finite values.
Results may differ from a plain program's by a relative error of at most 0.024.
Values may be sent and summed in bfloat16 or wider, within the bound.
No kernel may reach another device: no remote copies, remote signals or barrier semaphores. Data moves between devices by JAX's collectives and lax.ppermute only.
A program may use at most 192 MiB of HBM per device.

v0:
```python
import math

import jax
import jax.numpy as jnp
from jax import lax
from jax.sharding import PartitionSpec as P

HEADS = 12
BLK = 128
REACH = 16


exponent_divisor = 10.0
norm_eps = 1e-06


def padded(value, sides, width):
    for axis, dim in sides:
        size, length = (lax.axis_size(axis), value.shape[dim])
        up = [(i, (i + 1) % size) for i in range(size)]
        down = [(j, i) for i, j in up]
        last = lax.slice_in_dim(value, length - width, length, axis=dim)
        first = lax.slice_in_dim(value, 0, width, axis=dim)
        before = lax.ppermute(last, axis, up)
        after = lax.ppermute(first, axis, down)
        value = jnp.concatenate([before, value, after], axis=dim)
    return value


def passed_along(value, axis, steps):
    count = lax.axis_size(axis)
    pairs = [(source, (source + steps) % count) for source in range(count)]
    return lax.ppermute(value, axis, pairs)


def normalize(projected, head_dim):
    by_head = projected.reshape(projected.shape[:-1] + (projected.shape[-1] // head_dim, head_dim))
    length = jnp.sqrt(jnp.sum(by_head * by_head, -1, keepdims=True))
    divisor = jnp.maximum(length, 0.7 * math.sqrt(head_dim))
    return (by_head / divisor, divisor, length > 0.7 * math.sqrt(head_dim))


def unit_heads(projected, head_dim):
    unit, divisor, active = normalize(projected, head_dim)
    return unit.reshape(projected.shape)


def norm_back(projected, grad, head_dim):
    unit, divisor, active = normalize(projected, head_dim)
    along = grad.astype(jnp.float32).reshape(unit.shape)
    inner = jnp.sum(unit * along, -1, keepdims=True)
    result = (along - jnp.where(active, unit * inner, 0.0)) / divisor
    return result.reshape(projected.shape)


def attention_weights(asking_matrix, lookup_matrix, counts):
    slot_ids = jnp.arange(lookup_matrix.shape[1], dtype=jnp.int32) // asking_matrix.shape[1]
    raw_affinity = exponent_divisor * jnp.einsum(
        "pcxt,pqxt->pxcq", asking_matrix, lookup_matrix, preferred_element_type=jnp.float32
    )
    live_mask = (slot_ids[None, :] < counts[:, None]).astype(jnp.float32)
    raised = jnp.exp(raw_affinity) * live_mask[:, None, None, :]
    return raised / jnp.sum(raised, -1, keepdims=True)


def local(tokens, norm_gain, w_qkv, w_out, cotangent, neighbours, counts):
    width = tokens.shape[1]
    head_dim = width // HEADS
    n_head = lax.axis_size("head")
    n_slab = lax.axis_size("slab")
    head_cols = width // n_head
    heads_here = HEADS // n_head
    head_index = lax.axis_index("head")
    slab_index = lax.axis_index("slab")
    slab_blocks, n_slots = neighbours.shape
    block_rows = BLK
    slab_rows = slab_blocks * block_rows
    tok_f32 = tokens.astype(jnp.float32)
    inverse = lax.rsqrt(jnp.mean(tok_f32 * tok_f32, -1, keepdims=True) + norm_eps)
    normed = (tok_f32 * inverse * norm_gain).astype(jnp.bfloat16)
    w_here = lax.dynamic_slice_in_dim(w_qkv, head_index * head_cols, head_cols, 2)
    gathered = lax.all_gather(normed, "head", axis=0, tiled=True)
    projected = jnp.einsum("rd,cde->cre", gathered, w_here, preferred_element_type=jnp.float32)
    packed = jnp.stack(
        [unit_heads(projected[0], head_dim), unit_heads(projected[1], head_dim), projected[2]]
    ).astype(jnp.bfloat16)
    q_heads = packed[0]
    keys_values = packed[1:]
    extended = padded(keys_values, (("slab", 1),), REACH * block_rows)
    ext_blocks = slab_blocks + 2 * REACH
    n_blocks = slab_blocks * n_slab
    lookup = (neighbours - slab_index * slab_blocks + REACH) % n_blocks
    group_size = 8
    n_groups = slab_blocks // group_size
    key_blocks = extended.reshape(2, ext_blocks, block_rows, heads_here, head_dim)
    query_groups = q_heads.reshape(n_groups, group_size, block_rows, heads_here, head_dim)
    lookup_groups = lookup.reshape(n_groups, group_size, n_slots)
    count_groups = counts.reshape(n_groups, group_size)

    def fetch(lookup_rows):
        both = key_blocks[:, lookup_rows.reshape(-1)]
        return both.reshape(2, group_size, n_slots * block_rows, heads_here, head_dim)

    def attend(inputs):
        asking_matrix, lookup_rows, live = inputs
        both = fetch(lookup_rows)
        weights_bf = attention_weights(asking_matrix, both[0], live).astype(jnp.bfloat16)
        result = jnp.einsum(
            "ghqk,gkhd->gqhd", weights_bf, both[1], preferred_element_type=jnp.float32
        )
        return result.astype(jnp.bfloat16)

    attended_heads = lax.map(attend, (query_groups, lookup_groups, count_groups)).reshape(
        slab_rows, head_cols
    )
    attended = lax.all_to_all(attended_heads, "head", split_axis=0, concat_axis=1, tiled=True)
    output = (tok_f32 + jnp.dot(attended, w_out, preferred_element_type=jnp.float32)).astype(
        jnp.bfloat16
    )
    d_out_part = jnp.dot(attended.T, cotangent, preferred_element_type=jnp.float32)
    d_attended = jnp.dot(cotangent, w_out.T, preferred_element_type=jnp.float32).astype(
        jnp.bfloat16
    )
    d_heads = lax.all_to_all(d_attended, "head", split_axis=1, concat_axis=0, tiled=True)
    d_groups = d_heads.reshape(n_groups, group_size, block_rows, heads_here, head_dim)

    def backward_group(grad_buffer, inputs):
        asking_matrix, d_attn, lookup_rows, live = inputs
        both = fetch(lookup_rows)
        normalized_affinity = attention_weights(asking_matrix, both[0], live)
        weights_bf = normalized_affinity.astype(jnp.bfloat16)
        affinity_share_cotangent = jnp.einsum(
            "pcxt,pqxt->pxcq", d_attn, both[1], preferred_element_type=jnp.float32
        )
        pairwise_dot_sum = jnp.sum(
            affinity_share_cotangent * normalized_affinity, -1, keepdims=True
        )
        affinity_cotangent = (
            exponent_divisor * normalized_affinity * (affinity_share_cotangent - pairwise_dot_sum)
        ).astype(jnp.bfloat16)
        d_query = jnp.einsum(
            "ghqk,gkhd->gqhd", affinity_cotangent, both[0], preferred_element_type=jnp.float32
        )
        d_keys = jnp.einsum(
            "ghqk,gqhd->gkhd", affinity_cotangent, asking_matrix, preferred_element_type=jnp.float32
        )
        d_values = jnp.einsum(
            "ghqk,gqhd->gkhd", weights_bf, d_attn, preferred_element_type=jnp.float32
        )
        stacked = jnp.stack([d_keys, d_values]).reshape(
            2, group_size * n_slots, block_rows, heads_here, head_dim
        )
        grad_buffer = grad_buffer.at[:, lookup_rows.reshape(-1)].add(stacked)
        return (grad_buffer, d_query)

    start_buffer = jnp.zeros((2, ext_blocks, block_rows, heads_here, head_dim), jnp.float32)
    grad_buffer, d_query_groups = lax.scan(
        backward_group, start_buffer, (query_groups, d_groups, lookup_groups, count_groups)
    )
    low_rim = grad_buffer[:, :REACH]
    high_rim = grad_buffer[:, REACH + slab_blocks :]
    from_above = passed_along(low_rim.astype(jnp.bfloat16), "slab", -1).astype(low_rim.dtype)
    from_below = passed_along(high_rim, "slab", 1)
    own_grads = grad_buffer[:, REACH : REACH + slab_blocks]
    own_grads = own_grads.at[:, slab_blocks - REACH :].add(from_above)
    own_grads = own_grads.at[:, :REACH].add(from_below)
    d_packed = jnp.concatenate(
        [
            d_query_groups.reshape(1, slab_rows, head_cols),
            own_grads.reshape(2, slab_rows, head_cols),
        ],
        0,
    ).astype(jnp.bfloat16)
    d_query_part = norm_back(projected[0], d_packed[0], head_dim).astype(jnp.bfloat16)
    d_key_part = norm_back(projected[1], d_packed[1], head_dim).astype(jnp.bfloat16)
    d_qkv = jnp.stack([d_query_part, d_key_part, d_packed[2]])
    d_normed = lax.psum_scatter(
        jnp.einsum("crk,cdk->rd", d_qkv, w_here, preferred_element_type=jnp.float32).astype(
            jnp.bfloat16
        ),
        "head",
        scatter_dimension=0,
        tiled=True,
    ).astype(jnp.float32)
    d_qkv_part = jnp.einsum("rd,crk->cdk", gathered, d_qkv, preferred_element_type=jnp.float32)
    d_w_qkv = lax.psum(d_qkv_part.astype(jnp.bfloat16), "slab").astype(jnp.float32)
    d_gain_part = jnp.sum(d_normed * tok_f32 * inverse, 0)
    d_w_out, d_gain = lax.psum((d_out_part, d_gain_part), ("slab", "head"))
    scaled = d_normed * norm_gain
    d_tokens = (
        cotangent.astype(jnp.float32)
        + inverse * scaled
        - tok_f32 * inverse**3 * jnp.mean(scaled * tok_f32, -1, keepdims=True)
    )
    return (output, d_tokens.astype(jnp.bfloat16), d_w_qkv, d_w_out, d_gain)


def solution(mesh):
    placed = (
        P(("slab", "head"), None),
        P(),
        P(),
        P(),
        P(("slab", "head"), None),
        P("slab", None),
        P("slab"),
    )
    return jax.shard_map(
        local,
        mesh=mesh,
        in_specs=placed,
        out_specs=(
            P(("slab", "head"), None),
            P(("slab", "head"), None),
            P(None, None, "head"),
            P(),
            P(),
        ),
        check_vma=False,
    )
```

profile of v0, /device:TPU:1, one launch (start us, length us, event | category | flops | bytes accessed | tf_op | source)
XLA Modules:
  0.0 983.4 jit_solution(14949029409133314243)
XLA Ops:
  11.5 28.5 %all-gather.2.cloned.1.call-done = bf16[2048,384]{1,0:T(8,128)(2,1)} async-done(((bf16[512,384]{1,0:T(8,128)(2,1)}), bf16[2048,384]{1,0:T(8,128)(2,1)}) %all-gather.2.cloned.1.call-update) | async-done | bytes 1572880 | tf_op jit(solution)/shard_map/all_gather | solution.py:82
  57.7 28.7 %all-to-all-done.1 = bf16[512,4,96]{0,2,1:T(8,128)(2,1)S(1)} async-done(((bf16[512,4,96]{0,2,1:T(8,128)(2,1)}), bf16[512,4,96]{0,2,1:T(8,128)(2,1)S(1)}, u32[]{:S(2)}, u32[]{:S(2)}) %all-to-all-start.1) | async-done | bytes 393248 | tf_op jit(solution)/shard_map/all_to_all | solution.py:124
  90.6 13.4 %copy.64 = bf16[2,48,128,3,32]{4,3,2,1,0:T(4,128)(2,1)} copy(bf16[2,48,128,3,32]{2,1,4,3,0:T(8,128)(2,1)} %bitcast.220) | data formatting | bytes 4718592 | tf_op jit(solution)/shard_map/while | solution.py:113
  106.8 270.8 %while.31 = (s32[]{:T(128)}, f32[2,48,128,3,32]{2,4,3,1,0:T(8,128)}, bf16[2,8,128,3,32]{2,4,3,1,0:T(8,128)(2,1)}, s32[2,8,8]{2,1,0:T(8,128)S(1)}, bf16[2,8,128,3...) while((s32[]{:T(128)}, ...), condition=%wide.region_10.11_spmd, body=%wide.region_6.10_spmd.sunk | while | flops 1069567168 | bytes 201579056 | solution.py:157
  120.9 20.9 %gather_fusion.1 = bf16[64,2,128,3,32]{4,3,2,1,0:T(4,128)(2,1)} fusion(bf16[2,48,128,3,32]{4,3,2,1,0:T(4,128)(2,1)} %get-tuple-element.475, s32[1024]{0:T(1024)S(1)} %pad_clamp_fusion.5), kind=kCustom, calls=%fused_computation.1.clone.1 | custom fusion | bytes 6291712 | tf_op jit(solution)/shard_map/while/body/eval_jaxpr/gather | solution.py:101
  141.8 16.0 %fusion.128 = (bf16[1,64,128,3,32]{4,3,2,0,1:T(4,128)(2,1)}, bf16[1,64,128,3,32]{4,3,2,0,1:T(4,128)(2,1)}) fusion(bf16[2,64,128,3,32]{4,3,2,0,1:T(4,128)(2,1)} %bitcast.214), kind=kLoop, calls=%fused_computation.145.clone.1 | loop fusion | bytes 6291456 | tf_op jit(solution)/shard_map/while/body/eval_jaxpr/slice | solution.py:133
  157.8 10.5 %copy.130 = bf16[8,1024,3,32]{1,3,2,0:T(8,128)(2,1)S(1)} copy(bf16[8,1024,3,32]{3,2,1,0:T(4,128)(2,1)} %bitcast.216) | data formatting | bytes 3145728 | tf_op jit(solution)/shard_map/while/body/eval_jaxpr/squeeze | solution.py:130
  175.1 12.4 %multiply_reduce_fusion.6 = (f32[8,3,128]{2,1,0:T(4,128)S(1)}, f32[8,3,128,1024]{3,2,1,0:T(8,128)}) fusion(f32[8,3,128]{2,1,0:T(4,128)S(1)} %get-tuple-element.427, f32[8,1024]{1,0:T(8,128)S(1)} %compare_convert_fusion.5, f32[8,3,128,1024]{3,2,1,0:T(8,128)} %get-tuple-element.426, bf16[8,1024,3,32]{3,2,1,0:T(4,128)(2,1)S(1)} %bitcast.218, ...), kind=kOutput, calls=%fused_computation.32.clone.1 | convolution fusion | flops 217052160 | bytes 26992640 | tf_op jit(solution)/shard_map/while/body/eval_jaxpr/pcxt,pqxt->pxcq/dot_general | solution.py:132
  232.4 16.7 %scatter_fusion = f32[2,48,128,3,32]{2,4,3,1,0:T(8,128)} fusion(f32[2,48,128,3,32]{2,4,3,1,0:T(8,128)} %get-tuple-element.462, s32[64]{0:T(128)S(1)} %fusion.126, f32[64,2,128,3,32]{2,4,3,1,0:T(8,128)} %copy.133), kind=kCustom, calls=%fused_computation.2.clone.1 | custom fusion | flops 1572864 | bytes 18874624 | tf_op jit(solution)/shard_map/while/body/eval_jaxpr/scatter-add | solution.py:153
  249.1 20.9 %gather_fusion.1 = bf16[64,2,128,3,32]{4,3,2,1,0:T(4,128)(2,1)} fusion(bf16[2,48,128,3,32]{4,3,2,1,0:T(4,128)(2,1)} %get-tuple-element.475, s32[1024]{0:T(1024)S(1)} %pad_clamp_fusion.5), kind=kCustom, calls=%fused_computation.1.clone.1 | custom fusion | bytes 6291712 | tf_op jit(solution)/shard_map/while/body/eval_jaxpr/gather | solution.py:101
  270.0 16.0 %fusion.128 = (bf16[1,64,128,3,32]{4,3,2,0,1:T(4,128)(2,1)}, bf16[1,64,128,3,32]{4,3,2,0,1:T(4,128)(2,1)}) fusion(bf16[2,64,128,3,32]{4,3,2,0,1:T(4,128)(2,1)} %bitcast.214), kind=kLoop, calls=%fused_computation.145.clone.1 | loop fusion | bytes 6291456 | tf_op jit(solution)/shard_map/while/body/eval_jaxpr/slice | solution.py:133
  303.3 12.4 %multiply_reduce_fusion.6 = (f32[8,3,128]{2,1,0:T(4,128)S(1)}, f32[8,3,128,1024]{3,2,1,0:T(8,128)}) fusion(f32[8,3,128]{2,1,0:T(4,128)S(1)} %get-tuple-element.427, f32[8,1024]{1,0:T(8,128)S(1)} %compare_convert_fusion.5, f32[8,3,128,1024]{3,2,1,0:T(8,128)} %get-tuple-element.426, bf16[8,1024,3,32]{3,2,1,0:T(4,128)(2,1)S(1)} %bitcast.218, ...), kind=kOutput, calls=%fused_computation.32.clone.1 | convolution fusion | flops 217052160 | bytes 26992640 | tf_op jit(solution)/shard_map/while/body/eval_jaxpr/pcxt,pqxt->pxcq/dot_general | solution.py:132
  360.6 16.6 %scatter_fusion = f32[2,48,128,3,32]{2,4,3,1,0:T(8,128)} fusion(f32[2,48,128,3,32]{2,4,3,1,0:T(8,128)} %get-tuple-element.462, s32[64]{0:T(128)S(1)} %fusion.126, f32[64,2,128,3,32]{2,4,3,1,0:T(8,128)} %copy.133), kind=kCustom, calls=%fused_computation.2.clone.1 | custom fusion | flops 1572864 | bytes 18874624 | tf_op jit(solution)/shard_map/while/body/eval_jaxpr/scatter-add | solution.py:153
  396.2 38.9 %collective-permute-done.2 = bf16[2,16,128,3,32]{2,4,3,1,0:T(8,128)(2,1)} collective-permute-done((bf16[2,16,128,3,32]{2,4,3,1,0:T(8,128)(2,1)}, bf16[2,16,128,3,32]{2,4,3,1,0:T(8,128)(2,1)}, u32[]{:S(2)}, u32[]{:S(2)}) %collective-permute-start.2) | collective-permute-done | bytes 786464 | tf_op jit(solution)/shard_map/ppermute | solution.py:33
  455.3 102.4 %while.30 = (s32[]{:T(128)}, bf16[2,8,128,3,32]{2,1,0,4,3:T(8,128)(2,1)S(1)}, s32[2,8,8]{2,1,0:T(8,128)S(1)}, bf16[2,48,128,3,32]{4,3,2,1,0:T(4,128)(2,1)}, bf16...) while((s32[]{:T(128)}, bf16[2,8,128,3,32]{2,1,0,4,3:T(8,128)(2,1)S(1)}, ...), condition=%wide.region_5.6_spmd, body=%wide.region_3.5_spmd.sunk | while | flops 424794304 | bytes 48634044 | solution.py:113
  455.6 20.9 %gather_fusion = bf16[64,2,128,3,32]{4,3,2,1,0:T(4,128)(2,1)} fusion(bf16[2,48,128,3,32]{4,3,2,1,0:T(4,128)(2,1)} %get-tuple-element.448, s32[1024]{0:T(1024)S(1)} %pad_clamp_fusion.4), kind=kCustom, calls=%fused_computation.clone.1 | custom fusion | bytes 6291712 | tf_op jit(solution)/shard_map/while/body/eval_jaxpr/gather | solution.py:101
  476.5 13.1 %fusion.117 = (bf16[1,64,128,3,32]{4,3,2,0,1:T(4,128)(2,1)}, bf16[1,64,128,3,32]{4,3,2,0,1:T(4,128)(2,1)S(1)}) fusion(bf16[2,64,128,3,32]{4,3,2,0,1:T(4,128)(2,1)} %bitcast.215), kind=kLoop, calls=%fused_computation.144.clone.1 | loop fusion | bytes 6291456 | tf_op jit(solution)/shard_map/while/body/eval_jaxpr/slice | solution.py:109
  506.7 21.0 %gather_fusion = bf16[64,2,128,3,32]{4,3,2,1,0:T(4,128)(2,1)} fusion(bf16[2,48,128,3,32]{4,3,2,1,0:T(4,128)(2,1)} %get-tuple-element.448, s32[1024]{0:T(1024)S(1)} %pad_clamp_fusion.4), kind=kCustom, calls=%fused_computation.clone.1 | custom fusion | bytes 6291712 | tf_op jit(solution)/shard_map/while/body/eval_jaxpr/gather | solution.py:101
  527.7 13.1 %fusion.117 = (bf16[1,64,128,3,32]{4,3,2,0,1:T(4,128)(2,1)}, bf16[1,64,128,3,32]{4,3,2,0,1:T(4,128)(2,1)S(1)}) fusion(bf16[2,64,128,3,32]{4,3,2,0,1:T(4,128)(2,1)} %bitcast.215), kind=kLoop, calls=%fused_computation.144.clone.1 | loop fusion | bytes 6291456 | tf_op jit(solution)/shard_map/while/body/eval_jaxpr/slice | solution.py:109
  559.7 11.4 %all_to_all.35 = bf16[4,512,96]{1,2,0:T(8,128)(2,1)S(1)} all-to-all(bf16[4,512,96]{1,2,0:T(8,128)(2,1)S(1)} %copy.67), channel_id=1, replica_groups=mesh['slab'=32,'head'=4] {'head'}, dimensions={0} | all-to-all | bytes 786432 | tf_op jit(solution)/shard_map/all_to_all | solution.py:116
  573.6 203.3 %all-reduce.3.cloned.1.call-done = bf16[3,384,96]{1,2,0:T(8,128)(2,1)} async-done(((bf16[3,384,96]{1,2,0:T(8,128)(2,1)}), bf16[3,384,96]{1,2,0:T(8,128)(2,1)}) %all-reduce.3.cloned.1.call-update) | async-done | bytes 221200 | tf_op jit(solution)/shard_map/psum | solution.py:186
  778.5 43.5 %reduce-scatter.2.cloned.1.call-done = bf16[512,384]{1,0:T(8,128)(2,1)} async-done(((bf16[2048,384]{1,0:T(8,128)(2,1)}), bf16[512,384]{1,0:T(8,128)(2,1)}) %reduce-scatter.2.cloned.1.call-update) | async-done | bytes 393232 | tf_op jit(solution)/shard_map/reduce_scatter | solution.py:177
  823.5 66.1 %psum.23 = f32[384]{0:T(512)} all-reduce(f32[384]{0:T(512)S(1)} %get-tuple-element.271), channel_id=1, replica_groups=mesh['slab'=32,'head'=4] {'slab','head'}, use_global_device_ids=true, to_apply=%region_18.19 | all-reduce | flops 384 | bytes 3072 | tf_op jit(solution)/shard_map/psum | solution.py:188
  891.7 83.0 %all-reduce.5.cloned.1.call-done = f32[384,384]{1,0:T(8,128)} async-done(((f32[384,384]{1,0:T(8,128)}), f32[384,384]{1,0:T(8,128)}) %all-reduce.5.cloned.1.call-update) | async-done | bytes 589840 | tf_op jit(solution)/shard_map/psum | solution.py:188
  (196 shorter events, 226.7 us)
Async XLA Ops:
  7.2 32.9 %copy-start = (bf16[3,384,384]{2,1,0:T(8,128)(2,1)S(1)}, bf16[3,384,384]{2,1,0:T(8,128)(2,1)}, u32[]{:S(2)}) copy-start(bf16[3,384,384]{2,1,0:T(8,128)(2,1)} %param.21) | copy-start | bytes 2654212
  7.2 32.9 %all-gather.2.cloned.1.call-start = ((), (), s32[]{:S(2)}) async-start(), calls=%async_computation.3 | async-start | bytes 1966080 | tf_op jit(solution)/shard_map/all_gather | solution.py:82
  11.5 40.8 %copy-start.4 = (bf16[512,384]{1,0:T(8,128)(2,1)S(1)}, bf16[512,384]{1,0:T(8,128)(2,1)}, u32[]{:S(2)}) copy-start(bf16[512,384]{1,0:T(8,128)(2,1)} %param.23) | copy-start | bytes 1179652
  11.5 40.8 %copy-start.11 = (bf16[384,384]{1,0:T(8,128)(2,1)S(1)}, bf16[384,384]{1,0:T(8,128)(2,1)}, u32[]{:S(2)}) copy-start(bf16[384,384]{1,0:T(8,128)(2,1)} %param.22) | copy-start | bytes 884740
  42.6 15.0 %copy-start.31 = (s32[16]{0:T(128)S(1)}, s32[16]{0:T(128)}, u32[]{:S(2)}) copy-start(s32[16]{0:T(128)} %param.25) | copy-start | bytes 196
  45.1 41.9 %collective-permute-start = (bf16[2,2048,96]{1,2,0:T(8,128)(2,1)}, bf16[2,2048,96]{1,2,0:T(8,128)(2,1)}, u32[]{:S(2)}, u32[]{:S(2)}) collective-permute-start(bf16[2,2048,96]{1,2,0:T(8,128)(2,1)} %pad_maximum_fusion.2), channel_id=1, source_target_pairs={{0,4},{4,8},{8,12},{12,16},{16,20},{20,24},{24,28},{28,32},{32,36}... | collective-permute-start | bytes 2359304 | tf_op jit(solution)/shard_map/ppermute | solution.py:24
  47.5 39.5 %collective-permute-start.1 = (bf16[2,2048,96]{1,2,0:T(8,128)(2,1)}, bf16[2,2048,96]{1,2,0:T(8,128)(2,1)}, u32[]{:S(2)}, u32[]{:S(2)}) collective-permute-start(bf16[2,2048,96]{1,2,0:T(8,128)(2,1)} %pad_maximum_fusion.2), channel_id=1, source_target_pairs={{4,0},{8,4},{12,8},{16,12},{20,16},{24,20},{28,24},{32,28},{36,32}... | collective-permute-start | bytes 2359304 | tf_op jit(solution)/shard_map/ppermute | solution.py:25
  53.5 32.9 %all-to-all-start.1 = ((bf16[512,4,96]{0,2,1:T(8,128)(2,1)}), bf16[512,4,96]{0,2,1:T(8,128)(2,1)S(1)}, u32[]{:S(2)}, u32[]{:S(2)}) async-start(bf16[512,4,96]{0,2,1:T(8,128)(2,1)} %bitcast.28), calls=%async_computation.1 | async-start | bytes 786432 | tf_op jit(solution)/shard_map/all_to_all | solution.py:124
  57.5 719.3 %all-reduce.3.cloned.1.call-start = ((), (), s32[]{:S(2)}) async-start(), calls=%async_computation.5 | async-start | bytes 442368 | tf_op jit(solution)/shard_map/psum | solution.py:186
  106.8 283.2 %copy-start.24 = (f32[2048,3]{0,1:T(4,128)S(1)}, f32[2048,3]{0,1:T(4,128)}, u32[]{:S(2)}) copy-start(f32[2048,3]{0,1:T(4,128)} %copy-done.23) | copy-start | bytes 73732
  377.6 16.4 %copy-start.9 = (f32[1,2048,96]{1,2,0:T(8,128)S(1)}, f32[1,2048,96]{1,2,0:T(8,128)}, u32[]{:S(2)}) copy-start(f32[1,2048,96]{1,2,0:T(8,128)} %copy-done.8) | copy-start | bytes 2359300
  377.6 16.4 %copy-start.20 = (f32[2048,3]{0,1:T(4,128)S(1)}, f32[2048,3]{0,1:T(4,128)}, u32[]{:S(2)}) copy-start(f32[2048,3]{0,1:T(4,128)} %copy-done.19) | copy-start | bytes 73732
  380.4 54.7 %collective-permute-start.3 = (f32[2,16,128,3,32]{2,4,3,1,0:T(8,128)}, f32[2,16,128,3,32]{2,4,3,1,0:T(8,128)}, u32[]{:S(2)}, u32[]{:S(2)}) collective-permute-start(f32[2,16,128,3,32]{2,4,3,1,0:T(8,128)} %slice.135), channel_id=1, source_target_pairs={{0,4},{4,8},{8,12},{12,16},{16,20},{20,24},{24,28},{28,32},{32,36}... | collective-permute-start | bytes 4718600 | tf_op jit(solution)/shard_map/ppermute | solution.py:33
  385.1 50.0 %collective-permute-start.2 = (bf16[2,16,128,3,32]{2,4,3,1,0:T(8,128)(2,1)}, bf16[2,16,128,3,32]{2,4,3,1,0:T(8,128)(2,1)}, u32[]{:S(2)}, u32[]{:S(2)}) collective-permute-start(bf16[2,16,128,3,32]{2,4,3,1,0:T(8,128)(2,1)} %slice.163), channel_id=1, source_target_pairs={{0,124},{4,0},{8,4},{12,8},{16,12},{20,16},{24,20},{28,24},{32,28}... | collective-permute-start | bytes 2359304 | tf_op jit(solution)/shard_map/ppermute | solution.py:33
  396.2 44.8 %copy-start.7 = (f32[1,2048,96]{1,2,0:T(8,128)S(1)}, f32[1,2048,96]{1,2,0:T(8,128)}, u32[]{:S(2)}) copy-start(f32[1,2048,96]{1,2,0:T(8,128)} %copy-done.6) | copy-start | bytes 2359300
  396.2 44.8 %copy-start.22 = (f32[2048,3]{0,1:T(4,128)S(1)}, f32[2048,3]{0,1:T(4,128)}, u32[]{:S(2)}) copy-start(f32[2048,3]{0,1:T(4,128)} %copy-done.21) | copy-start | bytes 73732
  451.6 370.5 %reduce-scatter.2.cloned.1.call-start = ((), (), s32[]{:S(2)}) async-start(), calls=%async_computation.4 | async-start | bytes 1966080 | tf_op jit(solution)/shard_map/reduce_scatter | solution.py:177
  455.2 519.5 %all-reduce.5.cloned.1.call-start = ((), (), s32[]{:S(2)}) async-start(), calls=%async_computation.6 | async-start | bytes 1179648 | tf_op jit(solution)/shard_map/psum | solution.py:188
  455.3 115.9 %copy-start.5 = (bf16[512,384]{1,0:T(8,128)(2,1)S(1)}, bf16[512,384]{1,0:T(8,128)(2,1)}, u32[]{:S(2)}) copy-start(bf16[512,384]{1,0:T(8,128)(2,1)} %param.23) | copy-start | bytes 1179652
  455.3 117.1 %copy-start.3 = (bf16[512,384]{1,0:T(8,128)(2,1)S(1)}, bf16[512,384]{1,0:T(8,128)(2,1)}, u32[]{:S(2)}) copy-start(bf16[512,384]{1,0:T(8,128)(2,1)} %param.19) | copy-start | bytes 1179652
  455.3 117.1 %copy-start.12 = (bf16[384,384]{1,0:T(8,128)(2,1)S(1)}, bf16[384,384]{1,0:T(8,128)(2,1)}, u32[]{:S(2)}) copy-start(bf16[384,384]{1,0:T(8,128)(2,1)} %param.22) | copy-start | bytes 884740
  558.5 263.6 %copy-start.27 = (f32[512]{0:T(512)S(1)}, f32[512]{0:T(512)}, u32[]{:S(2)}) copy-start(f32[512]{0:T(512)} %copy-done.26) | copy-start | bytes 6148
  558.5 263.6 %copy-start.28 = (f32[384]{0:T(512)S(1)}, f32[384]{0:T(512)}, u32[]{:S(2)}) copy-start(f32[384]{0:T(512)} %param.20) | copy-start | bytes 4612
  558.5 331.1 %copy-start.29 = (f32[512]{0:T(512)S(1)}, f32[512]{0:T(512)}, u32[]{:S(2)}) copy-start(f32[512]{0:T(512)} %get-tuple-element.319) | copy-start | bytes 6148
  (20 other events, 110.5 us)
Sparse Core Ops, SparseCore 0:
  11.6 28.3 all-gather.1
  451.7 325.0 all-reduce.2
  779.2 42.8 reduce-scatter.1
  827.2 147.4 all-reduce.4
where the time goes:
time: 990 us; the launch traced here: 983 us
  waiting for transfers between devices  426 us (43%)
  local copies, waits for them, and re-layouts  247 us (25%)
  matrix products  102 us (10%)
  other arithmetic  83.3 us (8%)
  blocking collectives  77.5 us (8%)
  starting transfers between devices  18.5 us (2%)
  loops' own time  14.8 us (1%)
  between operations  14.3 us (1%)
    psum x1, waiting for transfers between devices, local(): lax.psum(d_qkv_part.astype(jnp.bfloat16), 'slab').astype(jnp.float32)  203 us
    gather x4, local copies, waits for them, and re-layouts, fetch(): both = key_blocks[:, lookup_rows.reshape(-1)]  83.8 us
    psum x1, waiting for transfers between devices, local(): d_w_out, d_gain = lax.psum((d_out_part, d_gain_part), ('slab', 'head'))  83 us
    psum x1, blocking collectives, local(): d_w_out, d_gain = lax.psum((d_out_part, d_gain_part), ('slab', 'head'))  66.1 us
    reduce_scatter x1, waiting for transfers between devices, local(): lax.psum_scatter(jnp.einsum('crk,cdk->rd', d_qkv, w_here, preferred_eleme...  43.5 us
    ppermute x2, waiting for transfers between devices, passed_along(): return lax.ppermute(value, axis, pairs)  38.9 us
    scatter-add x2, other arithmetic, backward_group(): grad_buffer = grad_buffer.at[:, lookup_rows.reshape(-1)].add(stacked)  33.3 us
    slice x2, local copies, waits for them, and re-layouts, backward_group(): both[1]  32 us
  transfers between devices with their start and end apart: 9, of which 6 were waited for; matrix products, arithmetic and copies ran while one was open for 13% of the time, Pallas kernels for 0%

commit v1 on v0

v1 whole, which is shorter than its diff:
```python
import math

import jax
import jax.numpy as jnp
from jax import lax
from jax.sharding import PartitionSpec as P

HEADS = 12
BLK = 128
REACH = 16


exponent_divisor = 10.0
norm_eps = 1e-06


def padded(value, sides, width):
    for axis, dim in sides:
        size, length = (lax.axis_size(axis), value.shape[dim])
        up = [(i, (i + 1) % size) for i in range(size)]
        down = [(j, i) for i, j in up]
        last = lax.slice_in_dim(value, length - width, length, axis=dim)
        first = lax.slice_in_dim(value, 0, width, axis=dim)
        before = lax.ppermute(last, axis, up)
        after = lax.ppermute(first, axis, down)
        value = jnp.concatenate([before, value, after], axis=dim)
    return value


def passed_along(value, axis, steps):
    count = lax.axis_size(axis)
    pairs = [(source, (source + steps) % count) for source in range(count)]
    return lax.ppermute(value, axis, pairs)


def normalize(projected, head_dim):
    by_head = projected.reshape(projected.shape[:-1] + (projected.shape[-1] // head_dim, head_dim))
    length = jnp.sqrt(jnp.sum(by_head * by_head, -1, keepdims=True))
    divisor = jnp.maximum(length, 0.7 * math.sqrt(head_dim))
    return (by_head / divisor, divisor, length > 0.7 * math.sqrt(head_dim))


def unit_heads(projected, head_dim):
    unit, divisor, active = normalize(projected, head_dim)
    return unit.reshape(projected.shape)


def norm_back(projected, grad, head_dim):
    unit, divisor, active = normalize(projected, head_dim)
    along = grad.astype(jnp.float32).reshape(unit.shape)
    inner = jnp.sum(unit * along, -1, keepdims=True)
    result = (along - jnp.where(active, unit * inner, 0.0)) / divisor
    return result.reshape(projected.shape)


def to_heads(value, blocks, heads_here, head_dim):
    lead = value.shape[:-2]
    value = value.reshape(lead + (blocks, BLK, heads_here, head_dim))
    return jnp.moveaxis(value, len(lead) + 2, len(lead))


def from_heads(value):
    lead = value.shape[:-4]
    heads_here, blocks, rows, head_dim = value.shape[len(lead) :]
    value = jnp.moveaxis(value, len(lead), len(lead) + 2)
    return value.reshape(lead + (blocks * rows, heads_here * head_dim))


def local(tokens, norm_gain, w_qkv, w_out, cotangent, neighbours, counts):
    f32, bf16 = jnp.float32, jnp.bfloat16
    width = tokens.shape[1]
    head_dim = width // HEADS
    n_head = lax.axis_size("head")
    n_slab = lax.axis_size("slab")
    head_cols = width // n_head
    heads_here = HEADS // n_head
    head_index = lax.axis_index("head")
    slab_index = lax.axis_index("slab")
    slab_blocks, n_slots = neighbours.shape
    ext_blocks = slab_blocks + 2 * REACH
    n_blocks = slab_blocks * n_slab
    tok_f32 = tokens.astype(f32)
    inverse = lax.rsqrt(jnp.mean(tok_f32 * tok_f32, -1, keepdims=True) + norm_eps)
    normed = (tok_f32 * inverse * norm_gain).astype(bf16)
    w_here = lax.dynamic_slice_in_dim(w_qkv, head_index * head_cols, head_cols, 2)
    gathered = lax.all_gather(normed, "head", axis=0, tiled=True)
    projected = jnp.einsum("rd,cde->cre", gathered, w_here, preferred_element_type=f32)
    packed = jnp.stack(
        [unit_heads(projected[0], head_dim), unit_heads(projected[1], head_dim), projected[2]]
    ).astype(bf16)
    split = lambda value: to_heads(value, slab_blocks, heads_here, head_dim)
    q_heads = split(packed[0])
    keys_values = split(packed[1:])
    extended = padded(keys_values, (("slab", 2),), REACH)
    lookup = (neighbours - slab_index * slab_blocks + REACH) % n_blocks
    choose = lookup[:, :, None] == jnp.arange(ext_blocks, dtype=jnp.int32)
    fetched = jnp.einsum(
        "bse,chekd->chbskd", choose.astype(bf16), extended, preferred_element_type=f32
    ).astype(bf16)
    keys, values = fetched[0], fetched[1]
    live = (jnp.arange(n_slots, dtype=jnp.int32)[None, :] < counts[:, None]).astype(f32)
    scores = exponent_divisor * jnp.einsum(
        "hbqd,hbskd->hbqsk", q_heads, keys, preferred_element_type=f32
    )
    raised = jnp.exp(scores) * live[None, :, None, :, None]
    weights = raised / jnp.sum(raised, (-2, -1), keepdims=True)
    weights_bf = weights.astype(bf16)
    attended_heads = jnp.einsum(
        "hbqsk,hbskd->hbqd", weights_bf, values, preferred_element_type=f32
    ).astype(bf16)
    attended = lax.all_to_all(
        from_heads(attended_heads), "head", split_axis=0, concat_axis=1, tiled=True
    )
    output = (tok_f32 + jnp.dot(attended, w_out, preferred_element_type=f32)).astype(bf16)
    d_out_part = jnp.dot(attended.T, cotangent, preferred_element_type=f32)
    d_attended = jnp.dot(cotangent, w_out.T, preferred_element_type=f32).astype(bf16)
    d_attn = split(lax.all_to_all(d_attended, "head", split_axis=1, concat_axis=0, tiled=True))
    d_weights = jnp.einsum("hbqd,hbskd->hbqsk", d_attn, values, preferred_element_type=f32)
    row_dot = jnp.sum(d_weights * weights, (-2, -1), keepdims=True)
    d_scores = (exponent_divisor * weights * (d_weights - row_dot)).astype(bf16)
    d_query = jnp.einsum("hbqsk,hbskd->hbqd", d_scores, keys, preferred_element_type=f32)
    d_keys = jnp.einsum("hbqsk,hbqd->hbskd", d_scores, q_heads, preferred_element_type=f32)
    d_values = jnp.einsum("hbqsk,hbqd->hbskd", weights_bf, d_attn, preferred_element_type=f32)
    grad_ext = jnp.einsum(
        "bse,chbskd->chekd",
        choose.astype(f32),
        jnp.stack([d_keys, d_values]),
        precision=lax.Precision.HIGHEST,
        preferred_element_type=f32,
    )
    low_rim = grad_ext[:, :, :REACH]
    high_rim = grad_ext[:, :, REACH + slab_blocks :]
    from_above = passed_along(low_rim.astype(bf16), "slab", -1).astype(f32)
    from_below = passed_along(high_rim, "slab", 1)
    own_grads = grad_ext[:, :, REACH : REACH + slab_blocks]
    own_grads = own_grads.at[:, :, slab_blocks - REACH :].add(from_above)
    own_grads = own_grads.at[:, :, :REACH].add(from_below)
    d_packed = jnp.concatenate(
        [from_heads(d_query)[None], from_heads(own_grads)], 0
    ).astype(bf16)
    d_query_part = norm_back(projected[0], d_packed[0], head_dim).astype(bf16)
    d_key_part = norm_back(projected[1], d_packed[1], head_dim).astype(bf16)
    d_qkv = jnp.stack([d_query_part, d_key_part, d_packed[2]])
    d_normed = lax.psum_scatter(
        jnp.einsum("crk,cdk->rd", d_qkv, w_here, preferred_element_type=f32).astype(bf16),
        "head",
        scatter_dimension=0,
        tiled=True,
    ).astype(f32)
    d_qkv_part = jnp.einsum("rd,crk->cdk", gathered, d_qkv, preferred_element_type=f32)
    d_gain_part = jnp.sum(d_normed * tok_f32 * inverse, 0)
    slots = jnp.zeros((n_head,) + d_qkv_part.shape, f32)
    slots = lax.dynamic_update_index_in_dim(slots, d_qkv_part, head_index, 0)
    pieces = [slots.reshape(-1, width), d_out_part, d_gain_part[None]]
    total = lax.psum(jnp.concatenate(pieces, 0), ("slab", "head"))
    slot_rows = pieces[0].shape[0]
    all_slots = total[:slot_rows].reshape(slots.shape)
    d_w_qkv = lax.dynamic_index_in_dim(all_slots, head_index, 0, keepdims=False)
    d_w_out = total[slot_rows : slot_rows + width]
    d_gain = total[slot_rows + width]
    scaled = d_normed * norm_gain
    d_tokens = (
        cotangent.astype(f32)
        + inverse * scaled
        - tok_f32 * inverse**3 * jnp.mean(scaled * tok_f32, -1, keepdims=True)
    )
    return (output, d_tokens.astype(bf16), d_w_qkv, d_w_out, d_gain)


def solution(mesh):
    placed = (
        P(("slab", "head"), None),
        P(),
        P(),
        P(),
        P(("slab", "head"), None),
        P("slab", None),
        P("slab"),
    )
    return jax.shard_map(
        local,
        mesh=mesh,
        in_specs=placed,
        out_specs=(
            P(("slab", "head"), None),
            P(("slab", "head"), None),
            P(None, None, "head"),
            P(),
            P(),
        ),
        check_vma=False,
    )
```

time: 990 us -> 499 us (0.50)
  local copies, waits for them, and re-layouts: 247 us -> 42 us
  waiting for transfers between devices: 426 us -> 245 us
  blocking collectives: 77.5 us -> 0 us
  other arithmetic: 83.3 us -> 56.6 us
  loops' own time: 14.8 us -> 0 us
    psum x2 -> x1, waiting for transfers between devices: 286 us -> 149 us  [local(): total = lax.psum(jnp.concatenate(pieces, 0), ('slab', 'head'))]
    gather x4 -> x0, local copies, waits for them, and re-layouts: 83.8 us -> none  [fetch(): both = key_blocks[:, lookup_rows.reshape(-1)]]
    psum x1 -> x0, blocking collectives: 66.1 us -> none  [local(): d_w_out, d_gain = lax.psum((d_out_part, d_gain_part), ('slab', 'head'))]
    slice x6, local copies, waits for them, and re-layouts: 63.5 us -> 6.95 us  [the longest x1 1.92 us: local(): d_w_out = total[slot_rows:slot_rows + width]]
    reduce_scatter x1, waiting for transfers between devices: 43.5 us -> 0.02 us  [local(): lax.psum_scatter(jnp.einsum('crk,cdk->rd', d_qkv, w_here, preferred_eleme...]
    scatter-add x2 -> x0, other arithmetic: 33.3 us -> none  [backward_group(): grad_buffer = grad_buffer.at[:, lookup_rows.reshape(-1)].add(stacked)]
    another operation x6 -> x0, local copies, waits for them, and re-layouts: 30.9 us -> none  [backward_group(): jnp.stack([d_keys, d_values])]
    squeeze x2 -> x1, local copies, waits for them, and re-layouts: 21 us -> 3.68 us  [local(): keys, values = (fetched[0], fetched[1])]
  transfers between devices with their start and end apart: 9 -> 9, of which waited for: 6 -> 5; matrix products, arithmetic and copies ran while one was open for 13% -> 10% of each run, Pallas kernels for 0% -> 0%
where the time goes in v1:
time: 499 us; the launch traced here: 492 us
  waiting for transfers between devices  245 us (49%)
  matrix products  110 us (22%)
  other arithmetic  56.6 us (11%)
  local copies, waits for them, and re-layouts  42 us (8%)
  starting transfers between devices  24.3 us (5%)
  between operations  14.3 us (3%)
    psum x1, waiting for transfers between devices, local(): total = lax.psum(jnp.concatenate(pieces, 0), ('slab', 'head'))  149 us
    ppermute x2, waiting for transfers between devices, passed_along(): return lax.ppermute(value, axis, pairs)  31.7 us
    all_gather x1, waiting for transfers between devices, local(): gathered = lax.all_gather(normed, 'head', axis=0, tiled=True)  28.5 us
    all_to_all x1, waiting for transfers between devices, local(): lax.all_to_all(d_attended, 'head', split_axis=1, concat_axis=0, tiled=True)  28.3 us
    convert_element_type x1, other arithmetic, local(): d_scores = (exponent_divisor * weights * (d_weights - row_dot)).astype(bf16)  22.6 us
    dot_general x1, matrix products, local(): jnp.einsum('hbqd,hbskd->hbqsk', d_attn, values, preferred_element_type=f32)  19.4 us
    dot_general x1, matrix products, local(): jnp.einsum('bse,chbskd->chekd', choose.astype(f32), jnp.stack([d_keys, d_...  16.1 us
    dot_general x1, matrix products, local(): jnp.einsum('hbqd,hbskd->hbqsk', q_heads, keys, preferred_element_type=f32)  13.5 us
  transfers between devices with their start and end apart: 9, of which 5 were waited for; matrix products, arithmetic and copies ran while one was open for 10% of the time, Pallas kernels for 0%

profile of v1, /device:TPU:1, one launch (start us, length us, event | category | flops | bytes accessed | tf_op | source)
XLA Modules:
  0.0 492.3 jit_solution(16731241766976111401)
XLA Ops:
  11.5 28.5 %all-gather.2.cloned.1.call-done = bf16[2048,384]{1,0:T(8,128)(2,1)} async-done(((bf16[512,384]{1,0:T(8,128)(2,1)}), bf16[2048,384]{1,0:T(8,128)(2,1)}) %all-gather.2.cloned.1.call-update) | async-done | bytes 1572880 | tf_op jit(solution)/shard_map/all_gather | solution.py:86
  40.0 2.5 convolution_bitcast_fusion
  47.5 4.8 collective-permute-start.1
  53.5 4.7 all-to-all-start.1
  58.2 28.3 %all-to-all-done.1 = bf16[512,4,96]{0,2,1:T(8,128)(2,1)} async-done(((bf16[512,4,96]{0,2,1:T(8,128)(2,1)}), bf16[512,4,96]{0,2,1:T(8,128)(2,1)}, u32[]{:S(2)}, u32[]{:S(2)}) %all-to-all-start.1) | async-done | bytes 393248 | tf_op jit(solution)/shard_map/all_to_all | solution.py:117
  91.5 3.6 convert_bitcast_fusion
  95.1 3.7 slice_bitcast_fusion
  98.8 13.5 %fusion.3 = (f32[3,16,128]{2,1,0:T(8,128)S(1)}, f32[3,16,128,8,128]{2,4,3,1,0:T(8,128)}) fusion(f32[16,8]{1,0:T(8,128)S(1)} %fusion.95, bf16[3,16,8,128,32]{3,1,2,4,0:T(8,128)(2,1)S(1)} %get-tuple-element.47, bf16[16,128,3,32]{1,0,3,2:T(8,128)(2,1)S(1)} %bitcast.184), kind=kOutput, calls=%fused_computation.6 | convolution fusion | flops 421521408 | bytes 28729856 | tf_op jit(solution)/shard_map/hbqd,hbskd->hbqsk/dot_general | solution.py:102
  112.3 12.5 %fusion.17 = f32[1,3,16,8,128,32]{4,5,3,2,1,0:T(8,128)} fusion(bf16[16,128,3,32]{1,0,3,2:T(8,128)(2,1)S(1)} %copy-done.15, f32[3,16,128,8,128]{2,4,3,1,0:T(8,128)} %get-tuple-element.60, f32[3,16,128]{2,1,0:T(8,128)S(1)} %get-tuple-element.59, f32[16,8]{1,0:T(8,128)S(1)} %fusion.95), kind=kOutput, calls=%fused_computation.26 | convolution fusion | flops 427819008 | bytes 31875584 | tf_op jit(solution)/shard_map/hbqsk,hbqd->hbskd/dot_general | solution.py:123
  124.9 19.4 %multiply_reduce_fusion = (f32[3,16,128]{2,1,0:T(8,128)S(1)}, f32[3,16,128,8,128]{2,4,3,1,0:T(8,128)}) fusion(f32[3,16,128]{2,1,0:T(8,128)S(1)} %get-tuple-element.59, f32[16,8]{1,0:T(8,128)S(1)} %fusion.95, f32[3,16,128,8,128]{2,4,3,1,0:T(8,128)} %get-tuple-element.60, bf16[3,16,8,128,32]{3,1,2,4,0:T(8,128)(2,1)} %get-tuple-element.48, ...), kind=kOutput, calls=%fused_computation.3 | convolution fusion | flops 434104320 | bytes 53920256 | tf_op jit(solution)/shard_map/hbqd,hbskd->hbqsk/dot_general | solution.py:118
  144.3 22.6 %multiply_convert_fusion = bf16[3,16,128,8,128]{2,4,3,1,0:T(8,128)(2,1)} fusion(f32[3,16,128,8,128]{2,4,3,1,0:T(8,128)} %get-tuple-element.62, f32[3,16,128]{2,1,0:T(8,128)S(1)} %get-tuple-element.61, f32[3,16,128]{2,1,0:T(8,128)S(1)} %get-tuple-element.59, f32[16,8]{1,0:T(8,128)S(1)} %fusion.95, f32[3,16,128,8,128]{2,4,3,1,0:T(8,128)} %get-tuple-element.60), kind=kLoop, calls=%fused_computation.2 | loop fusion | flops 44040192 | bytes 62964224 | tf_op jit(solution)/shard_map/convert_element_type | solution.py:120
  166.9 11.7 %convolution_bitcast_fusion.1 = f32[1,3,16,8,128,32]{4,5,3,2,1,0:T(8,128)} fusion(bf16[3,16,128,8,128]{2,4,3,1,0:T(8,128)(2,1)} %multiply_convert_fusion, bf16[16,128,3,32]{1,0,3,2:T(8,128)(2,1)} %bitcast.185), kind=kOutput, calls=%fused_computation.27 | convolution fusion | flops 402653184 | bytes 19267584 | tf_op jit(solution)/shard_map/hbqsk,hbqd->hbskd/dot_general | solution.py:122
  178.5 12.1 %pad_maximum_fusion = f32[2,3,16,8,128,32]{4,5,3,2,1,0:T(8,128)} fusion(f32[1,3,16,8,128,32]{4,5,3,2,1,0:T(8,128)} %fusion.17, f32[1,3,16,8,128,32]{4,5,3,2,1,0:T(8,128)} %convolution_bitcast_fusion.1), kind=kLoop, calls=%fused_computation.7 | loop fusion | flops 3145728 | bytes 25165824 | tf_op jit(solution)/shard_map/stack | solution.py:127
  190.6 16.1 %fusion.24 = f32[2,3,48,128,32]{3,2,4,1,0:T(8,128)S(1)} fusion(f32[2,3,16,8,128,32]{4,5,3,2,1,0:T(8,128)} %pad_maximum_fusion, s32[16,8]{0,1:T(8,128)S(1)} %add_select_fusion), kind=kOutput, calls=%fused_computation.34 | convolution fusion | flops 1811945472 | bytes 17302016 | tf_op jit(solution)/shard_map/bse,chbskd->chekd/dot_general | solution.py:124
  211.4 4.8 collective-permute-start.2
  216.2 7.8 %fusion.49 = f32[3,16,128,32]{2,3,1,0:T(8,128)S(1)} fusion(bf16[3,16,128,8,128]{2,4,3,1,0:T(8,128)(2,1)} %multiply_convert_fusion, bf16[3,16,8,128,32]{3,1,2,4,0:T(8,128)(2,1)S(1)} %copy-done.2), kind=kOutput, calls=%fused_computation.54 | convolution fusion | flops 403046400 | bytes 16515072 | tf_op jit(solution)/shard_map/hbqsk,hbskd->hbqd/dot_general | solution.py:121
  230.8 31.7 %collective-permute-done.2 = bf16[2,3,16,128,32]{3,2,4,1,0:T(8,128)(2,1)} collective-permute-done((bf16[2,3,16,128,32]{3,2,4,1,0:T(8,128)(2,1)}, bf16[2,3,16,128,32]{3,2,4,1,0:T(8,128)(2,1)}, u32[]{:S(2)}, u32[]{:S(2)}) %collective-permute-start.2) | collective-permute-done | bytes 786464 | tf_op jit(solution)/shard_map/ppermute | solution.py:33
  278.1 2.5 bitcast_convert_fusion
  280.6 12.8 %fusion.55 = bf16[16,128,3,32]{1,3,0,2:T(8,128)(2,1)S(1)} fusion(bf16[3,16,8,128,32]{3,1,2,4,0:T(8,128)(2,1)} %get-tuple-element.48, f32[3,16,128,8,128]{2,4,3,1,0:T(8,128)} %get-tuple-element.60, f32[3,16,128]{2,1,0:T(8,128)S(1)} %get-tuple-element.59, f32[16,8]{1,0:T(8,128)S(1)} %fusion.95), kind=kOutput, calls=%fused_computation.56 | convolution fusion | flops 428015616 | bytes 28729856 | tf_op jit(solution)/shard_map/hbqsk,hbskd->hbqd/dot_general | solution.py:108
  296.3 5.2 %all-to-all-start = ((bf16[4,512,96]{1,2,0:T(8,128)(2,1)}), bf16[4,512,96]{1,2,0:T(8,128)(2,1)S(1)}, u32[]{:S(2)}, u32[]{:S(2)}) async-start(bf16[4,512,96]{1,2,0:T(8,128)(2,1)} %copy.69), calls=%async_computation | async-start | bytes 786432 | tf_op jit(solution)/shard_map/all_to_all | solution.py:111
  301.5 8.1 %all-to-all-done = bf16[4,512,96]{1,2,0:T(8,128)(2,1)S(1)} async-done(((bf16[4,512,96]{1,2,0:T(8,128)(2,1)}), bf16[4,512,96]{1,2,0:T(8,128)(2,1)S(1)}, u32[]{:S(2)}, u32[]{:S(2)}) %all-to-all-start) | async-done | bytes 393248 | tf_op jit(solution)/shard_map/all_to_all | solution.py:111
  310.9 2.8 fusion.52
  321.1 2.6 pad_maximum_fusion.1
  328.1 148.7 %all-reduce.2.cloned.1.call-done = f32[1537,384]{1,0:T(8,128)} async-done(((f32[1537,384]{1,0:T(8,128)}), f32[1537,384]{1,0:T(8,128)}) %all-reduce.2.cloned.1.call-update) | async-done | bytes 2360848 | tf_op jit(solution)/shard_map/psum | solution.py:155
  (110 shorter events, 67.2 us)
Async XLA Ops:
  7.2 32.9 %copy-start = (bf16[3,384,384]{2,1,0:T(8,128)(2,1)S(1)}, bf16[3,384,384]{2,1,0:T(8,128)(2,1)}, u32[]{:S(2)}) copy-start(bf16[3,384,384]{2,1,0:T(8,128)(2,1)} %param.17) | copy-start | bytes 2654212
  7.2 32.9 %all-gather.2.cloned.1.call-start = ((), (), s32[]{:S(2)}) async-start(), calls=%async_computation.3 | async-start | bytes 1966080 | tf_op jit(solution)/shard_map/all_gather | solution.py:86
  42.7 10.8 %copy-start.10 = (f32[1,2048,96]{1,2,0:T(8,128)}, f32[1,2048,96]{1,2,0:T(8,128)S(1)}, u32[]{:S(2)}) copy-start(f32[1,2048,96]{1,2,0:T(8,128)S(1)} %get-tuple-element.54) | copy-start | bytes 2359300
  42.7 10.8 %copy-start.11 = (f32[1,2048,96]{1,2,0:T(8,128)}, f32[1,2048,96]{1,2,0:T(8,128)S(1)}, u32[]{:S(2)}) copy-start(f32[1,2048,96]{1,2,0:T(8,128)S(1)} %get-tuple-element.53) | copy-start | bytes 2359300
  42.7 9.6 %copy-start.6 = (bf16[512,384]{1,0:T(8,128)(2,1)S(1)}, bf16[512,384]{1,0:T(8,128)(2,1)}, u32[]{:S(2)}) copy-start(bf16[512,384]{1,0:T(8,128)(2,1)} %param.19) | copy-start | bytes 1179652
  42.7 9.6 %copy-start.13 = (bf16[384,384]{1,0:T(8,128)(2,1)S(1)}, bf16[384,384]{1,0:T(8,128)(2,1)}, u32[]{:S(2)}) copy-start(bf16[384,384]{1,0:T(8,128)(2,1)} %param.18) | copy-start | bytes 884740
  42.8 15.4 %copy-start.22 = (s32[16,8]{0,1:T(8,128)S(1)}, s32[16,8]{0,1:T(8,128)}, u32[]{:S(2)}) copy-start(s32[16,8]{0,1:T(8,128)} %param.20) | copy-start | bytes 1540
  42.8 15.4 %copy-start.23 = (s32[16]{0:T(128)S(1)}, s32[16]{0:T(128)}, u32[]{:S(2)}) copy-start(s32[16]{0:T(128)} %param.21) | copy-start | bytes 196
  45.1 46.4 %collective-permute-start = (bf16[2,3,16,128,32]{3,2,4,1,0:T(8,128)(2,1)}, bf16[2,3,16,128,32]{3,2,4,1,0:T(8,128)(2,1)}, u32[]{:S(2)}, u32[]{:S(2)}) collective-permute-start(bf16[2,3,16,128,32]{3,2,4,1,0:T(8,128)(2,1)} %bitcast.9), channel_id=1, source_target_pairs={{0,4},{4,8},{8,12},{12,16},{16,20},{20,24},{24,28},{28,32},{32,36}... | collective-permute-start | bytes 2359304 | tf_op jit(solution)/shard_map/ppermute | solution.py:24
  47.5 44.0 %collective-permute-start.1 = (bf16[2,3,16,128,32]{3,2,4,1,0:T(8,128)(2,1)}, bf16[2,3,16,128,32]{3,2,4,1,0:T(8,128)(2,1)}, u32[]{:S(2)}, u32[]{:S(2)}) collective-permute-start(bf16[2,3,16,128,32]{3,2,4,1,0:T(8,128)(2,1)} %bitcast.9), channel_id=1, source_target_pairs={{4,0},{8,4},{12,8},{16,12},{20,16},{24,20},{28,24},{32,28},{36,32}... | collective-permute-start | bytes 2359304 | tf_op jit(solution)/shard_map/ppermute | solution.py:25
  53.5 33.0 %all-to-all-start.1 = ((bf16[512,4,96]{0,2,1:T(8,128)(2,1)}), bf16[512,4,96]{0,2,1:T(8,128)(2,1)}, u32[]{:S(2)}, u32[]{:S(2)}) async-start(bf16[512,4,96]{0,2,1:T(8,128)(2,1)} %bitcast.194), calls=%async_computation.1 | async-start | bytes 786432 | tf_op jit(solution)/shard_map/all_to_all | solution.py:117
  58.1 261.5 %reduce-scatter.2.cloned.1.call-start = ((), (), s32[]{:S(2)}) async-start(), calls=%async_computation.4 | async-start | bytes 1966080 | tf_op jit(solution)/shard_map/reduce_scatter | solution.py:144
  91.5 7.3 %copy-start.5 = (bf16[12,8,16,128]{3,2,1,0:T(8,128)(2,1)}, bf16[12,8,16,128]{3,2,1,0:T(8,128)(2,1)S(1)}, u32[]{:S(2)}) copy-start(bf16[12,8,16,128]{3,2,1,0:T(8,128)(2,1)S(1)} %copy.96) | copy-start | bytes 1179652
  98.8 13.6 %copy-start.1 = (bf16[3,16,8,128,32]{3,1,2,4,0:T(8,128)(2,1)}, bf16[3,16,8,128,32]{3,1,2,4,0:T(8,128)(2,1)S(1)}, u32[]{:S(2)}) copy-start(bf16[3,16,8,128,32]{3,1,2,4,0:T(8,128)(2,1)S(1)} %get-tuple-element.47) | copy-start | bytes 9437188
  98.8 13.6 %copy-start.15 = (bf16[16,128,3,32]{1,0,3,2:T(8,128)(2,1)S(1)}, bf16[16,128,3,32]{1,0,3,2:T(8,128)(2,1)}, u32[]{:S(2)}) copy-start(bf16[16,128,3,32]{1,0,3,2:T(8,128)(2,1)} %reshape.232) | copy-start | bytes 1179652
  206.7 17.4 %copy-start.3 = (f32[2,3,48,128,32]{3,2,4,1,0:T(8,128)}, f32[2,3,48,128,32]{3,2,4,1,0:T(8,128)S(1)}, u32[]{:S(2)}) copy-start(f32[2,3,48,128,32]{3,2,4,1,0:T(8,128)S(1)} %fusion.24) | copy-start | bytes 14155780
  206.7 9.5 %copy-start.2 = (bf16[3,16,8,128,32]{3,1,2,4,0:T(8,128)(2,1)S(1)}, bf16[3,16,8,128,32]{3,1,2,4,0:T(8,128)(2,1)}, u32[]{:S(2)}) copy-start(bf16[3,16,8,128,32]{3,1,2,4,0:T(8,128)(2,1)} %copy-done.1) | copy-start | bytes 9437188
  207.9 54.7 %collective-permute-start.3 = (f32[2,3,16,128,32]{3,2,4,1,0:T(8,128)}, f32[2,3,16,128,32]{3,2,4,1,0:T(8,128)}, u32[]{:S(2)}, u32[]{:S(2)}) collective-permute-start(f32[2,3,16,128,32]{3,2,4,1,0:T(8,128)} %slice.138), channel_id=1, source_target_pairs={{0,4},{4,8},{8,12},{12,16},{16,20},{20,24},{24,28},{28,32},{32,36}... | collective-permute-start | bytes 4718600 | tf_op jit(solution)/shard_map/ppermute | solution.py:33
  211.4 51.2 %collective-permute-start.2 = (bf16[2,3,16,128,32]{3,2,4,1,0:T(8,128)(2,1)}, bf16[2,3,16,128,32]{3,2,4,1,0:T(8,128)(2,1)}, u32[]{:S(2)}, u32[]{:S(2)}) collective-permute-start(bf16[2,3,16,128,32]{3,2,4,1,0:T(8,128)(2,1)} %slice.162), channel_id=1, source_target_pairs={{0,124},{4,0},{8,4},{12,8},{16,12},{20,16},{24,20},{28,24},{32,28}... | collective-permute-start | bytes 2359304 | tf_op jit(solution)/shard_map/ppermute | solution.py:33
  280.6 29.1 %copy-start.7 = (bf16[512,384]{1,0:T(8,128)(2,1)S(1)}, bf16[512,384]{1,0:T(8,128)(2,1)}, u32[]{:S(2)}) copy-start(bf16[512,384]{1,0:T(8,128)(2,1)} %param.19) | copy-start | bytes 1179652
  280.6 30.3 %copy-start.12 = (bf16[2048,384]{1,0:T(8,128)(2,1)S(1)}, bf16[2048,384]{1,0:T(8,128)(2,1)}, u32[]{:S(2)}) copy-start(bf16[2048,384]{1,0:T(8,128)(2,1)} %all-gather.2.cloned.1.call-done) | copy-start | bytes 4718596
  296.3 13.3 %all-to-all-start = ((bf16[4,512,96]{1,2,0:T(8,128)(2,1)}), bf16[4,512,96]{1,2,0:T(8,128)(2,1)S(1)}, u32[]{:S(2)}, u32[]{:S(2)}) async-start(bf16[4,512,96]{1,2,0:T(8,128)(2,1)} %copy.69), calls=%async_computation | async-start | bytes 786432 | tf_op jit(solution)/shard_map/all_to_all | solution.py:111
  301.5 175.3 %all-reduce.2.cloned.1.call-start = ((), (), s32[]{:S(2)}) async-start(), calls=%async_computation.5 | async-start | bytes 4743168 | tf_op jit(solution)/shard_map/psum | solution.py:155
  319.6 6.4 %copy-start.21 = (f32[512]{0:T(512)S(1)}, f32[512]{0:T(512)}, u32[]{:S(2)}) copy-start(f32[512]{0:T(512)} %get-tuple-element.57) | copy-start | bytes 6148
  (10 other events, 27.2 us)
Sparse Core Ops, SparseCore 0:
  11.6 28.3 all-gather.1
  280.7 27.1 reduce-scatter.1
  323.9 152.8 all-reduce.1

commit v2 on v1

--- a/solution.py
+++ b/solution.py
@@ -121,17 +121,18 @@
     d_query = jnp.einsum("hbqsk,hbskd->hbqd", d_scores, keys, preferred_element_type=f32)
     d_keys = jnp.einsum("hbqsk,hbqd->hbskd", d_scores, q_heads, preferred_element_type=f32)
     d_values = jnp.einsum("hbqsk,hbqd->hbskd", weights_bf, d_attn, preferred_element_type=f32)
-    grad_ext = jnp.einsum(
-        "bse,chbskd->chekd",
+    scatter = lambda grads: jnp.einsum(
+        "bse,hbskd->hekd",
         choose.astype(f32),
-        jnp.stack([d_keys, d_values]),
+        grads,
         precision=lax.Precision.HIGHEST,
         preferred_element_type=f32,
     )
+    grad_ext = jnp.stack([scatter(d_keys), scatter(d_values)])
     low_rim = grad_ext[:, :, :REACH]
     high_rim = grad_ext[:, :, REACH + slab_blocks :]
     from_above = passed_along(low_rim.astype(bf16), "slab", -1).astype(f32)
-    from_below = passed_along(high_rim, "slab", 1)
+    from_below = passed_along(high_rim.astype(bf16), "slab", 1).astype(f32)
     own_grads = grad_ext[:, :, REACH : REACH + slab_blocks]
     own_grads = own_grads.at[:, :, slab_blocks - REACH :].add(from_above)
     own_grads = own_grads.at[:, :, :REACH].add(from_below)

time: 499 us -> 462 us (0.926)
  waiting for transfers between devices: 245 us -> 226 us
  other arithmetic: 56.6 us -> 43.7 us
  matrix products: 110 us -> 105 us
    all_to_all x1, waiting for transfers between devices: 28.3 us -> 0.01 us  [local(): lax.all_to_all(d_attended, 'head', split_axis=1, concat_axis=0, tiled=True)]
    ppermute x1, waiting for transfers between devices: 0.01 us -> 17.8 us  [padded(): before = lax.ppermute(last, axis, up)]
    ppermute x2, waiting for transfers between devices: 31.7 us -> 18.4 us  [passed_along(): return lax.ppermute(value, axis, pairs)]
    ppermute x1, waiting for transfers between devices: 0.01 us -> 11.4 us  [padded(): after = lax.ppermute(first, axis, down)]
    another operation x1, other arithmetic: 12.1 us -> 2.92 us  [local(): jnp.stack([d_keys, d_values])]
    all_gather x1, waiting for transfers between devices: 28.5 us -> 20.8 us  [local(): gathered = lax.all_gather(normed, 'head', axis=0, tiled=True)]
    dot_general x1 -> x2, matrix products: 16.1 us -> 16.3 us  [local(): jnp.einsum('bse,hbskd->hekd', choose.astype(f32), grads, precision=lax.Pr...]
  transfers between devices with their start and end apart: 9 -> 9, of which waited for: 5 -> 7; matrix products, arithmetic and copies ran while one was open for 10% -> 11% of each run, Pallas kernels for 0% -> 0%
where the time goes in v2:
time: 462 us; the launch traced here: 458 us
  waiting for transfers between devices  226 us (49%)
  matrix products  105 us (23%)
  other arithmetic  43.7 us (9%)
  local copies, waits for them, and re-layouts  42.8 us (9%)
  starting transfers between devices  26.2 us (6%)
  between operations  14.3 us (3%)
    psum x1, waiting for transfers between devices, local(): total = lax.psum(jnp.concatenate(pieces, 0), ('slab', 'head'))  149 us
    convert_element_type x1, other arithmetic, local(): d_scores = (exponent_divisor * weights * (d_weights - row_dot)).astype(bf16)  22.7 us
    all_gather x1, waiting for transfers between devices, local(): gathered = lax.all_gather(normed, 'head', axis=0, tiled=True)  20.8 us
    dot_general x1, matrix products, local(): jnp.einsum('hbqd,hbskd->hbqsk', d_attn, values, preferred_element_type=f32)  19.3 us
    ppermute x2, waiting for transfers between devices, passed_along(): return lax.ppermute(value, axis, pairs)  18.4 us
    ppermute x1, waiting for transfers between devices, padded(): before = lax.ppermute(last, axis, up)  17.8 us
    dot_general x2, matrix products, local(): jnp.einsum('bse,hbskd->hekd', choose.astype(f32), grads, precision=lax.Pr...  16.3 us
    dot_general x1, matrix products, local(): jnp.einsum('hbqd,hbskd->hbqsk', q_heads, keys, preferred_element_type=f32)  13.4 us
  transfers between devices with their start and end apart: 9, of which 7 were waited for; matrix products, arithmetic and copies ran while one was open for 11% of the time, Pallas kernels for 0%

profile of v2, /device:TPU:1, one launch (start us, length us, event | category | flops | bytes accessed | tf_op | source)
XLA Modules:
  0.0 458.3 jit_solution(10248214438248925586)
XLA Ops:
  13.8 5.5 %all-to-all-start.1 = ((bf16[512,4,96]{0,2,1:T(8,128)(2,1)}), bf16[512,4,96]{0,2,1:T(8,128)(2,1)}, u32[]{:S(2)}, u32[]{:S(2)}) async-start(bf16[512,4,96]{0,2,1:T(8,128)(2,1)} %bitcast.22), calls=%async_computation.1 | async-start | bytes 786432 | tf_op jit(solution)/shard_map/all_to_all | solution.py:117
  19.2 20.8 %all-gather.2.cloned.1.call-done = bf16[2048,384]{1,0:T(8,128)(2,1)} async-done(((bf16[512,384]{1,0:T(8,128)(2,1)}), bf16[2048,384]{1,0:T(8,128)(2,1)}) %all-gather.2.cloned.1.call-update) | async-done | bytes 1572880 | tf_op jit(solution)/shard_map/all_gather | solution.py:86
  45.2 7.6 %collective-permute-start.1 = (bf16[2,3,16,128,32]{3,2,4,1,0:T(8,128)(2,1)}, bf16[2,3,16,128,32]{3,2,4,1,0:T(8,128)(2,1)}, u32[]{:S(2)}, u32[]{:S(2)}) collective-permute-start(bf16[2,3,16,128,32]{3,2,4,1,0:T(8,128)(2,1)} %bitcast.9), channel_id=1, source_target_pairs={{4,0},{8,4},{12,8},{16,12},{20,16},{24,20},{28,24},{32,28},{36,32}... | collective-permute-start | bytes 2359304 | tf_op jit(solution)/shard_map/ppermute | solution.py:25
  58.3 11.4 %collective-permute-done.1 = bf16[2,3,16,128,32]{3,2,4,1,0:T(8,128)(2,1)} collective-permute-done((bf16[2,3,16,128,32]{3,2,4,1,0:T(8,128)(2,1)}, bf16[2,3,16,128,32]{3,2,4,1,0:T(8,128)(2,1)}, u32[]{:S(2)}, u32[]{:S(2)}) %collective-permute-start.1) | collective-permute-done | bytes 786464 | tf_op jit(solution)/shard_map/ppermute | solution.py:25
  69.7 17.8 %collective-permute-done = bf16[2,3,16,128,32]{3,2,4,1,0:T(8,128)(2,1)} collective-permute-done((bf16[2,3,16,128,32]{3,2,4,1,0:T(8,128)(2,1)}, bf16[2,3,16,128,32]{3,2,4,1,0:T(8,128)(2,1)}, u32[]{:S(2)}, u32[]{:S(2)}) %collective-permute-start) | collective-permute-done | bytes 786464 | tf_op jit(solution)/shard_map/ppermute | solution.py:24
  87.5 3.4 convert_bitcast_fusion
  91.0 3.6 slice_bitcast_fusion
  94.6 13.4 %fusion.3 = (f32[3,16,128]{2,1,0:T(8,128)S(1)}, f32[3,16,128,8,128]{2,4,3,1,0:T(8,128)}) fusion(f32[16,8]{1,0:T(8,128)S(1)} %fusion.104, bf16[3,16,8,128,32]{3,1,2,4,0:T(8,128)(2,1)S(1)} %get-tuple-element.47, bf16[16,128,3,32]{1,0,3,2:T(8,128)(2,1)S(1)} %bitcast.194), kind=kOutput, calls=%fused_computation.6 | convolution fusion | flops 421521408 | bytes 28729856 | tf_op jit(solution)/shard_map/hbqd,hbskd->hbqsk/dot_general | solution.py:102
  107.9 10.9 %fusion.8 = f32[3,16,8,128,32]{3,4,2,1,0:T(8,128)S(1)} fusion(bf16[16,128,3,32]{1,0,3,2:T(8,128)(2,1)S(1)} %copy-done.20, f32[3,16,128,8,128]{2,4,3,1,0:T(8,128)} %get-tuple-element.62, f32[3,16,128]{2,1,0:T(8,128)S(1)} %get-tuple-element.61, f32[16,8]{1,0:T(8,128)S(1)} %fusion.104), kind=kOutput, calls=%fused_computation.11 | convolution fusion | flops 427819008 | bytes 31875584 | tf_op jit(solution)/shard_map/hbqsk,hbqd->hbskd/dot_general | solution.py:123
  118.9 7.5 %fusion.27 = f32[1,3,48,128,32]{3,2,4,1,0:T(8,128)} fusion(f32[3,16,8,128,32]{3,4,2,1,0:T(8,128)S(1)} %fusion.8, s32[16,8]{0,1:T(8,128)S(1)} %add_select_fusion), kind=kOutput, calls=%fused_computation.44 | convolution fusion | flops 905975808 | bytes 8651264 | tf_op jit(solution)/shard_map/bse,hbskd->hekd/dot_general | solution.py:124
  126.4 19.3 %multiply_reduce_fusion = (f32[3,16,128]{2,1,0:T(8,128)S(1)}, f32[3,16,128,8,128]{2,4,3,1,0:T(8,128)}) fusion(f32[3,16,128]{2,1,0:T(8,128)S(1)} %get-tuple-element.61, f32[16,8]{1,0:T(8,128)S(1)} %fusion.104, f32[3,16,128,8,128]{2,4,3,1,0:T(8,128)} %get-tuple-element.62, bf16[3,16,8,128,32]{3,1,2,4,0:T(8,128)(2,1)} %get-tuple-element.48, ...), kind=kOutput, calls=%fused_computation.3 | convolution fusion | flops 434104320 | bytes 53920256 | tf_op jit(solution)/shard_map/hbqd,hbskd->hbqsk/dot_general | solution.py:118
  145.8 22.7 %multiply_convert_fusion = bf16[3,16,128,8,128]{2,4,3,1,0:T(8,128)(2,1)} fusion(f32[3,16,128,8,128]{2,4,3,1,0:T(8,128)} %get-tuple-element.64, f32[3,16,128]{2,1,0:T(8,128)S(1)} %get-tuple-element.63, f32[3,16,128]{2,1,0:T(8,128)S(1)} %get-tuple-element.61, f32[16,8]{1,0:T(8,128)S(1)} %fusion.104, f32[3,16,128,8,128]{2,4,3,1,0:T(8,128)} %get-tuple-element.62), kind=kLoop, calls=%fused_computation.2 | loop fusion | flops 44040192 | bytes 62964224 | tf_op jit(solution)/shard_map/convert_element_type | solution.py:120
  168.5 11.7 %fusion.86 = f32[3,16,8,128,32]{3,4,2,1,0:T(8,128)} fusion(bf16[3,16,128,8,128]{2,4,3,1,0:T(8,128)(2,1)} %multiply_convert_fusion, bf16[16,128,3,32]{1,0,3,2:T(8,128)(2,1)} %bitcast.195), kind=kOutput, calls=%fused_computation.97 | convolution fusion | flops 402653184 | bytes 19267584 | tf_op jit(solution)/shard_map/hbqsk,hbqd->hbskd/dot_general | solution.py:122
  180.2 8.8 %fusion.24 = f32[1,3,48,128,32]{3,2,4,1,0:T(8,128)S(1)} fusion(f32[3,16,8,128,32]{3,4,2,1,0:T(8,128)} %fusion.86, s32[16,8]{0,1:T(8,128)S(1)} %add_select_fusion), kind=kOutput, calls=%fused_computation.43 | convolution fusion | flops 905975808 | bytes 8651264 | tf_op jit(solution)/shard_map/bse,hbskd->hekd/dot_general | solution.py:124
  189.0 2.9 fusion.12
  196.2 4.6 %collective-permute-start.2 = (bf16[2,3,16,128,32]{3,2,4,1,0:T(8,128)(2,1)}, bf16[2,3,16,128,32]{3,2,4,1,0:T(8,128)(2,1)}, u32[]{:S(2)}, u32[]{:S(2)}) collective-permute-start(bf16[2,3,16,128,32]{3,2,4,1,0:T(8,128)(2,1)} %get-tuple-element.51), channel_id=1, source_target_pairs={{0,124},{4,0},{8,4},{12,8},{16,12},{20,16},{24,20},{28,24},{32,28}... | collective-permute-start | bytes 2359304 | tf_op jit(solution)/shard_map/ppermute | solution.py:33
  200.8 3.9 fusion.54
  211.7 5.7 %collective-permute-done.3 = bf16[2,3,16,128,32]{3,2,4,1,0:T(8,128)(2,1)} collective-permute-done((bf16[2,3,16,128,32]{3,2,4,1,0:T(8,128)(2,1)}, bf16[2,3,16,128,32]{3,2,4,1,0:T(8,128)(2,1)}, u32[]{:S(2)}, u32[]{:S(2)}) %collective-permute-start.3) | collective-permute-done | bytes 786464 | tf_op jit(solution)/shard_map/ppermute | solution.py:33
  217.4 12.7 %collective-permute-done.2 = bf16[2,3,16,128,32]{3,2,4,1,0:T(8,128)(2,1)} collective-permute-done((bf16[2,3,16,128,32]{3,2,4,1,0:T(8,128)(2,1)}, bf16[2,3,16,128,32]{3,2,4,1,0:T(8,128)(2,1)}, u32[]{:S(2)}, u32[]{:S(2)}) %collective-permute-start.2) | collective-permute-done | bytes 786464 | tf_op jit(solution)/shard_map/ppermute | solution.py:33
  245.4 12.7 %fusion.60 = bf16[16,128,3,32]{1,3,0,2:T(8,128)(2,1)S(1)} fusion(bf16[3,16,8,128,32]{3,1,2,4,0:T(8,128)(2,1)} %get-tuple-element.48, f32[3,16,128,8,128]{2,4,3,1,0:T(8,128)} %get-tuple-element.62, f32[3,16,128]{2,1,0:T(8,128)S(1)} %get-tuple-element.61, f32[16,8]{1,0:T(8,128)S(1)} %fusion.104), kind=kOutput, calls=%fused_computation.60 | convolution fusion | flops 428015616 | bytes 28729856 | tf_op jit(solution)/shard_map/hbqsk,hbskd->hbqd/dot_general | solution.py:108
  261.0 5.4 %all-to-all-start = ((bf16[4,512,96]{1,2,0:T(8,128)(2,1)}), bf16[4,512,96]{1,2,0:T(8,128)(2,1)S(1)}, u32[]{:S(2)}, u32[]{:S(2)}) async-start(bf16[4,512,96]{1,2,0:T(8,128)(2,1)} %copy.64), calls=%async_computation | async-start | bytes 786432 | tf_op jit(solution)/shard_map/all_to_all | solution.py:111
  266.5 8.3 %all-to-all-done = bf16[4,512,96]{1,2,0:T(8,128)(2,1)S(1)} async-done(((bf16[4,512,96]{1,2,0:T(8,128)(2,1)}), bf16[4,512,96]{1,2,0:T(8,128)(2,1)S(1)}, u32[]{:S(2)}, u32[]{:S(2)}) %all-to-all-start) | async-done | bytes 393248 | tf_op jit(solution)/shard_map/all_to_all | solution.py:111
  276.0 2.8 fusion.57
  292.1 149.3 %all-reduce.2.cloned.1.call-done = f32[1537,384]{1,0:T(8,128)} async-done(((f32[1537,384]{1,0:T(8,128)}), f32[1537,384]{1,0:T(8,128)}) %all-reduce.2.cloned.1.call-update) | async-done | bytes 2360848 | tf_op jit(solution)/shard_map/psum | solution.py:156
  (120 shorter events, 71.1 us)
Async XLA Ops:
  7.2 32.9 %copy-start = (bf16[3,384,384]{2,1,0:T(8,128)(2,1)S(1)}, bf16[3,384,384]{2,1,0:T(8,128)(2,1)}, u32[]{:S(2)}) copy-start(bf16[3,384,384]{2,1,0:T(8,128)(2,1)} %param.17) | copy-start | bytes 2654212
  7.2 32.9 %all-gather.2.cloned.1.call-start = ((), (), s32[]{:S(2)}) async-start(), calls=%async_computation.3 | async-start | bytes 1966080 | tf_op jit(solution)/shard_map/all_gather | solution.py:86
  13.8 39.4 %all-to-all-start.1 = ((bf16[512,4,96]{0,2,1:T(8,128)(2,1)}), bf16[512,4,96]{0,2,1:T(8,128)(2,1)}, u32[]{:S(2)}, u32[]{:S(2)}) async-start(bf16[512,4,96]{0,2,1:T(8,128)(2,1)} %bitcast.22), calls=%async_computation.1 | async-start | bytes 786432 | tf_op jit(solution)/shard_map/all_to_all | solution.py:117
  19.2 265.3 %reduce-scatter.2.cloned.1.call-start = ((), (), s32[]{:S(2)}) async-start(), calls=%async_computation.4 | async-start | bytes 1966080 | tf_op jit(solution)/shard_map/reduce_scatter | solution.py:145
  42.9 10.2 %copy-start.27 = (s32[16,8]{0,1:T(8,128)S(1)}, s32[16,8]{0,1:T(8,128)}, u32[]{:S(2)}) copy-start(s32[16,8]{0,1:T(8,128)} %param.20) | copy-start | bytes 1540
  42.9 10.2 %copy-start.28 = (s32[16]{0:T(128)S(1)}, s32[16]{0:T(128)}, u32[]{:S(2)}) copy-start(s32[16]{0:T(128)} %param.21) | copy-start | bytes 196
  45.2 24.5 %collective-permute-start.1 = (bf16[2,3,16,128,32]{3,2,4,1,0:T(8,128)(2,1)}, bf16[2,3,16,128,32]{3,2,4,1,0:T(8,128)(2,1)}, u32[]{:S(2)}, u32[]{:S(2)}) collective-permute-start(bf16[2,3,16,128,32]{3,2,4,1,0:T(8,128)(2,1)} %bitcast.9), channel_id=1, source_target_pairs={{4,0},{8,4},{12,8},{16,12},{20,16},{24,20},{28,24},{32,28},{36,32}... | collective-permute-start | bytes 2359304 | tf_op jit(solution)/shard_map/ppermute | solution.py:25
  52.8 34.7 %collective-permute-start = (bf16[2,3,16,128,32]{3,2,4,1,0:T(8,128)(2,1)}, bf16[2,3,16,128,32]{3,2,4,1,0:T(8,128)(2,1)}, u32[]{:S(2)}, u32[]{:S(2)}) collective-permute-start(bf16[2,3,16,128,32]{3,2,4,1,0:T(8,128)(2,1)} %bitcast.9), channel_id=1, source_target_pairs={{0,4},{4,8},{8,12},{12,16},{16,20},{20,24},{24,28},{28,32},{32,36}... | collective-permute-start | bytes 2359304 | tf_op jit(solution)/shard_map/ppermute | solution.py:24
  58.2 36.4 %copy-start.8 = (bf16[12,8,16,128]{3,2,1,0:T(8,128)(2,1)}, bf16[12,8,16,128]{3,2,1,0:T(8,128)(2,1)S(1)}, u32[]{:S(2)}) copy-start(bf16[12,8,16,128]{3,2,1,0:T(8,128)(2,1)S(1)} %copy.94) | copy-start | bytes 1179652
  94.6 13.4 %copy-start.2 = (bf16[3,16,8,128,32]{3,1,2,4,0:T(8,128)(2,1)}, bf16[3,16,8,128,32]{3,1,2,4,0:T(8,128)(2,1)S(1)}, u32[]{:S(2)}) copy-start(bf16[3,16,8,128,32]{3,1,2,4,0:T(8,128)(2,1)S(1)} %get-tuple-element.47) | copy-start | bytes 9437188
  94.6 13.4 %copy-start.20 = (bf16[16,128,3,32]{1,0,3,2:T(8,128)(2,1)S(1)}, bf16[16,128,3,32]{1,0,3,2:T(8,128)(2,1)}, u32[]{:S(2)}) copy-start(bf16[16,128,3,32]{1,0,3,2:T(8,128)(2,1)} %reshape.232) | copy-start | bytes 1179652
  180.2 20.6 %copy-start.1 = (bf16[3,16,128,8,128]{2,4,3,1,0:T(8,128)(2,1)S(1)}, bf16[3,16,128,8,128]{2,4,3,1,0:T(8,128)(2,1)}, u32[]{:S(2)}) copy-start(bf16[3,16,128,8,128]{2,4,3,1,0:T(8,128)(2,1)} %multiply_convert_fusion) | copy-start | bytes 37748740
  189.0 2.9 copy-start.5
  191.9 8.9 %copy-start.3 = (bf16[3,16,8,128,32]{3,1,2,4,0:T(8,128)(2,1)S(1)}, bf16[3,16,8,128,32]{3,1,2,4,0:T(8,128)(2,1)}, u32[]{:S(2)}) copy-start(bf16[3,16,8,128,32]{3,1,2,4,0:T(8,128)(2,1)} %copy-done.2) | copy-start | bytes 9437188
  193.5 23.9 %collective-permute-start.3 = (bf16[2,3,16,128,32]{3,2,4,1,0:T(8,128)(2,1)}, bf16[2,3,16,128,32]{3,2,4,1,0:T(8,128)(2,1)}, u32[]{:S(2)}, u32[]{:S(2)}) collective-permute-start(bf16[2,3,16,128,32]{3,2,4,1,0:T(8,128)(2,1)} %get-tuple-element.52), channel_id=1, source_target_pairs={{0,4},{4,8},{8,12},{12,16},{16,20},{20,24},{24,28},{28,32},{32,36}... | collective-permute-start | bytes 2359304 | tf_op jit(solution)/shard_map/ppermute | solution.py:33
  196.2 33.9 %collective-permute-start.2 = (bf16[2,3,16,128,32]{3,2,4,1,0:T(8,128)(2,1)}, bf16[2,3,16,128,32]{3,2,4,1,0:T(8,128)(2,1)}, u32[]{:S(2)}, u32[]{:S(2)}) collective-permute-start(bf16[2,3,16,128,32]{3,2,4,1,0:T(8,128)(2,1)} %get-tuple-element.51), channel_id=1, source_target_pairs={{0,124},{4,0},{8,4},{12,8},{16,12},{20,16},{24,20},{28,24},{32,28}... | collective-permute-start | bytes 2359304 | tf_op jit(solution)/shard_map/ppermute | solution.py:33
  209.2 20.9 %copy-start.4 = (f32[1,3,48,128,32]{3,2,4,1,0:T(8,128)S(1)}, f32[1,3,48,128,32]{3,2,4,1,0:T(8,128)}, u32[]{:S(2)}) copy-start(f32[1,3,48,128,32]{3,2,4,1,0:T(8,128)} %fusion.27) | copy-start | bytes 7077892
  258.2 16.7 %copy-start.9 = (bf16[512,384]{1,0:T(8,128)(2,1)S(1)}, bf16[512,384]{1,0:T(8,128)(2,1)}, u32[]{:S(2)}) copy-start(bf16[512,384]{1,0:T(8,128)(2,1)} %param.19) | copy-start | bytes 1179652
  258.2 17.9 %copy-start.16 = (bf16[2048,384]{1,0:T(8,128)(2,1)S(1)}, bf16[2048,384]{1,0:T(8,128)(2,1)}, u32[]{:S(2)}) copy-start(bf16[2048,384]{1,0:T(8,128)(2,1)} %all-gather.2.cloned.1.call-done) | copy-start | bytes 4718596
  261.0 13.8 %all-to-all-start = ((bf16[4,512,96]{1,2,0:T(8,128)(2,1)}), bf16[4,512,96]{1,2,0:T(8,128)(2,1)S(1)}, u32[]{:S(2)}, u32[]{:S(2)}) async-start(bf16[4,512,96]{1,2,0:T(8,128)(2,1)} %copy.64), calls=%async_computation | async-start | bytes 786432 | tf_op jit(solution)/shard_map/all_to_all | solution.py:111
  266.5 174.9 %all-reduce.2.cloned.1.call-start = ((), (), s32[]{:S(2)}) async-start(), calls=%async_computation.5 | async-start | bytes 4743168 | tf_op jit(solution)/shard_map/psum | solution.py:156
  274.8 4.0 copy-start.10
  286.0 5.0 %copy-start.26 = (f32[512]{0:T(512)S(1)}, f32[512]{0:T(512)}, u32[]{:S(2)}) copy-start(f32[512]{0:T(512)} %get-tuple-element.59) | copy-start | bytes 6148
  444.9 6.0 %copy-start.7 = (f32[1537,384]{1,0:T(8,128)S(1)}, f32[1537,384]{1,0:T(8,128)}, u32[]{:S(2)}) copy-start(f32[1537,384]{1,0:T(8,128)} %all-reduce.2.cloned.1.call-done) | copy-start | bytes 7082500
  (15 other events, 27.9 us)
Sparse Core Ops, SparseCore 0:
  11.7 28.3 all-gather.1
  245.5 27.7 reduce-scatter.1
  288.8 152.5 all-reduce.1

commit v3 on v2

--- a/solution.py
+++ b/solution.py
@@ -83,7 +83,10 @@
     inverse = lax.rsqrt(jnp.mean(tok_f32 * tok_f32, -1, keepdims=True) + norm_eps)
     normed = (tok_f32 * inverse * norm_gain).astype(bf16)
     w_here = lax.dynamic_slice_in_dim(w_qkv, head_index * head_cols, head_cols, 2)
-    gathered = lax.all_gather(normed, "head", axis=0, tiled=True)
+    slab_tok = lax.all_gather(tokens, "head", axis=0, tiled=True).astype(f32)
+    slab_inverse = lax.rsqrt(jnp.mean(slab_tok * slab_tok, -1, keepdims=True) + norm_eps)
+    slab_scaled = slab_tok * slab_inverse
+    gathered = (slab_scaled * norm_gain).astype(bf16)
     projected = jnp.einsum("rd,cde->cre", gathered, w_here, preferred_element_type=f32)
     packed = jnp.stack(
         [unit_heads(projected[0], head_dim), unit_heads(projected[1], head_dim), projected[2]]
@@ -142,14 +145,13 @@
     d_query_part = norm_back(projected[0], d_packed[0], head_dim).astype(bf16)
     d_key_part = norm_back(projected[1], d_packed[1], head_dim).astype(bf16)
     d_qkv = jnp.stack([d_query_part, d_key_part, d_packed[2]])
-    d_normed = lax.psum_scatter(
-        jnp.einsum("crk,cdk->rd", d_qkv, w_here, preferred_element_type=f32).astype(bf16),
-        "head",
-        scatter_dimension=0,
-        tiled=True,
-    ).astype(f32)
+    d_normed_part = jnp.einsum("crk,cdk->rd", d_qkv, w_here, preferred_element_type=f32)
+    d_gain_part = jnp.sum(d_normed_part * slab_scaled, 0)
+    shares = d_normed_part.astype(bf16).reshape(n_head, -1, width)
+    d_normed = jnp.sum(
+        lax.all_to_all(shares, "head", split_axis=0, concat_axis=0, tiled=True).astype(f32), 0
+    )
     d_qkv_part = jnp.einsum("rd,crk->cdk", gathered, d_qkv, preferred_element_type=f32)
-    d_gain_part = jnp.sum(d_normed * tok_f32 * inverse, 0)
     slots = jnp.zeros((n_head,) + d_qkv_part.shape, f32)
     slots = lax.dynamic_update_index_in_dim(slots, d_qkv_part, head_index, 0)
     pieces = [slots.reshape(-1, width), d_out_part, d_gain_part[None]]

time: 462 us -> 458 us (level)
  local copies, waits for them, and re-layouts: 42.8 us -> 34.7 us
    all_to_all x1, waiting for transfers between devices: 8.29 us -> 0.01 us  [local(): lax.all_to_all(from_heads(attended_heads), 'head', split_axis=0, concat_a...]
    psum x1, waiting for transfers between devices: 149 us -> 144 us  [local(): total = lax.psum(jnp.concatenate(pieces, 0), ('slab', 'head'))]
    all_to_all x0 -> x1, starting transfers between devices: none -> 4.93 us  [local(): lax.all_to_all(shares, 'head', split_axis=0, concat_axis=0, tiled=True)]
  transfers between devices with their start and end apart: 9 -> 9, of which waited for: 7 -> 7; matrix products, arithmetic and copies ran while one was open for 11% -> 20% of each run, Pallas kernels for 0% -> 0%
where the time goes in v3:
time: 458 us; the launch traced here: 451 us
  waiting for transfers between devices  222 us (48%)
  matrix products  108 us (24%)
  other arithmetic  41.9 us (9%)
  local copies, waits for them, and re-layouts  34.7 us (8%)
  starting transfers between devices  29.3 us (6%)
  between operations  14.8 us (3%)
    psum x1, waiting for transfers between devices, local(): total = lax.psum(jnp.concatenate(pieces, 0), ('slab', 'head'))  144 us
    all_gather x1, waiting for transfers between devices, local(): slab_tok = lax.all_gather(tokens, 'head', axis=0, tiled=True).astype(f32)  23.1 us
    convert_element_type x1, other arithmetic, local(): d_scores = (exponent_divisor * weights * (d_weights - row_dot)).astype(bf16)  22.2 us
    dot_general x1, matrix products, local(): jnp.einsum('hbqd,hbskd->hbqsk', d_attn, values, preferred_element_type=f32)  19.8 us
    ppermute x1, waiting for transfers between devices, padded(): before = lax.ppermute(last, axis, up)  18.3 us
    dot_general x2, matrix products, local(): jnp.einsum('bse,hbskd->hekd', choose.astype(f32), grads, precision=lax.Pr...  17.4 us
    ppermute x2, waiting for transfers between devices, passed_along(): return lax.ppermute(value, axis, pairs)  17.1 us
    ppermute x1, waiting for transfers between devices, padded(): after = lax.ppermute(first, axis, down)  15.5 us
  transfers between devices with their start and end apart: 9, of which 7 were waited for; matrix products, arithmetic and copies ran while one was open for 20% of the time, Pallas kernels for 0%

profile of v3, /device:TPU:1, one launch (start us, length us, event | category | flops | bytes accessed | tf_op | source)
XLA Modules:
  0.0 451.1 jit_solution(168770848847989604)
XLA Ops:
  10.2 4.8 %all-to-all-start.1 = ((bf16[512,4,96]{0,2,1:T(8,128)(2,1)}), bf16[512,4,96]{0,2,1:T(8,128)(2,1)S(1)}, u32[]{:S(2)}, u32[]{:S(2)}) async-start(bf16[512,4,96]{0,2,1:T(8,128)(2,1)} %bitcast.22), calls=%async_computation.1 | async-start | bytes 786432 | tf_op jit(solution)/shard_map/all_to_all | solution.py:120
  15.0 23.1 %all-gather.2.cloned.1.call-done = bf16[2048,384]{1,0:T(8,128)(2,1)} async-done(((bf16[512,384]{1,0:T(8,128)(2,1)}), bf16[2048,384]{1,0:T(8,128)(2,1)}) %all-gather.2.cloned.1.call-update) | async-done | bytes 1572880 | tf_op jit(solution)/shard_map/all_gather | solution.py:86
  44.5 7.0 %collective-permute-start.1 = (bf16[2,3,16,128,32]{3,2,4,1,0:T(8,128)(2,1)S(1)}, bf16[2,3,16,128,32]{3,2,4,1,0:T(8,128)(2,1)}, u32[]{:S(2)}, u32[]{:S(2)}) collective-permute-start(bf16[2,3,16,128,32]{3,2,4,1,0:T(8,128)(2,1)S(1)} %bitcast.202), channel_id=1, source_target_pairs={{4,0},{8,4},{12,8},{16,12},{20,16},{24,20},{28,24},{32,28},{36,32}... | collective-permute-start | bytes 2359304 | tf_op jit(solution)/shard_map/ppermute | solution.py:25
  52.9 15.5 %collective-permute-done.1 = bf16[2,3,16,128,32]{3,2,4,1,0:T(8,128)(2,1)} collective-permute-done((bf16[2,3,16,128,32]{3,2,4,1,0:T(8,128)(2,1)S(1)}, bf16[2,3,16,128,32]{3,2,4,1,0:T(8,128)(2,1)}, u32[]{:S(2)}, u32[]{:S(2)}) %collective-permute-start.1) | collective-permute-done | bytes 786464 | tf_op jit(solution)/shard_map/ppermute | solution.py:25
  68.4 18.3 %collective-permute-done = bf16[2,3,16,128,32]{3,2,4,1,0:T(8,128)(2,1)} collective-permute-done((bf16[2,3,16,128,32]{3,2,4,1,0:T(8,128)(2,1)S(1)}, bf16[2,3,16,128,32]{3,2,4,1,0:T(8,128)(2,1)}, u32[]{:S(2)}, u32[]{:S(2)}) %collective-permute-start) | collective-permute-done | bytes 786464 | tf_op jit(solution)/shard_map/ppermute | solution.py:24
  86.7 3.2 convert_bitcast_fusion
  92.5 13.6 %fusion.3 = (f32[3,16,128]{2,1,0:T(8,128)S(1)}, f32[3,16,128,8,128]{2,4,3,1,0:T(8,128)}) fusion(f32[16,8]{1,0:T(8,128)S(1)} %fusion.101, bf16[3,16,8,128,32]{3,1,2,4,0:T(8,128)(2,1)S(1)} %get-tuple-element.47, bf16[16,128,3,32]{1,0,3,2:T(8,128)(2,1)S(1)} %bitcast.194), kind=kOutput, calls=%fused_computation.6 | convolution fusion | flops 421521408 | bytes 28729856 | tf_op jit(solution)/shard_map/hbqd,hbskd->hbqsk/dot_general | solution.py:105
  106.2 11.8 %fusion.60 = bf16[16,128,3,32]{1,3,0,2:T(8,128)(2,1)S(1)} fusion(bf16[3,16,8,128,32]{3,1,2,4,0:T(8,128)(2,1)S(1)} %get-tuple-element.48, f32[3,16,128,8,128]{2,4,3,1,0:T(8,128)} %get-tuple-element.62, f32[3,16,128]{2,1,0:T(8,128)S(1)} %get-tuple-element.61, f32[16,8]{1,0:T(8,128)S(1)} %fusion.101), kind=kOutput, calls=%fused_computation.64 | convolution fusion | flops 428015616 | bytes 28729856 | tf_op jit(solution)/shard_map/hbqsk,hbskd->hbqd/dot_general | solution.py:111
  118.0 12.5 %fusion.8 = f32[3,16,8,128,32]{3,4,2,1,0:T(8,128)} fusion(bf16[16,128,3,32]{1,0,3,2:T(8,128)(2,1)S(1)} %reshape.243, f32[3,16,128,8,128]{2,4,3,1,0:T(8,128)} %get-tuple-element.62, f32[3,16,128]{2,1,0:T(8,128)S(1)} %get-tuple-element.61, f32[16,8]{1,0:T(8,128)S(1)} %fusion.101), kind=kOutput, calls=%fused_computation.11 | convolution fusion | flops 427819008 | bytes 31875584 | tf_op jit(solution)/shard_map/hbqsk,hbqd->hbskd/dot_general | solution.py:126
  130.5 19.8 %multiply_reduce_fusion = (f32[3,16,128]{2,1,0:T(8,128)S(1)}, f32[3,16,128,8,128]{2,4,3,1,0:T(8,128)}) fusion(f32[3,16,128]{2,1,0:T(8,128)S(1)} %get-tuple-element.61, f32[16,8]{1,0:T(8,128)S(1)} %fusion.101, f32[3,16,128,8,128]{2,4,3,1,0:T(8,128)} %get-tuple-element.62, bf16[3,16,8,128,32]{3,1,2,4,0:T(8,128)(2,1)} %copy-done.16, ...), kind=kOutput, calls=%fused_computation.3 | convolution fusion | flops 434104320 | bytes 53920256 | tf_op jit(solution)/shard_map/hbqd,hbskd->hbqsk/dot_general | solution.py:121
  151.4 4.9 %all-to-all-start = ((bf16[4,512,96]{1,2,0:T(8,128)(2,1)}), bf16[4,512,96]{1,2,0:T(8,128)(2,1)}, u32[]{:S(2)}, u32[]{:S(2)}) async-start(bf16[4,512,96]{1,2,0:T(8,128)(2,1)} %copy.64), calls=%async_computation | async-start | bytes 786432 | tf_op jit(solution)/shard_map/all_to_all | solution.py:114
  156.3 8.6 %fusion.32 = f32[1,3,48,128,32]{3,2,4,1,0:T(8,128)S(1)} fusion(f32[3,16,8,128,32]{3,4,2,1,0:T(8,128)} %fusion.8, s32[16,8]{0,1:T(8,128)S(1)} %add_select_fusion), kind=kOutput, calls=%fused_computation.46 | convolution fusion | flops 905975808 | bytes 8651264 | tf_op jit(solution)/shard_map/bse,hbskd->hekd/dot_general | solution.py:127
  165.0 22.2 %multiply_convert_fusion = bf16[3,16,128,8,128]{2,4,3,1,0:T(8,128)(2,1)} fusion(f32[3,16,128,8,128]{2,4,3,1,0:T(8,128)} %get-tuple-element.64, f32[3,16,128]{2,1,0:T(8,128)S(1)} %get-tuple-element.63, f32[3,16,128]{2,1,0:T(8,128)S(1)} %get-tuple-element.61, f32[16,8]{1,0:T(8,128)S(1)} %fusion.101, f32[3,16,128,8,128]{2,4,3,1,0:T(8,128)} %get-tuple-element.62), kind=kLoop, calls=%fused_computation.2 | loop fusion | flops 44040192 | bytes 62964224 | tf_op jit(solution)/shard_map/convert_element_type | solution.py:123
  187.2 11.6 %fusion.83 = f32[3,16,8,128,32]{3,4,2,1,0:T(8,128)} fusion(bf16[3,16,128,8,128]{2,4,3,1,0:T(8,128)(2,1)} %multiply_convert_fusion, bf16[16,128,3,32]{1,0,3,2:T(8,128)(2,1)} %bitcast.195), kind=kOutput, calls=%fused_computation.95 | convolution fusion | flops 402653184 | bytes 19267584 | tf_op jit(solution)/shard_map/hbqsk,hbqd->hbskd/dot_general | solution.py:125
  198.8 8.8 %fusion.29 = f32[1,3,48,128,32]{3,2,4,1,0:T(8,128)S(1)} fusion(f32[3,16,8,128,32]{3,4,2,1,0:T(8,128)} %fusion.83, s32[16,8]{0,1:T(8,128)S(1)} %add_select_fusion), kind=kOutput, calls=%fused_computation.45 | convolution fusion | flops 905975808 | bytes 8651264 | tf_op jit(solution)/shard_map/bse,hbskd->hekd/dot_general | solution.py:127
  213.0 4.9 %collective-permute-start.2 = (bf16[2,3,16,128,32]{3,2,4,1,0:T(8,128)(2,1)}, bf16[2,3,16,128,32]{3,2,4,1,0:T(8,128)(2,1)}, u32[]{:S(2)}, u32[]{:S(2)}) collective-permute-start(bf16[2,3,16,128,32]{3,2,4,1,0:T(8,128)(2,1)} %get-tuple-element.51), channel_id=1, source_target_pairs={{0,124},{4,0},{8,4},{12,8},{16,12},{20,16},{24,20},{28,24},{32,28}... | collective-permute-start | bytes 2359304 | tf_op jit(solution)/shard_map/ppermute | solution.py:33
  217.9 3.9 fusion.57
  230.9 4.7 %collective-permute-done.3 = bf16[2,3,16,128,32]{3,2,4,1,0:T(8,128)(2,1)} collective-permute-done((bf16[2,3,16,128,32]{3,2,4,1,0:T(8,128)(2,1)}, bf16[2,3,16,128,32]{3,2,4,1,0:T(8,128)(2,1)}, u32[]{:S(2)}, u32[]{:S(2)}) %collective-permute-start.3) | collective-permute-done | bytes 786464 | tf_op jit(solution)/shard_map/ppermute | solution.py:33
  235.7 12.4 %collective-permute-done.2 = bf16[2,3,16,128,32]{3,2,4,1,0:T(8,128)(2,1)} collective-permute-done((bf16[2,3,16,128,32]{3,2,4,1,0:T(8,128)(2,1)}, bf16[2,3,16,128,32]{3,2,4,1,0:T(8,128)(2,1)}, u32[]{:S(2)}, u32[]{:S(2)}) %collective-permute-start.2) | collective-permute-done | bytes 786464 | tf_op jit(solution)/shard_map/ppermute | solution.py:33
  259.7 3.4 bitcast_convert_fusion
  263.1 4.9 %all-to-all-start.2 = ((bf16[4,512,384]{2,1,0:T(8,128)(2,1)}), bf16[4,512,384]{2,1,0:T(8,128)(2,1)}, u32[]{:S(2)}, u32[]{:S(2)}) async-start(bf16[4,512,384]{2,1,0:T(8,128)(2,1)} %bitcast.193), calls=%async_computation.2 | async-start | bytes 3145728 | tf_op jit(solution)/shard_map/all_to_all | solution.py:152
  277.7 3.3 pad_maximum_fusion.1
  283.3 3.9 all-to-all-done.2
  290.4 143.5 %all-reduce.2.cloned.1.call-done = f32[1537,384]{1,0:T(8,128)} async-done(((f32[1537,384]{1,0:T(8,128)}), f32[1537,384]{1,0:T(8,128)}) %all-reduce.2.cloned.1.call-update) | async-done | bytes 2360848 | tf_op jit(solution)/shard_map/psum | solution.py:158
  (137 shorter events, 65.5 us)
Async XLA Ops:
  7.2 32.7 %copy-start = (bf16[3,384,384]{2,1,0:T(8,128)(2,1)S(1)}, bf16[3,384,384]{2,1,0:T(8,128)(2,1)}, u32[]{:S(2)}) copy-start(bf16[3,384,384]{2,1,0:T(8,128)(2,1)} %param.17) | copy-start | bytes 2654212
  7.2 32.7 %copy-start.33 = (f32[384]{0:T(512)S(1)}, f32[384]{0:T(512)}, u32[]{:S(2)}) copy-start(f32[384]{0:T(512)} %param.16) | copy-start | bytes 4612
  7.2 30.9 %all-gather.2.cloned.1.call-start = ((), (), s32[]{:S(2)}) async-start(), calls=%async_computation.3 | async-start | bytes 1966080 | tf_op jit(solution)/shard_map/all_gather | solution.py:86
  10.2 41.5 %all-to-all-start.1 = ((bf16[512,4,96]{0,2,1:T(8,128)(2,1)}), bf16[512,4,96]{0,2,1:T(8,128)(2,1)S(1)}, u32[]{:S(2)}, u32[]{:S(2)}) async-start(bf16[512,4,96]{0,2,1:T(8,128)(2,1)} %bitcast.22), calls=%async_computation.1 | async-start | bytes 786432 | tf_op jit(solution)/shard_map/all_to_all | solution.py:120
  43.0 8.6 %copy-start.35 = (s32[16,8]{0,1:T(8,128)S(1)}, s32[16,8]{0,1:T(8,128)}, u32[]{:S(2)}) copy-start(s32[16,8]{0,1:T(8,128)} %param.20) | copy-start | bytes 1540
  43.0 8.6 %copy-start.36 = (s32[16]{0:T(128)S(1)}, s32[16]{0:T(128)}, u32[]{:S(2)}) copy-start(s32[16]{0:T(128)} %param.21) | copy-start | bytes 196
  44.5 23.9 %collective-permute-start.1 = (bf16[2,3,16,128,32]{3,2,4,1,0:T(8,128)(2,1)S(1)}, bf16[2,3,16,128,32]{3,2,4,1,0:T(8,128)(2,1)}, u32[]{:S(2)}, u32[]{:S(2)}) collective-permute-start(bf16[2,3,16,128,32]{3,2,4,1,0:T(8,128)(2,1)S(1)} %bitcast.202), channel_id=1, source_target_pairs={{4,0},{8,4},{12,8},{16,12},{20,16},{24,20},{28,24},{32,28},{36,32}... | collective-permute-start | bytes 2359304 | tf_op jit(solution)/shard_map/ppermute | solution.py:25
  51.5 35.1 %collective-permute-start = (bf16[2,3,16,128,32]{3,2,4,1,0:T(8,128)(2,1)S(1)}, bf16[2,3,16,128,32]{3,2,4,1,0:T(8,128)(2,1)}, u32[]{:S(2)}, u32[]{:S(2)}) collective-permute-start(bf16[2,3,16,128,32]{3,2,4,1,0:T(8,128)(2,1)S(1)} %bitcast.203), channel_id=1, source_target_pairs={{0,4},{4,8},{8,12},{12,16},{16,20},{20,24},{24,28},{28,32},{32,36}... | collective-permute-start | bytes 2359304 | tf_op jit(solution)/shard_map/ppermute | solution.py:24
  52.2 40.4 %copy-start.11 = (bf16[12,8,16,128]{3,2,1,0:T(8,128)(2,1)}, bf16[12,8,16,128]{3,2,1,0:T(8,128)(2,1)S(1)}, u32[]{:S(2)}) copy-start(bf16[12,8,16,128]{3,2,1,0:T(8,128)(2,1)S(1)} %copy.94) | copy-start | bytes 1179652
  92.5 13.7 %copy-start.2 = (bf16[3,16,8,128,32]{3,1,2,4,0:T(8,128)(2,1)}, bf16[3,16,8,128,32]{3,1,2,4,0:T(8,128)(2,1)S(1)}, u32[]{:S(2)}) copy-start(bf16[3,16,8,128,32]{3,1,2,4,0:T(8,128)(2,1)S(1)} %get-tuple-element.47) | copy-start | bytes 9437188
  92.5 13.7 %copy-start.16 = (bf16[3,16,8,128,32]{3,1,2,4,0:T(8,128)(2,1)}, bf16[3,16,8,128,32]{3,1,2,4,0:T(8,128)(2,1)S(1)}, u32[]{:S(2)}) copy-start(bf16[3,16,8,128,32]{3,1,2,4,0:T(8,128)(2,1)S(1)} %get-tuple-element.48) | copy-start | bytes 9437188
  151.4 77.2 %all-to-all-start = ((bf16[4,512,96]{1,2,0:T(8,128)(2,1)}), bf16[4,512,96]{1,2,0:T(8,128)(2,1)}, u32[]{:S(2)}, u32[]{:S(2)}) async-start(bf16[4,512,96]{1,2,0:T(8,128)(2,1)} %copy.64), calls=%async_computation | async-start | bytes 786432 | tf_op jit(solution)/shard_map/all_to_all | solution.py:114
  198.8 19.1 %copy-start.1 = (bf16[3,16,128,8,128]{2,4,3,1,0:T(8,128)(2,1)S(1)}, bf16[3,16,128,8,128]{2,4,3,1,0:T(8,128)(2,1)}, u32[]{:S(2)}) copy-start(bf16[3,16,128,8,128]{2,4,3,1,0:T(8,128)(2,1)} %multiply_convert_fusion) | copy-start | bytes 37748740
  209.0 8.9 %copy-start.3 = (bf16[3,16,8,128,32]{3,1,2,4,0:T(8,128)(2,1)S(1)}, bf16[3,16,8,128,32]{3,1,2,4,0:T(8,128)(2,1)}, u32[]{:S(2)}) copy-start(bf16[3,16,8,128,32]{3,1,2,4,0:T(8,128)(2,1)} %copy-done.2) | copy-start | bytes 9437188
  210.6 25.1 %collective-permute-start.3 = (bf16[2,3,16,128,32]{3,2,4,1,0:T(8,128)(2,1)}, bf16[2,3,16,128,32]{3,2,4,1,0:T(8,128)(2,1)}, u32[]{:S(2)}, u32[]{:S(2)}) collective-permute-start(bf16[2,3,16,128,32]{3,2,4,1,0:T(8,128)(2,1)} %get-tuple-element.52), channel_id=1, source_target_pairs={{0,4},{4,8},{8,12},{12,16},{16,20},{20,24},{24,28},{28,32},{32,36}... | collective-permute-start | bytes 2359304 | tf_op jit(solution)/shard_map/ppermute | solution.py:33
  213.0 35.0 %collective-permute-start.2 = (bf16[2,3,16,128,32]{3,2,4,1,0:T(8,128)(2,1)}, bf16[2,3,16,128,32]{3,2,4,1,0:T(8,128)(2,1)}, u32[]{:S(2)}, u32[]{:S(2)}) collective-permute-start(bf16[2,3,16,128,32]{3,2,4,1,0:T(8,128)(2,1)} %get-tuple-element.51), channel_id=1, source_target_pairs={{0,124},{4,0},{8,4},{12,8},{16,12},{20,16},{24,20},{28,24},{32,28}... | collective-permute-start | bytes 2359304 | tf_op jit(solution)/shard_map/ppermute | solution.py:33
  249.9 7.1 %copy-start.28 = (f32[2048,3]{0,1:T(4,128)S(1)}, f32[2048,3]{0,1:T(4,128)}, u32[]{:S(2)}) copy-start(f32[2048,3]{0,1:T(4,128)} %copy-done.27) | copy-start | bytes 73732
  252.7 5.9 %copy-start.32 = (pred[2048,3]{0,1:T(4,128)(4,1)S(1)}, pred[2048,3]{0,1:T(4,128)(4,1)}, u32[]{:S(2)}) copy-start(pred[2048,3]{0,1:T(4,128)(4,1)} %get-tuple-element.70) | copy-start | bytes 18436
  259.7 8.6 %copy-start.7 = (bf16[2048,384]{1,0:T(8,128)(2,1)S(1)}, bf16[2048,384]{1,0:T(8,128)(2,1)}, u32[]{:S(2)}) copy-start(bf16[2048,384]{1,0:T(8,128)(2,1)} %all-gather.2.cloned.1.call-done) | copy-start | bytes 4718596
  259.7 8.6 %copy-start.30 = (f32[2048]{0:T(1024)S(1)}, f32[2048]{0:T(1024)}, u32[]{:S(2)}) copy-start(f32[2048]{0:T(1024)} %copy-done.29) | copy-start | bytes 24580
  263.1 24.1 %all-to-all-start.2 = ((bf16[4,512,384]{2,1,0:T(8,128)(2,1)}), bf16[4,512,384]{2,1,0:T(8,128)(2,1)}, u32[]{:S(2)}, u32[]{:S(2)}) async-start(bf16[4,512,384]{2,1,0:T(8,128)(2,1)} %bitcast.193), calls=%async_computation.2 | async-start | bytes 3145728 | tf_op jit(solution)/shard_map/all_to_all | solution.py:152
  268.1 165.8 %all-reduce.2.cloned.1.call-start = ((), (), s32[]{:S(2)}) async-start(), calls=%async_computation.4 | async-start | bytes 4743168 | tf_op jit(solution)/shard_map/psum | solution.py:158
  281.1 8.2 %copy-start.12 = (bf16[512,384]{1,0:T(8,128)(2,1)S(1)}, bf16[512,384]{1,0:T(8,128)(2,1)}, u32[]{:S(2)}) copy-start(bf16[512,384]{1,0:T(8,128)(2,1)} %param.19) | copy-start | bytes 1179652
  437.4 6.0 %copy-start.8 = (f32[1537,384]{1,0:T(8,128)S(1)}, f32[1537,384]{1,0:T(8,128)}, u32[]{:S(2)}) copy-start(f32[1537,384]{1,0:T(8,128)} %all-reduce.2.cloned.1.call-done) | copy-start | bytes 7082500
  (23 other events, 56.7 us)
Sparse Core Ops, SparseCore 0:
  9.7 28.3 all-gather.1
  281.2 152.6 all-reduce.1

commit v4 on v3

--- a/solution.py
+++ b/solution.py
@@ -51,6 +51,57 @@
     inner = jnp.sum(unit * along, -1, keepdims=True)
     result = (along - jnp.where(active, unit * inner, 0.0)) / divisor
     return result.reshape(projected.shape)
+
+
+def xor_steps():
+    steps = []
+    for axis in ("head", "slab"):
+        size = lax.axis_size(axis)
+        assert size & (size - 1) == 0
+        mask = 1
+        while mask < size:
+            steps.append((axis, mask))
+            mask *= 2
+    return steps
+
+
+def xor_swap(value, axis, mask):
+    size = lax.axis_size(axis)
+    return lax.ppermute(value, axis, [(i, i ^ mask) for i in range(size)])
+
+
+def ordered_pair(held, received, bit):
+    pair = jnp.stack([held, received])
+    first = lax.dynamic_index_in_dim(pair, bit, 0, keepdims=False)
+    second = lax.dynamic_index_in_dim(pair, 1 - bit, 0, keepdims=False)
+    return jnp.concatenate([first, second], 0)
+
+
+def butterfly_gather(value, axis):
+    size = lax.axis_size(axis)
+    held = value
+    mask = 1
+    while mask < size:
+        bit = (lax.axis_index(axis) // mask) % 2
+        held = ordered_pair(held, xor_swap(held, axis, mask), bit)
+        mask *= 2
+    return held
+
+
+def butterfly_psum(value):
+    steps = xor_steps()
+    held = value
+    bits = []
+    for axis, mask in steps:
+        bit = (lax.axis_index(axis) // mask) % 2
+        halves = held.reshape((2, held.shape[0] // 2) + held.shape[1:])
+        keep = lax.dynamic_index_in_dim(halves, bit, 0, keepdims=False)
+        send = lax.dynamic_index_in_dim(halves, 1 - bit, 0, keepdims=False)
+        held = keep + xor_swap(send, axis, mask)
+        bits.append(bit)
+    for (axis, mask), bit in reversed(list(zip(steps, bits))):
+        held = ordered_pair(held, xor_swap(held, axis, mask), bit)
+    return held
 
 
 def to_heads(value, blocks, heads_here, head_dim):
@@ -83,7 +134,7 @@
     inverse = lax.rsqrt(jnp.mean(tok_f32 * tok_f32, -1, keepdims=True) + norm_eps)
     normed = (tok_f32 * inverse * norm_gain).astype(bf16)
     w_here = lax.dynamic_slice_in_dim(w_qkv, head_index * head_cols, head_cols, 2)
-    slab_tok = lax.all_gather(tokens, "head", axis=0, tiled=True).astype(f32)
+    slab_tok = butterfly_gather(tokens, "head").astype(f32)
     slab_inverse = lax.rsqrt(jnp.mean(slab_tok * slab_tok, -1, keepdims=True) + norm_eps)
     slab_scaled = slab_tok * slab_inverse
     gathered = (slab_scaled * norm_gain).astype(bf16)
@@ -155,7 +206,10 @@
     slots = jnp.zeros((n_head,) + d_qkv_part.shape, f32)
     slots = lax.dynamic_update_index_in_dim(slots, d_qkv_part, head_index, 0)
     pieces = [slots.reshape(-1, width), d_out_part, d_gain_part[None]]
-    total = lax.psum(jnp.concatenate(pieces, 0), ("slab", "head"))
+    rows = sum(piece.shape[0] for piece in pieces)
+    n_dev = n_head * n_slab
+    pieces.append(jnp.zeros((-rows % n_dev, width), f32))
+    total = butterfly_psum(jnp.concatenate(pieces, 0))
     slot_rows = pieces[0].shape[0]
     all_slots = total[:slot_rows].reshape(slots.shape)
     d_w_qkv = lax.dynamic_index_in_dim(all_slots, head_index, 0, keepdims=False)

time: 458 us -> 406 us (0.89)
  the two profiles are of different devices: /device:TPU:1 before, /device:TPU:0 now
where the time goes in v4:
time: 406 us; the launch traced here: 399 us
  waiting for transfers between devices  163 us (40%)
  matrix products  105 us (26%)
  other arithmetic  46.6 us (11%)
  starting transfers between devices  44.3 us (11%)
  local copies, waits for them, and re-layouts  38 us (9%)
    ppermute x16, waiting for transfers between devices, xor_swap(): return lax.ppermute(value, axis, [(i, i ^ mask) for i in range(size)])  106 us
    convert_element_type x1, other arithmetic, local(): d_scores = (exponent_divisor * weights * (d_weights - row_dot)).astype(bf16)  22.3 us
    dot_general x1, matrix products, local(): jnp.einsum('hbqd,hbskd->hbqsk', d_attn, values, preferred_element_type=f32)  19.3 us
    dot_general x2, matrix products, local(): jnp.einsum('bse,hbskd->hekd', choose.astype(f32), grads, precision=lax.Pr...  17.4 us
    ppermute x2, waiting for transfers between devices, passed_along(): return lax.ppermute(value, axis, pairs)  17.1 us
    ppermute x1, waiting for transfers between devices, padded(): after = lax.ppermute(first, axis, down)  16.6 us
    ppermute x1, waiting for transfers between devices, padded(): before = lax.ppermute(last, axis, up)  15.4 us
    dot_general x1, matrix products, local(): jnp.einsum('hbqd,hbskd->hbqsk', q_heads, keys, preferred_element_type=f32)  13.7 us
  transfers between devices with their start and end apart: 23, of which 20 were waited for; matrix products, arithmetic and copies ran while one was open for 20% of the time, Pallas kernels for 0%

profile of v4, /device:TPU:0, one launch (start us, length us, event | category | flops | bytes accessed | tf_op | source)
XLA Modules:
  0.0 398.6 jit_solution(8996631664837631945)
XLA Ops:
  11.3 14.4 %collective-permute-done.1 = bf16[1024,384]{1,0:T(8,128)(2,1)S(1)} collective-permute-done((bf16[1024,384]{1,0:T(8,128)(2,1)}, bf16[1024,384]{1,0:T(8,128)(2,1)S(1)}, u32[]{:S(2)}, u32[]{:S(2)}) %collective-permute-start.1) | collective-permute-done | bytes 786464 | tf_op jit(solution)/shard_map/ppermute | solution.py:70
  30.1 9.1 %collective-permute-start.3 = (bf16[2,3,16,128,32]{3,2,4,1,0:T(8,128)(2,1)S(1)}, bf16[2,3,16,128,32]{3,2,4,1,0:T(8,128)(2,1)}, u32[]{:S(2)}, u32[]{:S(2)}) collective-permute-start(bf16[2,3,16,128,32]{3,2,4,1,0:T(8,128)(2,1)S(1)} %bitcast.302), channel_id=1, source_target_pairs={{4,0},{8,4},{12,8},{16,12},{20,16},{24,20},{28,24},{32,28},{36,32}... | collective-permute-start | bytes 2359304 | tf_op jit(solution)/shard_map/ppermute | solution.py:25
  40.6 16.6 %collective-permute-done.3 = bf16[2,3,16,128,32]{3,2,4,1,0:T(8,128)(2,1)} collective-permute-done((bf16[2,3,16,128,32]{3,2,4,1,0:T(8,128)(2,1)S(1)}, bf16[2,3,16,128,32]{3,2,4,1,0:T(8,128)(2,1)}, u32[]{:S(2)}, u32[]{:S(2)}) %collective-permute-start.3) | collective-permute-done | bytes 786464 | tf_op jit(solution)/shard_map/ppermute | solution.py:25
  57.1 15.4 %collective-permute-done.2 = bf16[2,3,16,128,32]{3,2,4,1,0:T(8,128)(2,1)} collective-permute-done((bf16[2,3,16,128,32]{3,2,4,1,0:T(8,128)(2,1)S(1)}, bf16[2,3,16,128,32]{3,2,4,1,0:T(8,128)(2,1)}, u32[]{:S(2)}, u32[]{:S(2)}) %collective-permute-start.2) | collective-permute-done | bytes 786464 | tf_op jit(solution)/shard_map/ppermute | solution.py:24
  78.4 13.7 %fusion.3 = (f32[3,16,128]{2,1,0:T(8,128)S(1)}, f32[3,16,128,8,128]{2,4,3,1,0:T(8,128)}) fusion(f32[16,8]{1,0:T(8,128)S(1)} %fusion.138, bf16[3,16,8,128,32]{3,1,2,4,0:T(8,128)(2,1)S(1)} %get-tuple-element.47, bf16[16,128,3,32]{1,0,3,2:T(8,128)(2,1)S(1)} %bitcast.294), kind=kOutput, calls=%fused_computation.6 | convolution fusion | flops 421521408 | bytes 28729856 | tf_op jit(solution)/shard_map/hbqd,hbskd->hbqsk/dot_general | solution.py:156
  92.0 11.8 %fusion.63 = bf16[16,128,3,32]{1,3,0,2:T(8,128)(2,1)S(1)} fusion(bf16[3,16,8,128,32]{3,1,2,4,0:T(8,128)(2,1)S(1)} %get-tuple-element.48, f32[3,16,128,8,128]{2,4,3,1,0:T(8,128)} %get-tuple-element.90, f32[3,16,128]{2,1,0:T(8,128)S(1)} %get-tuple-element.89, f32[16,8]{1,0:T(8,128)S(1)} %fusion.138), kind=kOutput, calls=%fused_computation.83 | convolution fusion | flops 428015616 | bytes 28729856 | tf_op jit(solution)/shard_map/hbqsk,hbskd->hbqd/dot_general | solution.py:162
  103.8 12.5 %fusion.8 = f32[3,16,8,128,32]{3,4,2,1,0:T(8,128)} fusion(bf16[16,128,3,32]{1,0,3,2:T(8,128)(2,1)S(1)} %reshape.267, f32[3,16,128,8,128]{2,4,3,1,0:T(8,128)} %get-tuple-element.90, f32[3,16,128]{2,1,0:T(8,128)S(1)} %get-tuple-element.89, f32[16,8]{1,0:T(8,128)S(1)} %fusion.138), kind=kOutput, calls=%fused_computation.11 | convolution fusion | flops 427819008 | bytes 31875584 | tf_op jit(solution)/shard_map/hbqsk,hbqd->hbskd/dot_general | solution.py:177
  116.4 19.3 %multiply_reduce_fusion = (f32[3,16,128]{2,1,0:T(8,128)S(1)}, f32[3,16,128,8,128]{2,4,3,1,0:T(8,128)}) fusion(f32[3,16,128]{2,1,0:T(8,128)S(1)} %get-tuple-element.89, f32[16,8]{1,0:T(8,128)S(1)} %fusion.138, f32[3,16,128,8,128]{2,4,3,1,0:T(8,128)} %get-tuple-element.90, bf16[3,16,8,128,32]{3,1,2,4,0:T(8,128)(2,1)} %copy-done.21, ...), kind=kOutput, calls=%fused_computation.3 | convolution fusion | flops 434104320 | bytes 53920256 | tf_op jit(solution)/shard_map/hbqd,hbskd->hbqsk/dot_general | solution.py:172
  136.8 13.0 %all-to-all-start = ((bf16[4,512,96]{1,2,0:T(8,128)(2,1)}), bf16[4,512,96]{1,2,0:T(8,128)(2,1)}, u32[]{:S(2)}, u32[]{:S(2)}) async-start(bf16[4,512,96]{1,2,0:T(8,128)(2,1)} %copy.62), calls=%async_computation | async-start | bytes 786432 | tf_op jit(solution)/shard_map/all_to_all | solution.py:165
  149.8 8.6 %fusion.32 = f32[1,3,48,128,32]{3,2,4,1,0:T(8,128)S(1)} fusion(f32[3,16,8,128,32]{3,4,2,1,0:T(8,128)} %fusion.8, s32[16,8]{0,1:T(8,128)S(1)} %add_select_fusion), kind=kOutput, calls=%fused_computation.54 | convolution fusion | flops 905975808 | bytes 8651264 | tf_op jit(solution)/shard_map/bse,hbskd->hekd/dot_general | solution.py:178
  158.4 22.3 %multiply_convert_fusion = bf16[3,16,128,8,128]{2,4,3,1,0:T(8,128)(2,1)} fusion(f32[3,16,128,8,128]{2,4,3,1,0:T(8,128)} %get-tuple-element.92, f32[3,16,128]{2,1,0:T(8,128)S(1)} %get-tuple-element.91, f32[3,16,128]{2,1,0:T(8,128)S(1)} %get-tuple-element.89, f32[16,8]{1,0:T(8,128)S(1)} %fusion.138, f32[3,16,128,8,128]{2,4,3,1,0:T(8,128)} %get-tuple-element.90), kind=kLoop, calls=%fused_computation.2 | loop fusion | flops 44040192 | bytes 62964224 | tf_op jit(solution)/shard_map/convert_element_type | solution.py:174
  180.7 11.7 %fusion.98 = f32[3,16,8,128,32]{3,4,2,1,0:T(8,128)} fusion(bf16[3,16,128,8,128]{2,4,3,1,0:T(8,128)(2,1)} %multiply_convert_fusion, bf16[16,128,3,32]{1,0,3,2:T(8,128)(2,1)} %bitcast.295), kind=kOutput, calls=%fused_computation.139 | convolution fusion | flops 402653184 | bytes 19267584 | tf_op jit(solution)/shard_map/hbqsk,hbqd->hbskd/dot_general | solution.py:176
  192.4 8.8 %fusion.29 = f32[1,3,48,128,32]{3,2,4,1,0:T(8,128)S(1)} fusion(f32[3,16,8,128,32]{3,4,2,1,0:T(8,128)} %fusion.98, s32[16,8]{0,1:T(8,128)S(1)} %add_select_fusion), kind=kOutput, calls=%fused_computation.53 | convolution fusion | flops 905975808 | bytes 8651264 | tf_op jit(solution)/shard_map/bse,hbskd->hekd/dot_general | solution.py:178
  225.2 5.4 %collective-permute-done.5 = bf16[2,3,16,128,32]{3,2,4,1,0:T(8,128)(2,1)} collective-permute-done((bf16[2,3,16,128,32]{3,2,4,1,0:T(8,128)(2,1)}, bf16[2,3,16,128,32]{3,2,4,1,0:T(8,128)(2,1)}, u32[]{:S(2)}, u32[]{:S(2)}) %collective-permute-start.5) | collective-permute-done | bytes 786464 | tf_op jit(solution)/shard_map/ppermute | solution.py:33
  230.5 11.7 %collective-permute-done.4 = bf16[2,3,16,128,32]{3,2,4,1,0:T(8,128)(2,1)} collective-permute-done((bf16[2,3,16,128,32]{3,2,4,1,0:T(8,128)(2,1)}, bf16[2,3,16,128,32]{3,2,4,1,0:T(8,128)(2,1)}, u32[]{:S(2)}, u32[]{:S(2)}) %collective-permute-start.4) | collective-permute-done | bytes 786464 | tf_op jit(solution)/shard_map/ppermute | solution.py:33
  266.0 7.0 %concatenate.43 = f32[1664,384]{1,0:T(8,128)S(1)} concatenate(f32[1152,384]{1,0:T(8,128)} %reshape.269, f32[384,384]{1,0:T(8,128)} %fusion.153, f32[1,384]{1,0:T(1,128)S(1)} %broadcast_in_dim.60, f32[127,384]{1,0:T(8,128)} %broadcast_in_dim.61), dimensions={0} | concatenate | bytes 5111808 | tf_op jit(solution)/shard_map/concatenate | solution.py:212
  278.6 15.4 %collective-permute-done.7 = f32[416,384]{1,0:T(8,128)S(1)} collective-permute-done((f32[416,384]{1,0:T(8,128)S(1)}, f32[416,384]{1,0:T(8,128)S(1)}, u32[]{:S(2)}, u32[]{:S(2)}) %collective-permute-start.7) | collective-permute-done | bytes 639008 | tf_op jit(solution)/shard_map/ppermute | solution.py:70
  295.3 10.2 %collective-permute-done.8 = f32[208,384]{1,0:T(8,128)S(1)} collective-permute-done((f32[208,384]{1,0:T(8,128)S(1)}, f32[208,384]{1,0:T(8,128)S(1)}, u32[]{:S(2)}, u32[]{:S(2)}) %collective-permute-start.8) | collective-permute-done | bytes 319520 | tf_op jit(solution)/shard_map/ppermute | solution.py:70
  305.7 5.8 %collective-permute-done.9 = f32[104,384]{1,0:T(8,128)S(1)} collective-permute-done((f32[104,384]{1,0:T(8,128)S(1)}, f32[104,384]{1,0:T(8,128)S(1)}, u32[]{:S(2)}, u32[]{:S(2)}) %collective-permute-start.9) | collective-permute-done | bytes 159776 | tf_op jit(solution)/shard_map/ppermute | solution.py:70
  311.9 5.9 %collective-permute-done.10 = f32[52,384]{1,0:T(8,128)S(1)} collective-permute-done((f32[52,384]{1,0:T(8,128)S(1)}, f32[52,384]{1,0:T(8,128)S(1)}, u32[]{:S(2)}, u32[]{:S(2)}) %collective-permute-start.10) | collective-permute-done | bytes 79904 | tf_op jit(solution)/shard_map/ppermute | solution.py:70
  343.4 5.2 %collective-permute-done.16 = f32[104,384]{1,0:T(8,128)S(1)} collective-permute-done((f32[104,384]{1,0:T(8,128)S(1)}, f32[104,384]{1,0:T(8,128)S(1)}, u32[]{:S(2)}, u32[]{:S(2)}) %collective-permute-start.16) | collective-permute-done | bytes 159776 | tf_op jit(solution)/shard_map/ppermute | solution.py:70
  349.3 11.5 %collective-permute-done.17 = f32[208,384]{1,0:T(8,128)S(1)} collective-permute-done((f32[208,384]{1,0:T(8,128)S(1)}, f32[208,384]{1,0:T(8,128)S(1)}, u32[]{:S(2)}, u32[]{:S(2)}) %collective-permute-start.17) | collective-permute-done | bytes 319520 | tf_op jit(solution)/shard_map/ppermute | solution.py:70
  365.8 10.2 %collective-permute-done.18 = f32[416,384]{1,0:T(8,128)} collective-permute-done((f32[416,384]{1,0:T(8,128)}, f32[416,384]{1,0:T(8,128)}, u32[]{:S(2)}, u32[]{:S(2)}) %collective-permute-start.18) | collective-permute-done | bytes 639008 | tf_op jit(solution)/shard_map/ppermute | solution.py:70
  381.2 8.1 %all-to-all-done.2 = bf16[4,512,384]{2,1,0:T(8,128)(2,1)S(1)} async-done(((bf16[4,512,384]{2,1,0:T(8,128)(2,1)}), bf16[4,512,384]{2,1,0:T(8,128)(2,1)S(1)}, u32[]{:S(2)}, u32[]{:S(2)}) %all-to-all-start.2) | async-done | bytes 1572896 | tf_op jit(solution)/shard_map/all_to_all | solution.py:203
  (200 shorter events, 123.2 us)
Async XLA Ops:
  0.7 2.0 collective-permute-start
  5.1 20.6 %collective-permute-start.1 = (bf16[1024,384]{1,0:T(8,128)(2,1)}, bf16[1024,384]{1,0:T(8,128)(2,1)S(1)}, u32[]{:S(2)}, u32[]{:S(2)}) collective-permute-start(bf16[1024,384]{1,0:T(8,128)(2,1)} %get-tuple-element.67), channel_id=1, source_target_pairs={{0,2},{1,3},{2,0},{3,1},{4,6},{5,7},{6,4},{7,5},{8,10},{9,11},{10,... | collective-permute-start | bytes 2359304 | tf_op jit(solution)/shard_map/ppermute | solution.py:70
  7.8 31.5 %all-to-all-start.1 = ((bf16[512,4,96]{0,2,1:T(8,128)(2,1)}), bf16[512,4,96]{0,2,1:T(8,128)(2,1)S(1)}, u32[]{:S(2)}, u32[]{:S(2)}) async-start(bf16[512,4,96]{0,2,1:T(8,128)(2,1)} %bitcast.30), calls=%async_computation.1 | async-start | bytes 786432 | tf_op jit(solution)/shard_map/all_to_all | solution.py:171
  30.1 27.0 %collective-permute-start.3 = (bf16[2,3,16,128,32]{3,2,4,1,0:T(8,128)(2,1)S(1)}, bf16[2,3,16,128,32]{3,2,4,1,0:T(8,128)(2,1)}, u32[]{:S(2)}, u32[]{:S(2)}) collective-permute-start(bf16[2,3,16,128,32]{3,2,4,1,0:T(8,128)(2,1)S(1)} %bitcast.302), channel_id=1, source_target_pairs={{4,0},{8,4},{12,8},{16,12},{20,16},{24,20},{28,24},{32,28},{36,32}... | collective-permute-start | bytes 2359304 | tf_op jit(solution)/shard_map/ppermute | solution.py:25
  39.2 33.3 %collective-permute-start.2 = (bf16[2,3,16,128,32]{3,2,4,1,0:T(8,128)(2,1)S(1)}, bf16[2,3,16,128,32]{3,2,4,1,0:T(8,128)(2,1)}, u32[]{:S(2)}, u32[]{:S(2)}) collective-permute-start(bf16[2,3,16,128,32]{3,2,4,1,0:T(8,128)(2,1)S(1)} %bitcast.303), channel_id=1, source_target_pairs={{0,4},{4,8},{8,12},{12,16},{16,20},{20,24},{24,28},{28,32},{32,36}... | collective-permute-start | bytes 2359304 | tf_op jit(solution)/shard_map/ppermute | solution.py:24
  39.8 38.6 %copy-start.15 = (bf16[12,8,16,128]{3,2,1,0:T(8,128)(2,1)}, bf16[12,8,16,128]{3,2,1,0:T(8,128)(2,1)S(1)}, u32[]{:S(2)}) copy-start(bf16[12,8,16,128]{3,2,1,0:T(8,128)(2,1)S(1)} %copy.92) | copy-start | bytes 1179652
  136.8 86.0 %all-to-all-start = ((bf16[4,512,96]{1,2,0:T(8,128)(2,1)}), bf16[4,512,96]{1,2,0:T(8,128)(2,1)}, u32[]{:S(2)}, u32[]{:S(2)}) async-start(bf16[4,512,96]{1,2,0:T(8,128)(2,1)} %copy.62), calls=%async_computation | async-start | bytes 786432 | tf_op jit(solution)/shard_map/all_to_all | solution.py:165
  204.1 26.5 %collective-permute-start.5 = (bf16[2,3,16,128,32]{3,2,4,1,0:T(8,128)(2,1)}, bf16[2,3,16,128,32]{3,2,4,1,0:T(8,128)(2,1)}, u32[]{:S(2)}, u32[]{:S(2)}) collective-permute-start(bf16[2,3,16,128,32]{3,2,4,1,0:T(8,128)(2,1)} %get-tuple-element.54), channel_id=1, source_target_pairs={{0,4},{4,8},{8,12},{12,16},{16,20},{20,24},{24,28},{28,32},{32,36}... | collective-permute-start | bytes 2359304 | tf_op jit(solution)/shard_map/ppermute | solution.py:33
  207.1 35.1 %collective-permute-start.4 = (bf16[2,3,16,128,32]{3,2,4,1,0:T(8,128)(2,1)}, bf16[2,3,16,128,32]{3,2,4,1,0:T(8,128)(2,1)}, u32[]{:S(2)}, u32[]{:S(2)}) collective-permute-start(bf16[2,3,16,128,32]{3,2,4,1,0:T(8,128)(2,1)} %get-tuple-element.53), channel_id=1, source_target_pairs={{0,124},{4,0},{8,4},{12,8},{16,12},{20,16},{24,20},{28,24},{32,28}... | collective-permute-start | bytes 2359304 | tf_op jit(solution)/shard_map/ppermute | solution.py:33
  273.1 3.1 collective-permute-start.6
  277.5 16.5 %collective-permute-start.7 = (f32[416,384]{1,0:T(8,128)S(1)}, f32[416,384]{1,0:T(8,128)S(1)}, u32[]{:S(2)}, u32[]{:S(2)}) collective-permute-start(f32[416,384]{1,0:T(8,128)S(1)} %dynamic-slice_bitcast_fusion.1), channel_id=1, source_target_pairs={{0,2},{1,3},{2,0},{3,1},{4,6},{5,7},{6,4},{7,5},{8,10},{9,11},{10,... | collective-permute-start | bytes 1916936 | tf_op jit(solution)/shard_map/ppermute | solution.py:70
  295.2 10.3 %collective-permute-start.8 = (f32[208,384]{1,0:T(8,128)S(1)}, f32[208,384]{1,0:T(8,128)S(1)}, u32[]{:S(2)}, u32[]{:S(2)}) collective-permute-start(f32[208,384]{1,0:T(8,128)S(1)} %dynamic-slice_bitcast_fusion.2), channel_id=1, source_target_pairs={{0,4},{4,0},{8,12},{12,8},{16,20},{20,16},{24,28},{28,24},{32,36},... | collective-permute-start | bytes 958472 | tf_op jit(solution)/shard_map/ppermute | solution.py:70
  305.5 5.9 %collective-permute-start.9 = (f32[104,384]{1,0:T(8,128)S(1)}, f32[104,384]{1,0:T(8,128)S(1)}, u32[]{:S(2)}, u32[]{:S(2)}) collective-permute-start(f32[104,384]{1,0:T(8,128)S(1)} %dynamic-slice_bitcast_fusion.3), channel_id=1, source_target_pairs={{0,8},{4,12},{8,0},{12,4},{16,24},{20,28},{24,16},{28,20},{32,40},... | collective-permute-start | bytes 479240 | tf_op jit(solution)/shard_map/ppermute | solution.py:70
  311.5 6.3 %collective-permute-start.10 = (f32[52,384]{1,0:T(8,128)S(1)}, f32[52,384]{1,0:T(8,128)S(1)}, u32[]{:S(2)}, u32[]{:S(2)}) collective-permute-start(f32[52,384]{1,0:T(8,128)S(1)} %dynamic-slice_bitcast_fusion.4), channel_id=1, source_target_pairs={{0,16},{4,20},{8,24},{12,28},{16,0},{20,4},{24,8},{28,12},{32,48},... | collective-permute-start | bytes 239624 | tf_op jit(solution)/shard_map/ppermute | solution.py:70
  317.9 4.2 %collective-permute-start.11 = (f32[26,384]{1,0:T(8,128)S(1)}, f32[26,384]{1,0:T(8,128)S(1)}, u32[]{:S(2)}, u32[]{:S(2)}) collective-permute-start(f32[26,384]{1,0:T(8,128)S(1)} %dynamic-slice_bitcast_fusion.5), channel_id=1, source_target_pairs={{0,32},{4,36},{8,40},{12,44},{16,48},{20,52},{24,56},{28,60},{32,0... | collective-permute-start | bytes 119816 | tf_op jit(solution)/shard_map/ppermute | solution.py:70
  322.1 5.4 %collective-permute-start.12 = (f32[13,384]{1,0:T(8,128)S(1)}, f32[13,384]{1,0:T(8,128)S(1)}, u32[]{:S(2)}, u32[]{:S(2)}) collective-permute-start(f32[13,384]{1,0:T(8,128)S(1)} %dynamic-slice_bitcast_fusion.6), channel_id=1, source_target_pairs={{0,64},{4,68},{8,72},{12,76},{16,80},{20,84},{24,88},{28,92},{32,9... | collective-permute-start | bytes 59912 | tf_op jit(solution)/shard_map/ppermute | solution.py:70
  327.5 5.3 %collective-permute-start.13 = (f32[13,384]{1,0:T(8,128)S(1)}, f32[13,384]{1,0:T(8,128)S(1)}, u32[]{:S(2)}, u32[]{:S(2)}) collective-permute-start(f32[13,384]{1,0:T(8,128)S(1)} %bitcast_add_fusion.6), channel_id=1, source_target_pairs={{0,64},{4,68},{8,72},{12,76},{16,80},{20,84},{24,88},{28,92},{32,9... | collective-permute-start | bytes 59912 | tf_op jit(solution)/shard_map/ppermute | solution.py:70
  332.9 4.2 %collective-permute-start.14 = (f32[26,384]{1,0:T(8,128)S(1)}, f32[26,384]{1,0:T(8,128)S(1)}, u32[]{:S(2)}, u32[]{:S(2)}) collective-permute-start(f32[26,384]{1,0:T(8,128)S(1)} %get-tuple-element.83), channel_id=1, source_target_pairs={{0,32},{4,36},{8,40},{12,44},{16,48},{20,52},{24,56},{28,60},{32,0... | collective-permute-start | bytes 119816 | tf_op jit(solution)/shard_map/ppermute | solution.py:70
  337.1 6.1 %collective-permute-start.15 = (f32[52,384]{1,0:T(8,128)S(1)}, f32[52,384]{1,0:T(8,128)S(1)}, u32[]{:S(2)}, u32[]{:S(2)}) collective-permute-start(f32[52,384]{1,0:T(8,128)S(1)} %pad_maximum_fusion.12), channel_id=1, source_target_pairs={{0,16},{4,20},{8,24},{12,28},{16,0},{20,4},{24,8},{28,12},{32,48},... | collective-permute-start | bytes 239624 | tf_op jit(solution)/shard_map/ppermute | solution.py:70
  343.3 5.4 %collective-permute-start.16 = (f32[104,384]{1,0:T(8,128)S(1)}, f32[104,384]{1,0:T(8,128)S(1)}, u32[]{:S(2)}, u32[]{:S(2)}) collective-permute-start(f32[104,384]{1,0:T(8,128)S(1)} %pad_maximum_fusion.11), channel_id=1, source_target_pairs={{0,8},{4,12},{8,0},{12,4},{16,24},{20,28},{24,16},{28,20},{32,40},... | collective-permute-start | bytes 479240 | tf_op jit(solution)/shard_map/ppermute | solution.py:70
  348.7 12.0 %collective-permute-start.17 = (f32[208,384]{1,0:T(8,128)S(1)}, f32[208,384]{1,0:T(8,128)S(1)}, u32[]{:S(2)}, u32[]{:S(2)}) collective-permute-start(f32[208,384]{1,0:T(8,128)S(1)} %get-tuple-element.75), channel_id=1, source_target_pairs={{0,4},{4,0},{8,12},{12,8},{16,20},{20,16},{24,28},{28,24},{32,36},... | collective-permute-start | bytes 958472 | tf_op jit(solution)/shard_map/ppermute | solution.py:70
  361.8 14.2 %collective-permute-start.18 = (f32[416,384]{1,0:T(8,128)}, f32[416,384]{1,0:T(8,128)}, u32[]{:S(2)}, u32[]{:S(2)}) collective-permute-start(f32[416,384]{1,0:T(8,128)} %get-tuple-element.71), channel_id=1, source_target_pairs={{0,2},{1,3},{2,0},{3,1},{4,6},{5,7},{6,4},{7,5},{8,10},{9,11},{10,... | collective-permute-start | bytes 1916936 | tf_op jit(solution)/shard_map/ppermute | solution.py:70
  362.2 27.1 %all-to-all-start.2 = ((bf16[4,512,384]{2,1,0:T(8,128)(2,1)}), bf16[4,512,384]{2,1,0:T(8,128)(2,1)S(1)}, u32[]{:S(2)}, u32[]{:S(2)}) async-start(bf16[4,512,384]{2,1,0:T(8,128)(2,1)} %bitcast.290), calls=%async_computation.2 | async-start | bytes 3145728 | tf_op jit(solution)/shard_map/all_to_all | solution.py:203
  378.9 12.0 %collective-permute-start.19 = (f32[832,384]{1,0:T(8,128)}, f32[832,384]{1,0:T(8,128)}, u32[]{:S(2)}, u32[]{:S(2)}) collective-permute-start(f32[832,384]{1,0:T(8,128)} %get-tuple-element.61), channel_id=1, source_target_pairs={{0,1},{1,0},{2,3},{3,2},{4,5},{5,4},{6,7},{7,6},{8,9},{9,8},{10,11... | collective-permute-start | bytes 3833864 | tf_op jit(solution)/shard_map/ppermute | solution.py:70
  (37 other events, 217.4 us)

commit v5 on v4

--- a/solution.py
+++ b/solution.py
@@ -88,20 +88,23 @@
     return held
 
 
-def butterfly_psum(value):
+def butterfly_psum(value, wire, tie, tie_step):
     steps = xor_steps()
     held = value
     bits = []
-    for axis, mask in steps:
+    for index, (axis, mask) in enumerate(steps):
+        if index == tie_step:
+            held, tie = lax.optimization_barrier((held, tie))
         bit = (lax.axis_index(axis) // mask) % 2
         halves = held.reshape((2, held.shape[0] // 2) + held.shape[1:])
         keep = lax.dynamic_index_in_dim(halves, bit, 0, keepdims=False)
         send = lax.dynamic_index_in_dim(halves, 1 - bit, 0, keepdims=False)
-        held = keep + xor_swap(send, axis, mask)
+        held = keep + xor_swap(send.astype(wire), axis, mask).astype(value.dtype)
         bits.append(bit)
+    held = held.astype(wire)
     for (axis, mask), bit in reversed(list(zip(steps, bits))):
         held = ordered_pair(held, xor_swap(held, axis, mask), bit)
-    return held
+    return held.astype(value.dtype), tie
 
 
 def to_heads(value, blocks, heads_here, head_dim):
@@ -144,14 +147,15 @@
     ).astype(bf16)
     split = lambda value: to_heads(value, slab_blocks, heads_here, head_dim)
     q_heads = split(packed[0])
-    keys_values = split(packed[1:])
-    extended = padded(keys_values, (("slab", 2),), REACH)
     lookup = (neighbours - slab_index * slab_blocks + REACH) % n_blocks
     choose = lookup[:, :, None] == jnp.arange(ext_blocks, dtype=jnp.int32)
-    fetched = jnp.einsum(
-        "bse,chekd->chbskd", choose.astype(bf16), extended, preferred_element_type=f32
-    ).astype(bf16)
-    keys, values = fetched[0], fetched[1]
+    fetch = lambda value: jnp.einsum(
+        "bse,hekd->hbskd",
+        choose.astype(bf16),
+        padded(split(value), (("slab", 1),), REACH),
+        preferred_element_type=f32,
+    ).astype(bf16)
+    keys, values = fetch(packed[1]), fetch(packed[2])
     live = (jnp.arange(n_slots, dtype=jnp.int32)[None, :] < counts[:, None]).astype(f32)
     scores = exponent_divisor * jnp.einsum(
         "hbqd,hbskd->hbqsk", q_heads, keys, preferred_element_type=f32
@@ -199,9 +203,7 @@
     d_normed_part = jnp.einsum("crk,cdk->rd", d_qkv, w_here, preferred_element_type=f32)
     d_gain_part = jnp.sum(d_normed_part * slab_scaled, 0)
     shares = d_normed_part.astype(bf16).reshape(n_head, -1, width)
-    d_normed = jnp.sum(
-        lax.all_to_all(shares, "head", split_axis=0, concat_axis=0, tiled=True).astype(f32), 0
-    )
+    received = lax.all_to_all(shares, "head", split_axis=0, concat_axis=0, tiled=True)
     d_qkv_part = jnp.einsum("rd,crk->cdk", gathered, d_qkv, preferred_element_type=f32)
     slots = jnp.zeros((n_head,) + d_qkv_part.shape, f32)
     slots = lax.dynamic_update_index_in_dim(slots, d_qkv_part, head_index, 0)
@@ -209,7 +211,8 @@
     rows = sum(piece.shape[0] for piece in pieces)
     n_dev = n_head * n_slab
     pieces.append(jnp.zeros((-rows % n_dev, width), f32))
-    total = butterfly_psum(jnp.concatenate(pieces, 0))
+    total, received = butterfly_psum(jnp.concatenate(pieces, 0), bf16, received, 2)
+    d_normed = jnp.sum(received.astype(f32), 0)
     slot_rows = pieces[0].shape[0]
     all_slots = total[:slot_rows].reshape(slots.shape)
     d_w_qkv = lax.dynamic_index_in_dim(all_slots, head_index, 0, keepdims=False)

time: 406 us -> 360 us (0.89)
  the two profiles are of different devices: /device:TPU:0 before, /device:TPU:1 now
where the time goes in v5:
time: 360 us; the launch traced here: 354 us
  matrix products  113 us (31%)
  waiting for transfers between devices  90.5 us (25%)
  starting transfers between devices  65.4 us (18%)
  other arithmetic  45.4 us (13%)
  local copies, waits for them, and re-layouts  37.5 us (10%)
    ppermute x16, waiting for transfers between devices, xor_swap(): return lax.ppermute(value, axis, [(i, i ^ mask) for i in range(size)])  60.7 us
    ppermute x16, starting transfers between devices, xor_swap(): return lax.ppermute(value, axis, [(i, i ^ mask) for i in range(size)])  26.3 us
    convert_element_type x1, other arithmetic, local(): d_scores = (exponent_divisor * weights * (d_weights - row_dot)).astype(bf16)  22.4 us
    dot_general x1, matrix products, local(): jnp.einsum('hbqd,hbskd->hbqsk', d_attn, values, preferred_element_type=f32)  19.7 us
    dot_general x2, matrix products, local(): jnp.einsum('bse,hbskd->hekd', choose.astype(f32), grads, precision=lax.Pr...  17.2 us
    all_to_all x1, waiting for transfers between devices, local(): lax.all_to_all(d_attended, 'head', split_axis=1, concat_axis=0, tiled=True)  16.5 us
    dot_general x1, matrix products, local(): jnp.einsum('hbqsk,hbskd->hbqd', weights_bf, values, preferred_element_typ...  13.4 us
    dot_general x1, matrix products, local(): jnp.einsum('hbqd,hbskd->hbqsk', q_heads, keys, preferred_element_type=f32)  13.4 us
  transfers between devices with their start and end apart: 25, of which 18 were waited for; matrix products, arithmetic and copies ran while one was open for 16% of the time, Pallas kernels for 0%

profile of v5, /device:TPU:1, one launch (start us, length us, event | category | flops | bytes accessed | tf_op | source)
XLA Modules:
  0.0 354.0 jit_solution(13889435807742717839)
XLA Ops:
  8.5 4.1 %all-to-all-start.1 = ((bf16[512,4,96]{0,2,1:T(8,128)(2,1)}), bf16[512,4,96]{0,2,1:T(8,128)(2,1)S(1)}, u32[]{:S(2)}, u32[]{:S(2)}) async-start(bf16[512,4,96]{0,2,1:T(8,128)(2,1)} %bitcast.33), calls=%async_computation.1 | async-start | bytes 786432 | tf_op jit(solution)/shard_map/all_to_all | solution.py:175
  12.8 16.5 %all-to-all-done.1 = bf16[512,4,96]{0,2,1:T(8,128)(2,1)S(1)} async-done(((bf16[512,4,96]{0,2,1:T(8,128)(2,1)}), bf16[512,4,96]{0,2,1:T(8,128)(2,1)S(1)}, u32[]{:S(2)}, u32[]{:S(2)}) %all-to-all-start.1) | async-done | bytes 393248 | tf_op jit(solution)/shard_map/all_to_all | solution.py:175
  36.6 6.0 %collective-permute-start.3 = (bf16[3,16,128,32]{2,1,3,0:T(8,128)(2,1)S(1)}, bf16[3,16,128,32]{2,1,3,0:T(8,128)(2,1)S(1)}, u32[]{:S(2)}, u32[]{:S(2)}) collective-permute-start(bf16[3,16,128,32]{2,1,3,0:T(8,128)(2,1)S(1)} %bitcast.319), channel_id=1, source_target_pairs={{4,0},{8,4},{12,8},{16,12},{20,16},{24,20},{28,24},{32,28},{36,32}... | collective-permute-start | bytes 1179656 | tf_op jit(solution)/shard_map/ppermute | solution.py:25
  42.8 7.4 %collective-permute-start.5 = (bf16[3,16,128,32]{2,1,3,0:T(8,128)(2,1)S(1)}, bf16[3,16,128,32]{2,1,3,0:T(8,128)(2,1)S(1)}, u32[]{:S(2)}, u32[]{:S(2)}) collective-permute-start(bf16[3,16,128,32]{2,1,3,0:T(8,128)(2,1)S(1)} %bitcast.316), channel_id=1, source_target_pairs={{4,0},{8,4},{12,8},{16,12},{20,16},{24,20},{28,24},{32,28},{36,32}... | collective-permute-start | bytes 1179656 | tf_op jit(solution)/shard_map/ppermute | solution.py:25
  55.3 13.4 %fusion.3 = (f32[3,16,128]{2,1,0:T(8,128)S(1)}, f32[3,16,128,8,128]{2,4,3,1,0:T(8,128)}) fusion(f32[16,8]{1,0:T(8,128)S(1)} %fusion.152, bf16[3,16,8,128,32]{3,1,2,4,0:T(8,128)(2,1)S(1)} %convert_bitcast_fusion.1, bf16[16,128,3,32]{1,0,3,2:T(8,128)(2,1)S(1)} %bitcast.302), kind=kOutput, calls=%fused_computation.6 | convolution fusion | flops 421521408 | bytes 28729856 | tf_op jit(solution)/shard_map/hbqd,hbskd->hbqsk/dot_general | solution.py:160
  68.7 12.5 %fusion.8 = f32[3,16,8,128,32]{3,4,2,1,0:T(8,128)} fusion(bf16[16,128,3,32]{1,0,3,2:T(8,128)(2,1)S(1)} %copy-done.19, f32[3,16,128,8,128]{2,4,3,1,0:T(8,128)} %get-tuple-element.92, f32[3,16,128]{2,1,0:T(8,128)S(1)} %get-tuple-element.91, f32[16,8]{1,0:T(8,128)S(1)} %fusion.152), kind=kOutput, calls=%fused_computation.11 | convolution fusion | flops 427819008 | bytes 31875584 | tf_op jit(solution)/shard_map/hbqsk,hbqd->hbskd/dot_general | solution.py:181
  83.9 19.7 %multiply_reduce_fusion = (f32[3,16,128]{2,1,0:T(8,128)S(1)}, f32[3,16,128,8,128]{2,4,3,1,0:T(8,128)}) fusion(f32[3,16,128]{2,1,0:T(8,128)S(1)} %get-tuple-element.91, f32[16,8]{1,0:T(8,128)S(1)} %fusion.152, f32[3,16,128,8,128]{2,4,3,1,0:T(8,128)} %get-tuple-element.92, bf16[3,16,8,128,32]{3,1,2,4,0:T(8,128)(2,1)} %convert_bitcast_fusion, ...), kind=kOutput, calls=%fused_computation.3 | convolution fusion | flops 434104320 | bytes 53920256 | tf_op jit(solution)/shard_map/hbqd,hbskd->hbqsk/dot_general | solution.py:176
  103.6 13.4 %fusion.56 = bf16[16,128,3,32]{1,3,0,2:T(8,128)(2,1)} fusion(bf16[3,16,8,128,32]{3,1,2,4,0:T(8,128)(2,1)} %convert_bitcast_fusion, f32[3,16,128,8,128]{2,4,3,1,0:T(8,128)} %get-tuple-element.92, f32[3,16,128]{2,1,0:T(8,128)S(1)} %get-tuple-element.91, f32[16,8]{1,0:T(8,128)S(1)} %fusion.152), kind=kOutput, calls=%fused_computation.69 | convolution fusion | flops 428015616 | bytes 28729856 | tf_op jit(solution)/shard_map/hbqsk,hbskd->hbqd/dot_general | solution.py:166
  117.0 22.4 %multiply_convert_fusion = bf16[3,16,128,8,128]{2,4,3,1,0:T(8,128)(2,1)} fusion(f32[3,16,128,8,128]{2,4,3,1,0:T(8,128)} %get-tuple-element.94, f32[3,16,128]{2,1,0:T(8,128)S(1)} %get-tuple-element.93, f32[3,16,128]{2,1,0:T(8,128)S(1)} %get-tuple-element.91, f32[16,8]{1,0:T(8,128)S(1)} %fusion.152, f32[3,16,128,8,128]{2,4,3,1,0:T(8,128)} %get-tuple-element.92), kind=kLoop, calls=%fused_computation.2 | loop fusion | flops 44040192 | bytes 62964224 | tf_op jit(solution)/shard_map/convert_element_type | solution.py:178
  139.4 11.7 %fusion.101 = f32[3,16,8,128,32]{3,4,2,1,0:T(8,128)} fusion(bf16[3,16,128,8,128]{2,4,3,1,0:T(8,128)(2,1)} %multiply_convert_fusion, bf16[16,128,3,32]{1,0,3,2:T(8,128)(2,1)S(1)} %bitcast.303), kind=kOutput, calls=%fused_computation.135 | convolution fusion | flops 402653184 | bytes 19267584 | tf_op jit(solution)/shard_map/hbqsk,hbqd->hbskd/dot_general | solution.py:180
  151.1 8.6 %fusion.25 = f32[1,3,48,128,32]{3,2,4,1,0:T(8,128)S(1)} fusion(f32[3,16,8,128,32]{3,4,2,1,0:T(8,128)} %fusion.101, s32[16,8]{0,1:T(8,128)S(1)} %add_select_fusion), kind=kOutput, calls=%fused_computation.42 | convolution fusion | flops 905975808 | bytes 8651264 | tf_op jit(solution)/shard_map/bse,hbskd->hekd/dot_general | solution.py:182
  159.7 8.6 %fusion.28 = f32[1,3,48,128,32]{3,2,4,1,0:T(8,128)S(1)} fusion(f32[3,16,8,128,32]{3,4,2,1,0:T(8,128)} %fusion.8, s32[16,8]{0,1:T(8,128)S(1)} %add_select_fusion), kind=kOutput, calls=%fused_computation.43 | convolution fusion | flops 905975808 | bytes 8651264 | tf_op jit(solution)/shard_map/bse,hbskd->hekd/dot_general | solution.py:182
  171.3 5.9 %collective-permute-start.6 = (bf16[2,3,16,128,32]{3,2,4,1,0:T(8,128)(2,1)}, bf16[2,3,16,128,32]{3,2,4,1,0:T(8,128)(2,1)}, u32[]{:S(2)}, u32[]{:S(2)}) collective-permute-start(bf16[2,3,16,128,32]{3,2,4,1,0:T(8,128)(2,1)} %get-tuple-element.53), channel_id=1, source_target_pairs={{0,124},{4,0},{8,4},{12,8},{16,12},{20,16},{24,20},{28,24},{32,28}... | collective-permute-start | bytes 2359304 | tf_op jit(solution)/shard_map/ppermute | solution.py:33
  181.8 8.4 %all-to-all-start = ((bf16[4,512,96]{1,2,0:T(8,128)(2,1)}), bf16[4,512,96]{1,2,0:T(8,128)(2,1)}, u32[]{:S(2)}, u32[]{:S(2)}) async-start(bf16[4,512,96]{1,2,0:T(8,128)(2,1)} %copy.63), calls=%async_computation | async-start | bytes 786432 | tf_op jit(solution)/shard_map/all_to_all | solution.py:169
  190.2 9.5 %fusion.53 = f32[3,16,128,32]{2,3,1,0:T(8,128)S(1)} fusion(bf16[3,16,128,8,128]{2,4,3,1,0:T(8,128)(2,1)} %multiply_convert_fusion, bf16[3,16,8,128,32]{3,1,2,4,0:T(8,128)(2,1)} %copy-done.1), kind=kOutput, calls=%fused_computation.67 | convolution fusion | flops 403046400 | bytes 16515072 | tf_op jit(solution)/shard_map/hbqsk,hbskd->hbqd/dot_general | solution.py:179
  206.5 9.5 %all-to-all-done = bf16[4,512,96]{1,2,0:T(8,128)(2,1)} async-done(((bf16[4,512,96]{1,2,0:T(8,128)(2,1)}), bf16[4,512,96]{1,2,0:T(8,128)(2,1)}, u32[]{:S(2)}, u32[]{:S(2)}) %all-to-all-start) | async-done | bytes 393248 | tf_op jit(solution)/shard_map/all_to_all | solution.py:169
  232.1 4.2 %fusion.16 = (f32[384]{0:T(512)S(1)}, bf16[2048,384,1]{1,0,2:T(8,128)(2,1)}) fusion(f32[2048]{0:T(1024)S(1)} %copy-done.23, bf16[1024,384]{1,0:T(8,128)(2,1)S(1)} %copy-done.14, bf16[1024,384]{1,0:T(8,128)(2,1)S(1)} %copy-done.12, bf16[3,384,384]{2,1,0:T(8,128)(2,1)S(1)} %copy-done, s32[]{:T(128)S(6)} %select_n.157, ...), kind=kOutput, calls=%fused_computation.24 | convolution fusion | flops 460455552 | bytes 4630020 | tf_op jit(solution)/shard_map/crk,cdk->rd/dot_general | solution.py:203
  242.2 7.0 %concatenate.46 = f32[1664,384]{1,0:T(8,128)S(1)} concatenate(f32[1152,384]{1,0:T(8,128)} %reshape.268, f32[384,384]{1,0:T(8,128)} %fusion.168, f32[1,384]{1,0:T(1,128)S(1)} %broadcast_in_dim.60, f32[127,384]{1,0:T(8,128)} %broadcast_in_dim.61), dimensions={0} | concatenate | bytes 5111808 | tf_op jit(solution)/shard_map/concatenate | solution.py:214
  251.5 4.3 %all-to-all-start.2 = ((bf16[4,512,384]{2,1,0:T(8,128)(2,1)}), bf16[4,512,384]{2,1,0:T(8,128)(2,1)}, u32[]{:S(2)}, u32[]{:S(2)}) async-start(bf16[4,512,384]{2,1,0:T(8,128)(2,1)} %bitcast.313), calls=%async_computation.2 | async-start | bytes 3145728 | tf_op jit(solution)/shard_map/all_to_all | solution.py:206
  259.5 22.2 %collective-permute-done.9 = bf16[416,384]{1,0:T(8,128)(2,1)S(1)} collective-permute-done((bf16[416,384]{1,0:T(8,128)(2,1)S(1)}, bf16[416,384]{1,0:T(8,128)(2,1)S(1)}, u32[]{:S(2)}, u32[]{:S(2)}) %collective-permute-start.9) | collective-permute-done | bytes 319520 | tf_op jit(solution)/shard_map/ppermute | solution.py:70
  283.1 6.1 %collective-permute-done.10 = bf16[208,384]{1,0:T(8,128)(2,1)S(1)} collective-permute-done((bf16[208,384]{1,0:T(8,128)(2,1)S(1)}, bf16[208,384]{1,0:T(8,128)(2,1)S(1)}, u32[]{:S(2)}, u32[]{:S(2)}) %collective-permute-start.10) | collective-permute-done | bytes 159776 | tf_op jit(solution)/shard_map/ppermute | solution.py:70
  293.1 4.3 %collective-permute-done.12 = bf16[52,384]{1,0:T(8,128)(2,1)S(1)} collective-permute-done((bf16[52,384]{1,0:T(8,128)(2,1)S(1)}, bf16[52,384]{1,0:T(8,128)(2,1)S(1)}, u32[]{:S(2)}, u32[]{:S(2)}) %collective-permute-start.12) | collective-permute-done | bytes 39968 | tf_op jit(solution)/shard_map/ppermute | solution.py:70
  311.8 4.3 %collective-permute-done.17 = bf16[52,384]{1,0:T(8,128)(2,1)S(1)} collective-permute-done((bf16[52,384]{1,0:T(8,128)(2,1)S(1)}, bf16[52,384]{1,0:T(8,128)(2,1)S(1)}, u32[]{:S(2)}, u32[]{:S(2)}) %collective-permute-start.17) | collective-permute-done | bytes 39968 | tf_op jit(solution)/shard_map/ppermute | solution.py:70
  332.3 13.2 %collective-permute-start.21 = (bf16[832,384]{1,0:T(8,128)(2,1)S(1)}, bf16[832,384]{1,0:T(8,128)(2,1)S(1)}, u32[]{:S(2)}, u32[]{:S(2)}) collective-permute-start(bf16[832,384]{1,0:T(8,128)(2,1)S(1)} %get-tuple-element.69), channel_id=1, source_target_pairs={{0,1},{1,0},{2,3},{3,2},{4,5},{5,4},{6,7},{7,6},{8,9},{9,8},{10,11... | collective-permute-start | bytes 1916936 | tf_op jit(solution)/shard_map/ppermute | solution.py:70
  (184 shorter events, 108.7 us)
Async XLA Ops:
  0.7 3.0 collective-permute-start
  6.1 24.4 %collective-permute-start.1 = (bf16[1024,384]{1,0:T(8,128)(2,1)}, bf16[1024,384]{1,0:T(8,128)(2,1)S(1)}, u32[]{:S(2)}, u32[]{:S(2)}) collective-permute-start(bf16[1024,384]{1,0:T(8,128)(2,1)} %get-tuple-element.65), channel_id=1, source_target_pairs={{0,2},{1,3},{2,0},{3,1},{4,6},{5,7},{6,4},{7,5},{8,10},{9,11},{10,... | collective-permute-start | bytes 2359304 | tf_op jit(solution)/shard_map/ppermute | solution.py:70
  8.5 20.7 %all-to-all-start.1 = ((bf16[512,4,96]{0,2,1:T(8,128)(2,1)}), bf16[512,4,96]{0,2,1:T(8,128)(2,1)S(1)}, u32[]{:S(2)}, u32[]{:S(2)}) async-start(bf16[512,4,96]{0,2,1:T(8,128)(2,1)} %bitcast.33), calls=%async_computation.1 | async-start | bytes 786432 | tf_op jit(solution)/shard_map/all_to_all | solution.py:175
  33.6 17.1 %collective-permute-start.2 = (bf16[3,16,128,32]{2,1,3,0:T(8,128)(2,1)S(1)}, bf16[3,16,128,32]{2,1,3,0:T(8,128)(2,1)S(1)}, u32[]{:S(2)}, u32[]{:S(2)}) collective-permute-start(bf16[3,16,128,32]{2,1,3,0:T(8,128)(2,1)S(1)} %bitcast.318), channel_id=1, source_target_pairs={{0,4},{4,8},{8,12},{12,16},{16,20},{20,24},{24,28},{28,32},{32,36}... | collective-permute-start | bytes 1179656 | tf_op jit(solution)/shard_map/ppermute | solution.py:24
  36.6 17.7 %collective-permute-start.3 = (bf16[3,16,128,32]{2,1,3,0:T(8,128)(2,1)S(1)}, bf16[3,16,128,32]{2,1,3,0:T(8,128)(2,1)S(1)}, u32[]{:S(2)}, u32[]{:S(2)}) collective-permute-start(bf16[3,16,128,32]{2,1,3,0:T(8,128)(2,1)S(1)} %bitcast.319), channel_id=1, source_target_pairs={{4,0},{8,4},{12,8},{16,12},{20,16},{24,20},{28,24},{32,28},{36,32}... | collective-permute-start | bytes 1179656 | tf_op jit(solution)/shard_map/ppermute | solution.py:25
  42.7 38.4 %collective-permute-start.4 = (bf16[3,16,128,32]{2,1,3,0:T(8,128)(2,1)S(1)}, bf16[3,16,128,32]{2,1,3,0:T(8,128)(2,1)S(1)}, u32[]{:S(2)}, u32[]{:S(2)}) collective-permute-start(bf16[3,16,128,32]{2,1,3,0:T(8,128)(2,1)S(1)} %bitcast.315), channel_id=1, source_target_pairs={{0,4},{4,8},{8,12},{12,16},{16,20},{20,24},{24,28},{28,32},{32,36}... | collective-permute-start | bytes 1179656 | tf_op jit(solution)/shard_map/ppermute | solution.py:24
  42.8 38.4 %collective-permute-start.5 = (bf16[3,16,128,32]{2,1,3,0:T(8,128)(2,1)S(1)}, bf16[3,16,128,32]{2,1,3,0:T(8,128)(2,1)S(1)}, u32[]{:S(2)}, u32[]{:S(2)}) collective-permute-start(bf16[3,16,128,32]{2,1,3,0:T(8,128)(2,1)S(1)} %bitcast.316), channel_id=1, source_target_pairs={{4,0},{8,4},{12,8},{16,12},{20,16},{24,20},{28,24},{32,28},{36,32}... | collective-permute-start | bytes 1179656 | tf_op jit(solution)/shard_map/ppermute | solution.py:25
  171.3 47.0 %collective-permute-start.6 = (bf16[2,3,16,128,32]{3,2,4,1,0:T(8,128)(2,1)}, bf16[2,3,16,128,32]{3,2,4,1,0:T(8,128)(2,1)}, u32[]{:S(2)}, u32[]{:S(2)}) collective-permute-start(bf16[2,3,16,128,32]{3,2,4,1,0:T(8,128)(2,1)} %get-tuple-element.53), channel_id=1, source_target_pairs={{0,124},{4,0},{8,4},{12,8},{16,12},{20,16},{24,20},{28,24},{32,28}... | collective-permute-start | bytes 2359304 | tf_op jit(solution)/shard_map/ppermute | solution.py:33
  177.2 41.0 %collective-permute-start.7 = (bf16[2,3,16,128,32]{3,2,4,1,0:T(8,128)(2,1)}, bf16[2,3,16,128,32]{3,2,4,1,0:T(8,128)(2,1)}, u32[]{:S(2)}, u32[]{:S(2)}) collective-permute-start(bf16[2,3,16,128,32]{3,2,4,1,0:T(8,128)(2,1)} %get-tuple-element.54), channel_id=1, source_target_pairs={{0,4},{4,8},{8,12},{12,16},{16,20},{20,24},{24,28},{28,32},{32,36}... | collective-permute-start | bytes 2359304 | tf_op jit(solution)/shard_map/ppermute | solution.py:33
  181.8 34.2 %all-to-all-start = ((bf16[4,512,96]{1,2,0:T(8,128)(2,1)}), bf16[4,512,96]{1,2,0:T(8,128)(2,1)}, u32[]{:S(2)}, u32[]{:S(2)}) async-start(bf16[4,512,96]{1,2,0:T(8,128)(2,1)} %copy.63), calls=%async_computation | async-start | bytes 786432 | tf_op jit(solution)/shard_map/all_to_all | solution.py:169
  250.1 5.8 %collective-permute-start.8 = (bf16[832,384]{1,0:T(8,128)(2,1)}, bf16[832,384]{1,0:T(8,128)(2,1)}, u32[]{:S(2)}, u32[]{:S(2)}) collective-permute-start(bf16[832,384]{1,0:T(8,128)(2,1)} %fusion.88), channel_id=1, source_target_pairs={{0,1},{1,0},{2,3},{3,2},{4,5},{5,4},{6,7},{7,6},{8,9},{9,8},{10,11... | collective-permute-start | bytes 1916936 | tf_op jit(solution)/shard_map/ppermute | solution.py:70
  251.5 31.4 %all-to-all-start.2 = ((bf16[4,512,384]{2,1,0:T(8,128)(2,1)}), bf16[4,512,384]{2,1,0:T(8,128)(2,1)}, u32[]{:S(2)}, u32[]{:S(2)}) async-start(bf16[4,512,384]{2,1,0:T(8,128)(2,1)} %bitcast.313), calls=%async_computation.2 | async-start | bytes 3145728 | tf_op jit(solution)/shard_map/all_to_all | solution.py:206
  258.2 23.6 %collective-permute-start.9 = (bf16[416,384]{1,0:T(8,128)(2,1)S(1)}, bf16[416,384]{1,0:T(8,128)(2,1)S(1)}, u32[]{:S(2)}, u32[]{:S(2)}) collective-permute-start(bf16[416,384]{1,0:T(8,128)(2,1)S(1)} %fusion.108), channel_id=1, source_target_pairs={{0,2},{1,3},{2,0},{3,1},{4,6},{5,7},{6,4},{7,5},{8,10},{9,11},{10,... | collective-permute-start | bytes 958472 | tf_op jit(solution)/shard_map/ppermute | solution.py:70
  282.9 6.3 %collective-permute-start.10 = (bf16[208,384]{1,0:T(8,128)(2,1)S(1)}, bf16[208,384]{1,0:T(8,128)(2,1)S(1)}, u32[]{:S(2)}, u32[]{:S(2)}) collective-permute-start(bf16[208,384]{1,0:T(8,128)(2,1)S(1)} %fusion.115), channel_id=1, source_target_pairs={{0,4},{4,0},{8,12},{12,8},{16,20},{20,16},{24,28},{28,24},{32,36},... | collective-permute-start | bytes 479240 | tf_op jit(solution)/shard_map/ppermute | solution.py:70
  289.3 3.3 collective-permute-start.11
  292.7 4.7 %collective-permute-start.12 = (bf16[52,384]{1,0:T(8,128)(2,1)S(1)}, bf16[52,384]{1,0:T(8,128)(2,1)S(1)}, u32[]{:S(2)}, u32[]{:S(2)}) collective-permute-start(bf16[52,384]{1,0:T(8,128)(2,1)S(1)} %fusion.130), channel_id=1, source_target_pairs={{0,16},{4,20},{8,24},{12,28},{16,0},{20,4},{24,8},{28,12},{32,48},... | collective-permute-start | bytes 119816 | tf_op jit(solution)/shard_map/ppermute | solution.py:70
  297.5 3.1 collective-permute-start.13
  300.6 4.1 %collective-permute-start.14 = (bf16[13,384]{1,0:T(8,128)(2,1)S(1)}, bf16[13,384]{1,0:T(8,128)(2,1)S(1)}, u32[]{:S(2)}, u32[]{:S(2)}) collective-permute-start(bf16[13,384]{1,0:T(8,128)(2,1)S(1)} %fusion.147), channel_id=1, source_target_pairs={{0,64},{4,68},{8,72},{12,76},{16,80},{20,84},{24,88},{28,92},{32,9... | collective-permute-start | bytes 29960 | tf_op jit(solution)/shard_map/ppermute | solution.py:70
  304.7 4.1 %collective-permute-start.15 = (bf16[13,384]{1,0:T(8,128)(2,1)S(1)}, bf16[13,384]{1,0:T(8,128)(2,1)S(1)}, u32[]{:S(2)}, u32[]{:S(2)}) collective-permute-start(bf16[13,384]{1,0:T(8,128)(2,1)S(1)} %fusion.144), channel_id=1, source_target_pairs={{0,64},{4,68},{8,72},{12,76},{16,80},{20,84},{24,88},{28,92},{32,9... | collective-permute-start | bytes 29960 | tf_op jit(solution)/shard_map/ppermute | solution.py:70
  311.7 4.5 %collective-permute-start.17 = (bf16[52,384]{1,0:T(8,128)(2,1)S(1)}, bf16[52,384]{1,0:T(8,128)(2,1)S(1)}, u32[]{:S(2)}, u32[]{:S(2)}) collective-permute-start(bf16[52,384]{1,0:T(8,128)(2,1)S(1)} %pad_maximum_fusion.10), channel_id=1, source_target_pairs={{0,16},{4,20},{8,24},{12,28},{16,0},{20,4},{24,8},{28,12},{32,48},... | collective-permute-start | bytes 119816 | tf_op jit(solution)/shard_map/ppermute | solution.py:70
  316.2 3.6 %collective-permute-start.18 = (bf16[104,384]{1,0:T(8,128)(2,1)S(1)}, bf16[104,384]{1,0:T(8,128)(2,1)S(1)}, u32[]{:S(2)}, u32[]{:S(2)}) collective-permute-start(bf16[104,384]{1,0:T(8,128)(2,1)S(1)} %pad_maximum_fusion.9), channel_id=1, source_target_pairs={{0,8},{4,12},{8,0},{12,4},{16,24},{20,28},{24,16},{28,20},{32,40},... | collective-permute-start | bytes 239624 | tf_op jit(solution)/shard_map/ppermute | solution.py:70
  320.0 5.7 %collective-permute-start.19 = (bf16[208,384]{1,0:T(8,128)(2,1)S(1)}, bf16[208,384]{1,0:T(8,128)(2,1)S(1)}, u32[]{:S(2)}, u32[]{:S(2)}) collective-permute-start(bf16[208,384]{1,0:T(8,128)(2,1)S(1)} %get-tuple-element.77), channel_id=1, source_target_pairs={{0,4},{4,0},{8,12},{12,8},{16,20},{20,16},{24,28},{28,24},{32,36},... | collective-permute-start | bytes 479240 | tf_op jit(solution)/shard_map/ppermute | solution.py:70
  326.0 5.9 %collective-permute-start.20 = (bf16[416,384]{1,0:T(8,128)(2,1)S(1)}, bf16[416,384]{1,0:T(8,128)(2,1)S(1)}, u32[]{:S(2)}, u32[]{:S(2)}) collective-permute-start(bf16[416,384]{1,0:T(8,128)(2,1)S(1)} %get-tuple-element.73), channel_id=1, source_target_pairs={{0,2},{1,3},{2,0},{3,1},{4,6},{5,7},{6,4},{7,5},{8,10},{9,11},{10,... | collective-permute-start | bytes 958472 | tf_op jit(solution)/shard_map/ppermute | solution.py:70
  332.3 14.9 %collective-permute-start.21 = (bf16[832,384]{1,0:T(8,128)(2,1)S(1)}, bf16[832,384]{1,0:T(8,128)(2,1)S(1)}, u32[]{:S(2)}, u32[]{:S(2)}) collective-permute-start(bf16[832,384]{1,0:T(8,128)(2,1)S(1)} %get-tuple-element.69), channel_id=1, source_target_pairs={{0,1},{1,0},{2,3},{3,2},{4,5},{5,4},{6,7},{7,6},{8,9},{9,8},{10,11... | collective-permute-start | bytes 1916936 | tf_op jit(solution)/shard_map/ppermute | solution.py:70
  (29 other events, 309.5 us)

commit v6 on v5

--- a/solution.py
+++ b/solution.py
@@ -88,13 +88,15 @@
     return held
 
 
-def butterfly_psum(value, wire, tie, tie_step):
+def butterfly_psum(value, wire, side_input, side_fn, start_step, join_step):
     steps = xor_steps()
     held = value
     bits = []
+    side = None
     for index, (axis, mask) in enumerate(steps):
-        if index == tie_step:
-            held, tie = lax.optimization_barrier((held, tie))
+        if index == start_step:
+            held, side_input = lax.optimization_barrier((held, side_input))
+            side = side_fn(side_input)
         bit = (lax.axis_index(axis) // mask) % 2
         halves = held.reshape((2, held.shape[0] // 2) + held.shape[1:])
         keep = lax.dynamic_index_in_dim(halves, bit, 0, keepdims=False)
@@ -102,9 +104,11 @@
         held = keep + xor_swap(send.astype(wire), axis, mask).astype(value.dtype)
         bits.append(bit)
     held = held.astype(wire)
-    for (axis, mask), bit in reversed(list(zip(steps, bits))):
+    for index, ((axis, mask), bit) in enumerate(reversed(list(zip(steps, bits)))):
+        if index == join_step:
+            held, side = lax.optimization_barrier((held, side))
         held = ordered_pair(held, xor_swap(held, axis, mask), bit)
-    return held.astype(value.dtype), tie
+    return held.astype(value.dtype), side
 
 
 def to_heads(value, blocks, heads_here, head_dim):
@@ -172,10 +176,12 @@
     output = (tok_f32 + jnp.dot(attended, w_out, preferred_element_type=f32)).astype(bf16)
     d_out_part = jnp.dot(attended.T, cotangent, preferred_element_type=f32)
     d_attended = jnp.dot(cotangent, w_out.T, preferred_element_type=f32).astype(bf16)
+    d_attended, keys = lax.optimization_barrier((d_attended, keys))
     d_attn = split(lax.all_to_all(d_attended, "head", split_axis=1, concat_axis=0, tiled=True))
     d_weights = jnp.einsum("hbqd,hbskd->hbqsk", d_attn, values, preferred_element_type=f32)
     row_dot = jnp.sum(d_weights * weights, (-2, -1), keepdims=True)
     d_scores = (exponent_divisor * weights * (d_weights - row_dot)).astype(bf16)
+    attended, d_scores = lax.optimization_barrier((attended, d_scores))
     d_query = jnp.einsum("hbqsk,hbskd->hbqd", d_scores, keys, preferred_element_type=f32)
     d_keys = jnp.einsum("hbqsk,hbqd->hbskd", d_scores, q_heads, preferred_element_type=f32)
     d_values = jnp.einsum("hbqsk,hbqd->hbskd", weights_bf, d_attn, preferred_element_type=f32)
@@ -203,7 +209,6 @@
     d_normed_part = jnp.einsum("crk,cdk->rd", d_qkv, w_here, preferred_element_type=f32)
     d_gain_part = jnp.sum(d_normed_part * slab_scaled, 0)
     shares = d_normed_part.astype(bf16).reshape(n_head, -1, width)
-    received = lax.all_to_all(shares, "head", split_axis=0, concat_axis=0, tiled=True)
     d_qkv_part = jnp.einsum("rd,crk->cdk", gathered, d_qkv, preferred_element_type=f32)
     slots = jnp.zeros((n_head,) + d_qkv_part.shape, f32)
     slots = lax.dynamic_update_index_in_dim(slots, d_qkv_part, head_index, 0)
@@ -211,7 +216,11 @@
     rows = sum(piece.shape[0] for piece in pieces)
     n_dev = n_head * n_slab
     pieces.append(jnp.zeros((-rows % n_dev, width), f32))
-    total, received = butterfly_psum(jnp.concatenate(pieces, 0), bf16, received, 2)
+    exchange = lambda value: lax.all_to_all(value, "head", split_axis=0, concat_axis=0, tiled=True)
+    head_steps = sum(1 for axis, _ in xor_steps() if axis == "head")
+    total, received = butterfly_psum(
+        jnp.concatenate(pieces, 0), bf16, shares, exchange, head_steps, 1
+    )
     d_normed = jnp.sum(received.astype(f32), 0)
     slot_rows = pieces[0].shape[0]
     all_slots = total[:slot_rows].reshape(slots.shape)

time: 360 us -> 357 us (level)
  matrix products: 113 us -> 107 us
  waiting for transfers between devices: 90.5 us -> 85 us
  starting transfers between devices: 65.4 us -> 69.1 us
    ppermute x2, waiting for transfers between devices: 0.01 us -> 22.8 us  [passed_along(): return lax.ppermute(value, axis, pairs)]
    all_to_all x1, waiting for transfers between devices: 16.5 us -> 0.01 us  [local(): lax.all_to_all(d_attended, 'head', split_axis=1, concat_axis=0, tiled=True)]
    all_to_all x1, waiting for transfers between devices: 9.49 us -> 0.01 us  [local(): lax.all_to_all(from_heads(attended_heads), 'head', split_axis=0, concat_a...]
    dot_general x1, matrix products: 9.46 us -> 3.92 us  [local(): jnp.einsum('hbqsk,hbskd->hbqd', d_scores, keys, preferred_element_type=f32)]
    all_to_all x1, starting transfers between devices: 8.38 us -> 3.86 us  [local(): lax.all_to_all(from_heads(attended_heads), 'head', split_axis=0, concat_a...]
  transfers between devices with their start and end apart: 25 -> 25, of which waited for: 18 -> 19; matrix products, arithmetic and copies ran while one was open for 16% -> 32% of each run, Pallas kernels for 0% -> 0%
where the time goes in v6:
time: 357 us; the launch traced here: 350 us
  matrix products  107 us (30%)
  waiting for transfers between devices  85 us (24%)
  starting transfers between devices  69.1 us (19%)
  other arithmetic  47.6 us (13%)
  local copies, waits for them, and re-layouts  39.9 us (11%)
    ppermute x16, waiting for transfers between devices, xor_swap(): return lax.ppermute(value, axis, [(i, i ^ mask) for i in range(size)])  58.2 us
    ppermute x16, starting transfers between devices, xor_swap(): return lax.ppermute(value, axis, [(i, i ^ mask) for i in range(size)])  28.2 us
    ppermute x2, waiting for transfers between devices, passed_along(): return lax.ppermute(value, axis, pairs)  22.8 us
    convert_element_type x1, other arithmetic, local(): d_scores = (exponent_divisor * weights * (d_weights - row_dot)).astype(bf16)  22.4 us
    dot_general x1, matrix products, local(): jnp.einsum('hbqd,hbskd->hbqsk', d_attn, values, preferred_element_type=f32)  19.3 us
    dot_general x2, matrix products, local(): jnp.einsum('bse,hbskd->hekd', choose.astype(f32), grads, precision=lax.Pr...  17.5 us
    dot_general x1, matrix products, local(): jnp.einsum('hbqd,hbskd->hbqsk', q_heads, keys, preferred_element_type=f32)  14.5 us
    ppermute x2, starting transfers between devices, padded(): after = lax.ppermute(first, axis, down)  13.2 us
  transfers between devices with their start and end apart: 25, of which 19 were waited for; matrix products, arithmetic and copies ran while one was open for 32% of the time, Pallas kernels for 0%

profile of v6, /device:TPU:1, one launch (start us, length us, event | category | flops | bytes accessed | tf_op | source)
XLA Modules:
  0.0 350.4 jit_solution(17458717410352352855)
XLA Ops:
  7.9 17.1 %collective-permute-done.1 = bf16[1024,384]{1,0:T(8,128)(2,1)S(1)} collective-permute-done((bf16[1024,384]{1,0:T(8,128)(2,1)}, bf16[1024,384]{1,0:T(8,128)(2,1)S(1)}, u32[]{:S(2)}, u32[]{:S(2)}) %collective-permute-start.1) | collective-permute-done | bytes 786464 | tf_op jit(solution)/shard_map/ppermute | solution.py:70
  31.1 6.0 %collective-permute-start.3 = (bf16[3,16,128,32]{2,1,3,0:T(8,128)(2,1)S(1)}, bf16[3,16,128,32]{2,1,3,0:T(8,128)(2,1)S(1)}, u32[]{:S(2)}, u32[]{:S(2)}) collective-permute-start(bf16[3,16,128,32]{2,1,3,0:T(8,128)(2,1)S(1)} %bitcast.322), channel_id=1, source_target_pairs={{4,0},{8,4},{12,8},{16,12},{20,16},{24,20},{28,24},{32,28},{36,32}... | collective-permute-start | bytes 1179656 | tf_op jit(solution)/shard_map/ppermute | solution.py:25
  37.4 7.2 %collective-permute-start.5 = (bf16[3,16,128,32]{2,1,3,0:T(8,128)(2,1)S(1)}, bf16[3,16,128,32]{2,1,3,0:T(8,128)(2,1)S(1)}, u32[]{:S(2)}, u32[]{:S(2)}) collective-permute-start(bf16[3,16,128,32]{2,1,3,0:T(8,128)(2,1)S(1)} %bitcast.318), channel_id=1, source_target_pairs={{4,0},{8,4},{12,8},{16,12},{20,16},{24,20},{28,24},{32,28},{36,32}... | collective-permute-start | bytes 1179656 | tf_op jit(solution)/shard_map/ppermute | solution.py:25
  52.5 7.4 %all-to-all-start.1 = ((bf16[512,4,96]{0,2,1:T(8,128)(2,1)}), bf16[512,4,96]{0,2,1:T(8,128)(2,1)S(1)}, u32[]{:S(2)}, u32[]{:S(2)}) async-start(bf16[512,4,96]{0,2,1:T(8,128)(2,1)} %bitcast.34), calls=%async_computation.1 | async-start | bytes 786432 | tf_op jit(solution)/shard_map/all_to_all | solution.py:180
  59.9 14.5 %fusion.3 = (f32[3,16,128]{2,1,0:T(8,128)S(1)}, f32[3,16,128,8,128]{2,4,3,1,0:T(8,128)}) fusion(f32[16,8]{1,0:T(8,128)S(1)} %fusion.152, bf16[3,16,8,128,32]{3,1,2,4,0:T(8,128)(2,1)} %convert_bitcast_fusion.1, bf16[16,128,3,32]{1,0,3,2:T(8,128)(2,1)S(1)} %bitcast.303), kind=kOutput, calls=%fused_computation.6 | convolution fusion | flops 421521408 | bytes 28729856 | tf_op jit(solution)/shard_map/hbqd,hbskd->hbqsk/dot_general | solution.py:164
  75.5 13.0 %fusion.56 = bf16[16,128,3,32]{1,3,0,2:T(8,128)(2,1)S(1)} fusion(bf16[3,16,8,128,32]{3,1,2,4,0:T(8,128)(2,1)S(1)} %convert_bitcast_fusion, f32[3,16,128,8,128]{2,4,3,1,0:T(8,128)} %get-tuple-element.100, f32[3,16,128]{2,1,0:T(8,128)S(1)} %get-tuple-element.99, f32[16,8]{1,0:T(8,128)S(1)} %fusion.152), kind=kOutput, calls=%fused_computation.69 | convolution fusion | flops 428015616 | bytes 28729856 | tf_op jit(solution)/shard_map/hbqsk,hbskd->hbqd/dot_general | solution.py:170
  89.7 3.9 %all-to-all-start = ((bf16[4,512,96]{1,2,0:T(8,128)(2,1)}), bf16[4,512,96]{1,2,0:T(8,128)(2,1)S(1)}, u32[]{:S(2)}, u32[]{:S(2)}) async-start(bf16[4,512,96]{1,2,0:T(8,128)(2,1)} %copy.65), calls=%async_computation | async-start | bytes 786432 | tf_op jit(solution)/shard_map/all_to_all | solution.py:173
  94.0 19.3 %multiply_reduce_fusion = (f32[3,16,128]{2,1,0:T(8,128)S(1)}, f32[3,16,128,8,128]{2,4,3,1,0:T(8,128)}) fusion(f32[3,16,128]{2,1,0:T(8,128)S(1)} %get-tuple-element.99, f32[16,8]{1,0:T(8,128)S(1)} %fusion.152, f32[3,16,128,8,128]{2,4,3,1,0:T(8,128)} %get-tuple-element.100, bf16[3,16,8,128,32]{3,1,2,4,0:T(8,128)(2,1)} %copy-done.14, ...), kind=kOutput, calls=%fused_computation.3 | convolution fusion | flops 434104320 | bytes 53920256 | tf_op jit(solution)/shard_map/hbqd,hbskd->hbqsk/dot_general | solution.py:181
  113.4 12.5 %fusion.8 = f32[3,16,8,128,32]{3,4,2,1,0:T(8,128)} fusion(bf16[16,128,3,32]{1,0,3,2:T(8,128)(2,1)S(1)} %reshape.267, f32[3,16,128,8,128]{2,4,3,1,0:T(8,128)} %get-tuple-element.100, f32[3,16,128]{2,1,0:T(8,128)S(1)} %get-tuple-element.99, f32[16,8]{1,0:T(8,128)S(1)} %fusion.152), kind=kOutput, calls=%fused_computation.11 | convolution fusion | flops 427819008 | bytes 31875584 | tf_op jit(solution)/shard_map/hbqsk,hbqd->hbskd/dot_general | solution.py:187
  125.8 22.4 %multiply_convert_fusion = bf16[3,16,128,8,128]{2,4,3,1,0:T(8,128)(2,1)} fusion(f32[3,16,128,8,128]{2,4,3,1,0:T(8,128)} %get-tuple-element.102, f32[3,16,128]{2,1,0:T(8,128)S(1)} %get-tuple-element.101, f32[3,16,128]{2,1,0:T(8,128)S(1)} %get-tuple-element.99, f32[16,8]{1,0:T(8,128)S(1)} %fusion.152, f32[3,16,128,8,128]{2,4,3,1,0:T(8,128)} %get-tuple-element.100), kind=kLoop, calls=%fused_computation.2 | loop fusion | flops 44040192 | bytes 62964224 | tf_op jit(solution)/shard_map/convert_element_type | solution.py:183
  149.0 11.7 %fusion.101 = f32[3,16,8,128,32]{3,4,2,1,0:T(8,128)} fusion(bf16[3,16,128,8,128]{2,4,3,1,0:T(8,128)(2,1)} %multiply_convert_fusion, bf16[16,128,3,32]{1,0,3,2:T(8,128)(2,1)S(1)} %bitcast.304), kind=kOutput, calls=%fused_computation.135 | convolution fusion | flops 402653184 | bytes 19267584 | tf_op jit(solution)/shard_map/hbqsk,hbqd->hbskd/dot_general | solution.py:186
  160.7 8.8 %fusion.25 = f32[1,3,48,128,32]{3,2,4,1,0:T(8,128)S(1)} fusion(f32[3,16,8,128,32]{3,4,2,1,0:T(8,128)} %fusion.101, s32[16,8]{0,1:T(8,128)S(1)} %add_select_fusion), kind=kOutput, calls=%fused_computation.42 | convolution fusion | flops 905975808 | bytes 8651264 | tf_op jit(solution)/shard_map/bse,hbskd->hekd/dot_general | solution.py:188
  169.5 8.8 %fusion.28 = f32[1,3,48,128,32]{3,2,4,1,0:T(8,128)S(1)} fusion(f32[3,16,8,128,32]{3,4,2,1,0:T(8,128)} %fusion.8, s32[16,8]{0,1:T(8,128)S(1)} %add_select_fusion), kind=kOutput, calls=%fused_computation.43 | convolution fusion | flops 905975808 | bytes 8651264 | tf_op jit(solution)/shard_map/bse,hbskd->hekd/dot_general | solution.py:188
  181.2 5.9 %collective-permute-start.6 = (bf16[2,3,16,128,32]{3,2,4,1,0:T(8,128)(2,1)}, bf16[2,3,16,128,32]{3,2,4,1,0:T(8,128)(2,1)}, u32[]{:S(2)}, u32[]{:S(2)}) collective-permute-start(bf16[2,3,16,128,32]{3,2,4,1,0:T(8,128)(2,1)} %get-tuple-element.63), channel_id=1, source_target_pairs={{0,124},{4,0},{8,4},{12,8},{16,12},{20,16},{24,20},{28,24},{32,28}... | collective-permute-start | bytes 2359304 | tf_op jit(solution)/shard_map/ppermute | solution.py:33
  187.4 3.9 %fusion.53 = f32[3,16,128,32]{2,3,1,0:T(8,128)S(1)} fusion(bf16[3,16,128,8,128]{2,4,3,1,0:T(8,128)(2,1)S(1)} %bitcast.299, bf16[3,16,8,128,32]{3,1,2,4,0:T(8,128)(2,1)S(1)} %copy-done.1), kind=kOutput, calls=%fused_computation.67 | convolution fusion | flops 403046400 | bytes 16515072 | tf_op jit(solution)/shard_map/hbqsk,hbskd->hbqd/dot_general | solution.py:185
  200.6 3.7 %collective-permute-done.6 = bf16[2,3,16,128,32]{3,2,4,1,0:T(8,128)(2,1)} collective-permute-done((bf16[2,3,16,128,32]{3,2,4,1,0:T(8,128)(2,1)}, bf16[2,3,16,128,32]{3,2,4,1,0:T(8,128)(2,1)}, u32[]{:S(2)}, u32[]{:S(2)}) %collective-permute-start.6) | collective-permute-done | bytes 786464 | tf_op jit(solution)/shard_map/ppermute | solution.py:33
  204.3 19.0 %collective-permute-done.7 = bf16[2,3,16,128,32]{3,2,4,1,0:T(8,128)(2,1)} collective-permute-done((bf16[2,3,16,128,32]{3,2,4,1,0:T(8,128)(2,1)}, bf16[2,3,16,128,32]{3,2,4,1,0:T(8,128)(2,1)}, u32[]{:S(2)}, u32[]{:S(2)}) %collective-permute-start.7) | collective-permute-done | bytes 786464 | tf_op jit(solution)/shard_map/ppermute | solution.py:33
  236.9 4.2 %fusion.16 = (f32[384]{0:T(512)S(1)}, bf16[2048,384,1]{1,0,2:T(8,128)(2,1)}) fusion(f32[2048]{0:T(1024)S(1)} %copy-done.26, bf16[1024,384]{1,0:T(8,128)(2,1)S(1)} %copy-done.18, bf16[1024,384]{1,0:T(8,128)(2,1)S(1)} %copy-done.16, bf16[3,384,384]{2,1,0:T(8,128)(2,1)S(1)} %copy-done, s32[]{:T(128)S(6)} %select_n.157, ...), kind=kOutput, calls=%fused_computation.24 | convolution fusion | flops 460455552 | bytes 4630020 | tf_op jit(solution)/shard_map/crk,cdk->rd/dot_general | solution.py:209
  247.0 7.0 %concatenate.46 = f32[1664,384]{1,0:T(8,128)S(1)} concatenate(f32[1152,384]{1,0:T(8,128)} %reshape.268, f32[384,384]{1,0:T(8,128)} %fusion.167, f32[1,384]{1,0:T(1,128)S(1)} %broadcast_in_dim.60, f32[127,384]{1,0:T(8,128)} %broadcast_in_dim.61), dimensions={0} | concatenate | bytes 5111808 | tf_op jit(solution)/shard_map/concatenate | solution.py:222
  259.4 7.4 %collective-permute-done.9 = bf16[416,384]{1,0:T(8,128)(2,1)S(1)} collective-permute-done((bf16[416,384]{1,0:T(8,128)(2,1)S(1)}, bf16[416,384]{1,0:T(8,128)(2,1)S(1)}, u32[]{:S(2)}, u32[]{:S(2)}) %collective-permute-start.9) | collective-permute-done | bytes 319520 | tf_op jit(solution)/shard_map/ppermute | solution.py:70
  269.6 4.4 %collective-permute-done.10 = bf16[208,384]{1,0:T(8,128)(2,1)S(1)} collective-permute-done((bf16[208,384]{1,0:T(8,128)(2,1)S(1)}, bf16[208,384]{1,0:T(8,128)(2,1)S(1)}, u32[]{:S(2)}, u32[]{:S(2)}) %collective-permute-start.10) | collective-permute-done | bytes 159776 | tf_op jit(solution)/shard_map/ppermute | solution.py:70
  278.4 7.2 %all-to-all-start.2 = ((bf16[4,512,384]{2,1,0:T(8,128)(2,1)}), bf16[4,512,384]{2,1,0:T(8,128)(2,1)S(1)}, u32[]{:S(2)}, u32[]{:S(2)}) async-start(bf16[4,512,384]{2,1,0:T(8,128)(2,1)} %bitcast.316), calls=%async_computation.2 | async-start | bytes 3145728 | tf_op jit(solution)/shard_map/all_to_all | solution.py:219
  326.3 4.0 %collective-permute-done.20 = bf16[416,384]{1,0:T(8,128)(2,1)S(1)} collective-permute-done((bf16[416,384]{1,0:T(8,128)(2,1)S(1)}, bf16[416,384]{1,0:T(8,128)(2,1)S(1)}, u32[]{:S(2)}, u32[]{:S(2)}) %collective-permute-start.20) | collective-permute-done | bytes 319520 | tf_op jit(solution)/shard_map/ppermute | solution.py:70
  330.7 11.2 %collective-permute-start.21 = (bf16[832,384]{1,0:T(8,128)(2,1)S(1)}, bf16[832,384]{1,0:T(8,128)(2,1)S(1)}, u32[]{:S(2)}, u32[]{:S(2)}) collective-permute-start(bf16[832,384]{1,0:T(8,128)(2,1)S(1)} %get-tuple-element.79), channel_id=1, source_target_pairs={{0,1},{1,0},{2,3},{3,2},{4,5},{5,4},{6,7},{7,6},{8,9},{9,8},{10,11... | collective-permute-start | bytes 1916936 | tf_op jit(solution)/shard_map/ppermute | solution.py:70
  (198 shorter events, 117.9 us)
Async XLA Ops:
  0.7 3.0 collective-permute-start
  6.1 18.9 %collective-permute-start.1 = (bf16[1024,384]{1,0:T(8,128)(2,1)}, bf16[1024,384]{1,0:T(8,128)(2,1)S(1)}, u32[]{:S(2)}, u32[]{:S(2)}) collective-permute-start(bf16[1024,384]{1,0:T(8,128)(2,1)} %get-tuple-element.75), channel_id=1, source_target_pairs={{0,2},{1,3},{2,0},{3,1},{4,6},{5,7},{6,4},{7,5},{8,10},{9,11},{10,... | collective-permute-start | bytes 2359304 | tf_op jit(solution)/shard_map/ppermute | solution.py:70
  28.2 17.1 %collective-permute-start.2 = (bf16[3,16,128,32]{2,1,3,0:T(8,128)(2,1)S(1)}, bf16[3,16,128,32]{2,1,3,0:T(8,128)(2,1)S(1)}, u32[]{:S(2)}, u32[]{:S(2)}) collective-permute-start(bf16[3,16,128,32]{2,1,3,0:T(8,128)(2,1)S(1)} %bitcast.321), channel_id=1, source_target_pairs={{0,4},{4,8},{8,12},{12,16},{16,20},{20,24},{24,28},{28,32},{32,36}... | collective-permute-start | bytes 1179656 | tf_op jit(solution)/shard_map/ppermute | solution.py:24
  31.1 17.6 %collective-permute-start.3 = (bf16[3,16,128,32]{2,1,3,0:T(8,128)(2,1)S(1)}, bf16[3,16,128,32]{2,1,3,0:T(8,128)(2,1)S(1)}, u32[]{:S(2)}, u32[]{:S(2)}) collective-permute-start(bf16[3,16,128,32]{2,1,3,0:T(8,128)(2,1)S(1)} %bitcast.322), channel_id=1, source_target_pairs={{4,0},{8,4},{12,8},{16,12},{20,16},{24,20},{28,24},{32,28},{36,32}... | collective-permute-start | bytes 1179656 | tf_op jit(solution)/shard_map/ppermute | solution.py:25
  37.3 37.1 %collective-permute-start.4 = (bf16[3,16,128,32]{2,1,3,0:T(8,128)(2,1)S(1)}, bf16[3,16,128,32]{2,1,3,0:T(8,128)(2,1)S(1)}, u32[]{:S(2)}, u32[]{:S(2)}) collective-permute-start(bf16[3,16,128,32]{2,1,3,0:T(8,128)(2,1)S(1)} %bitcast.317), channel_id=1, source_target_pairs={{0,4},{4,8},{8,12},{12,16},{16,20},{20,24},{24,28},{28,32},{32,36}... | collective-permute-start | bytes 1179656 | tf_op jit(solution)/shard_map/ppermute | solution.py:24
  37.4 37.1 %collective-permute-start.5 = (bf16[3,16,128,32]{2,1,3,0:T(8,128)(2,1)S(1)}, bf16[3,16,128,32]{2,1,3,0:T(8,128)(2,1)S(1)}, u32[]{:S(2)}, u32[]{:S(2)}) collective-permute-start(bf16[3,16,128,32]{2,1,3,0:T(8,128)(2,1)S(1)} %bitcast.318), channel_id=1, source_target_pairs={{4,0},{8,4},{12,8},{16,12},{20,16},{24,20},{28,24},{32,28},{36,32}... | collective-permute-start | bytes 1179656 | tf_op jit(solution)/shard_map/ppermute | solution.py:25
  52.5 37.2 %all-to-all-start.1 = ((bf16[512,4,96]{0,2,1:T(8,128)(2,1)}), bf16[512,4,96]{0,2,1:T(8,128)(2,1)S(1)}, u32[]{:S(2)}, u32[]{:S(2)}) async-start(bf16[512,4,96]{0,2,1:T(8,128)(2,1)} %bitcast.34), calls=%async_computation.1 | async-start | bytes 786432 | tf_op jit(solution)/shard_map/all_to_all | solution.py:180
  89.7 58.6 %all-to-all-start = ((bf16[4,512,96]{1,2,0:T(8,128)(2,1)}), bf16[4,512,96]{1,2,0:T(8,128)(2,1)S(1)}, u32[]{:S(2)}, u32[]{:S(2)}) async-start(bf16[4,512,96]{1,2,0:T(8,128)(2,1)} %copy.65), calls=%async_computation | async-start | bytes 786432 | tf_op jit(solution)/shard_map/all_to_all | solution.py:173
  181.2 23.1 %collective-permute-start.6 = (bf16[2,3,16,128,32]{3,2,4,1,0:T(8,128)(2,1)}, bf16[2,3,16,128,32]{3,2,4,1,0:T(8,128)(2,1)}, u32[]{:S(2)}, u32[]{:S(2)}) collective-permute-start(bf16[2,3,16,128,32]{3,2,4,1,0:T(8,128)(2,1)} %get-tuple-element.63), channel_id=1, source_target_pairs={{0,124},{4,0},{8,4},{12,8},{16,12},{20,16},{24,20},{28,24},{32,28}... | collective-permute-start | bytes 2359304 | tf_op jit(solution)/shard_map/ppermute | solution.py:33
  187.1 36.2 %collective-permute-start.7 = (bf16[2,3,16,128,32]{3,2,4,1,0:T(8,128)(2,1)}, bf16[2,3,16,128,32]{3,2,4,1,0:T(8,128)(2,1)}, u32[]{:S(2)}, u32[]{:S(2)}) collective-permute-start(bf16[2,3,16,128,32]{3,2,4,1,0:T(8,128)(2,1)} %get-tuple-element.64), channel_id=1, source_target_pairs={{0,4},{4,8},{8,12},{12,16},{16,20},{20,24},{24,28},{28,32},{32,36}... | collective-permute-start | bytes 2359304 | tf_op jit(solution)/shard_map/ppermute | solution.py:33
  258.0 8.8 %collective-permute-start.9 = (bf16[416,384]{1,0:T(8,128)(2,1)S(1)}, bf16[416,384]{1,0:T(8,128)(2,1)S(1)}, u32[]{:S(2)}, u32[]{:S(2)}) collective-permute-start(bf16[416,384]{1,0:T(8,128)(2,1)S(1)} %fusion.108), channel_id=1, source_target_pairs={{0,2},{1,3},{2,0},{3,1},{4,6},{5,7},{6,4},{7,5},{8,10},{9,11},{10,... | collective-permute-start | bytes 958472 | tf_op jit(solution)/shard_map/ppermute | solution.py:70
  268.0 6.0 %collective-permute-start.10 = (bf16[208,384]{1,0:T(8,128)(2,1)S(1)}, bf16[208,384]{1,0:T(8,128)(2,1)S(1)}, u32[]{:S(2)}, u32[]{:S(2)}) collective-permute-start(bf16[208,384]{1,0:T(8,128)(2,1)S(1)} %fusion.115), channel_id=1, source_target_pairs={{0,4},{4,0},{8,12},{12,8},{16,20},{20,16},{24,28},{28,24},{32,36},... | collective-permute-start | bytes 479240 | tf_op jit(solution)/shard_map/ppermute | solution.py:70
  274.1 3.3 collective-permute-start.11
  278.1 7.4 %collective-permute-start.12 = (bf16[52,384]{1,0:T(8,128)(2,1)}, bf16[52,384]{1,0:T(8,128)(2,1)}, u32[]{:S(2)}, u32[]{:S(2)}) collective-permute-start(bf16[52,384]{1,0:T(8,128)(2,1)} %fusion.130), channel_id=1, source_target_pairs={{0,16},{4,20},{8,24},{12,28},{16,0},{20,4},{24,8},{28,12},{32,48},... | collective-permute-start | bytes 119816 | tf_op jit(solution)/shard_map/ppermute | solution.py:70
  278.4 28.1 %all-to-all-start.2 = ((bf16[4,512,384]{2,1,0:T(8,128)(2,1)}), bf16[4,512,384]{2,1,0:T(8,128)(2,1)S(1)}, u32[]{:S(2)}, u32[]{:S(2)}) async-start(bf16[4,512,384]{2,1,0:T(8,128)(2,1)} %bitcast.316), calls=%async_computation.2 | async-start | bytes 3145728 | tf_op jit(solution)/shard_map/all_to_all | solution.py:219
  290.1 3.2 collective-permute-start.13
  296.9 4.2 %collective-permute-start.14 = (bf16[13,384]{1,0:T(8,128)(2,1)S(1)}, bf16[13,384]{1,0:T(8,128)(2,1)}, u32[]{:S(2)}, u32[]{:S(2)}) collective-permute-start(bf16[13,384]{1,0:T(8,128)(2,1)S(1)} %fusion.147), channel_id=1, source_target_pairs={{0,64},{4,68},{8,72},{12,76},{16,80},{20,84},{24,88},{28,92},{32,9... | collective-permute-start | bytes 29960 | tf_op jit(solution)/shard_map/ppermute | solution.py:70
  301.8 4.0 %collective-permute-start.15 = (bf16[13,384]{1,0:T(8,128)(2,1)S(1)}, bf16[13,384]{1,0:T(8,128)(2,1)S(1)}, u32[]{:S(2)}, u32[]{:S(2)}) collective-permute-start(bf16[13,384]{1,0:T(8,128)(2,1)S(1)} %fusion.144), channel_id=1, source_target_pairs={{0,64},{4,68},{8,72},{12,76},{16,80},{20,84},{24,88},{28,92},{32,9... | collective-permute-start | bytes 29960 | tf_op jit(solution)/shard_map/ppermute | solution.py:70
  306.5 3.0 collective-permute-start.16
  310.3 4.6 %collective-permute-start.17 = (bf16[52,384]{1,0:T(8,128)(2,1)S(1)}, bf16[52,384]{1,0:T(8,128)(2,1)S(1)}, u32[]{:S(2)}, u32[]{:S(2)}) collective-permute-start(bf16[52,384]{1,0:T(8,128)(2,1)S(1)} %pad_maximum_fusion.10), channel_id=1, source_target_pairs={{0,16},{4,20},{8,24},{12,28},{16,0},{20,4},{24,8},{28,12},{32,48},... | collective-permute-start | bytes 119816 | tf_op jit(solution)/shard_map/ppermute | solution.py:70
  315.0 3.3 collective-permute-start.18
  318.4 5.7 %collective-permute-start.19 = (bf16[208,384]{1,0:T(8,128)(2,1)S(1)}, bf16[208,384]{1,0:T(8,128)(2,1)S(1)}, u32[]{:S(2)}, u32[]{:S(2)}) collective-permute-start(bf16[208,384]{1,0:T(8,128)(2,1)S(1)} %get-tuple-element.87), channel_id=1, source_target_pairs={{0,4},{4,0},{8,12},{12,8},{16,20},{20,16},{24,28},{28,24},{32,36},... | collective-permute-start | bytes 479240 | tf_op jit(solution)/shard_map/ppermute | solution.py:70
  324.4 5.9 %collective-permute-start.20 = (bf16[416,384]{1,0:T(8,128)(2,1)S(1)}, bf16[416,384]{1,0:T(8,128)(2,1)S(1)}, u32[]{:S(2)}, u32[]{:S(2)}) collective-permute-start(bf16[416,384]{1,0:T(8,128)(2,1)S(1)} %get-tuple-element.83), channel_id=1, source_target_pairs={{0,2},{1,3},{2,0},{3,1},{4,6},{5,7},{6,4},{7,5},{8,10},{9,11},{10,... | collective-permute-start | bytes 958472 | tf_op jit(solution)/shard_map/ppermute | solution.py:70
  330.7 12.9 %collective-permute-start.21 = (bf16[832,384]{1,0:T(8,128)(2,1)S(1)}, bf16[832,384]{1,0:T(8,128)(2,1)S(1)}, u32[]{:S(2)}, u32[]{:S(2)}) collective-permute-start(bf16[832,384]{1,0:T(8,128)(2,1)S(1)} %get-tuple-element.79), channel_id=1, source_target_pairs={{0,1},{1,0},{2,3},{3,2},{4,5},{5,4},{6,7},{7,6},{8,9},{9,8},{10,11... | collective-permute-start | bytes 1916936 | tf_op jit(solution)/shard_map/ppermute | solution.py:70
  (35 other events, 385.4 us)

commit v7 on v5

--- a/solution.py
+++ b/solution.py
@@ -53,9 +53,9 @@
     return result.reshape(projected.shape)
 
 
-def xor_steps():
+def xor_steps(axes):
     steps = []
-    for axis in ("head", "slab"):
+    for axis in axes:
         size = lax.axis_size(axis)
         assert size & (size - 1) == 0
         mask = 1
@@ -88,23 +88,28 @@
     return held
 
 
-def butterfly_psum(value, wire, tie, tie_step):
-    steps = xor_steps()
-    held = value
+def scatter_steps(held, steps, wire):
     bits = []
-    for index, (axis, mask) in enumerate(steps):
-        if index == tie_step:
-            held, tie = lax.optimization_barrier((held, tie))
+    for axis, mask in steps:
         bit = (lax.axis_index(axis) // mask) % 2
         halves = held.reshape((2, held.shape[0] // 2) + held.shape[1:])
         keep = lax.dynamic_index_in_dim(halves, bit, 0, keepdims=False)
         send = lax.dynamic_index_in_dim(halves, 1 - bit, 0, keepdims=False)
-        held = keep + xor_swap(send.astype(wire), axis, mask).astype(value.dtype)
+        held = keep + xor_swap(send.astype(wire), axis, mask).astype(held.dtype)
         bits.append(bit)
-    held = held.astype(wire)
+    return held, bits
+
+
+def gather_steps(held, steps, bits):
     for (axis, mask), bit in reversed(list(zip(steps, bits))):
         held = ordered_pair(held, xor_swap(held, axis, mask), bit)
-    return held.astype(value.dtype), tie
+    return held
+
+
+def pad_rows(value, multiple):
+    return jnp.concatenate(
+        [value, jnp.zeros((-value.shape[0] % multiple,) + value.shape[1:], value.dtype)], 0
+    )
 
 
 def to_heads(value, blocks, heads_here, head_dim):
@@ -172,10 +177,12 @@
     output = (tok_f32 + jnp.dot(attended, w_out, preferred_element_type=f32)).astype(bf16)
     d_out_part = jnp.dot(attended.T, cotangent, preferred_element_type=f32)
     d_attended = jnp.dot(cotangent, w_out.T, preferred_element_type=f32).astype(bf16)
+    d_attended, keys = lax.optimization_barrier((d_attended, keys))
     d_attn = split(lax.all_to_all(d_attended, "head", split_axis=1, concat_axis=0, tiled=True))
     d_weights = jnp.einsum("hbqd,hbskd->hbqsk", d_attn, values, preferred_element_type=f32)
     row_dot = jnp.sum(d_weights * weights, (-2, -1), keepdims=True)
     d_scores = (exponent_divisor * weights * (d_weights - row_dot)).astype(bf16)
+    attended, d_scores = lax.optimization_barrier((attended, d_scores))
     d_query = jnp.einsum("hbqsk,hbskd->hbqd", d_scores, keys, preferred_element_type=f32)
     d_keys = jnp.einsum("hbqsk,hbqd->hbskd", d_scores, q_heads, preferred_element_type=f32)
     d_values = jnp.einsum("hbqsk,hbqd->hbskd", weights_bf, d_attn, preferred_element_type=f32)
@@ -183,7 +190,7 @@
         "bse,hbskd->hekd",
         choose.astype(f32),
         grads,
-        precision=lax.Precision.HIGHEST,
+        precision=lax.Precision.HIGH,
         preferred_element_type=f32,
     )
     grad_ext = jnp.stack([scatter(d_keys), scatter(d_values)])
@@ -203,21 +210,25 @@
     d_normed_part = jnp.einsum("crk,cdk->rd", d_qkv, w_here, preferred_element_type=f32)
     d_gain_part = jnp.sum(d_normed_part * slab_scaled, 0)
     shares = d_normed_part.astype(bf16).reshape(n_head, -1, width)
+    d_qkv_part = jnp.einsum("rd,crk->cdk", gathered, d_qkv, preferred_element_type=f32)
+    head_steps, slab_steps = xor_steps(("head",)), xor_steps(("slab",))
+    sub = 8
+    wide = pad_rows(jnp.concatenate([d_out_part, d_gain_part[None]], 0), n_head * sub)
+    wide_part, head_bits = scatter_steps(wide, head_steps, bf16)
+    wide_part, shares = lax.optimization_barrier((wide_part, shares))
     received = lax.all_to_all(shares, "head", split_axis=0, concat_axis=0, tiled=True)
-    d_qkv_part = jnp.einsum("rd,crk->cdk", gathered, d_qkv, preferred_element_type=f32)
-    slots = jnp.zeros((n_head,) + d_qkv_part.shape, f32)
-    slots = lax.dynamic_update_index_in_dim(slots, d_qkv_part, head_index, 0)
-    pieces = [slots.reshape(-1, width), d_out_part, d_gain_part[None]]
-    rows = sum(piece.shape[0] for piece in pieces)
-    n_dev = n_head * n_slab
-    pieces.append(jnp.zeros((-rows % n_dev, width), f32))
-    total, received = butterfly_psum(jnp.concatenate(pieces, 0), bf16, received, 2)
+    narrow = d_qkv_part.reshape(-1, width)
+    both = pad_rows(jnp.concatenate([narrow, wide_part], 0), n_slab)
+    both_part, slab_bits = scatter_steps(both, slab_steps, bf16)
+    both = gather_steps(both_part.astype(bf16), slab_steps, slab_bits)
+    narrow_rows = narrow.shape[0]
+    wide_part = both[narrow_rows : narrow_rows + wide_part.shape[0]]
+    wide_part, received = lax.optimization_barrier((wide_part, received))
+    wide = gather_steps(wide_part, head_steps, head_bits).astype(f32)
+    d_w_qkv = both[:narrow_rows].astype(f32).reshape(d_qkv_part.shape)
+    d_w_out = wide[:width]
+    d_gain = wide[width]
     d_normed = jnp.sum(received.astype(f32), 0)
-    slot_rows = pieces[0].shape[0]
-    all_slots = total[:slot_rows].reshape(slots.shape)
-    d_w_qkv = lax.dynamic_index_in_dim(all_slots, head_index, 0, keepdims=False)
-    d_w_out = total[slot_rows : slot_rows + width]
-    d_gain = total[slot_rows + width]
     scaled = d_normed * norm_gain
     d_tokens = (
         cotangent.astype(f32)

time: 360 us -> 338 us (0.939)
  the two profiles are of different devices: /device:TPU:1 before, /device:TPU:89 now
where the time goes in v7:
time: 338 us; the launch traced here: 331 us
  waiting for transfers between devices  107 us (32%)
  matrix products  107 us (32%)
  starting transfers between devices  51.9 us (15%)
  other arithmetic  39.2 us (12%)
  local copies, waits for them, and re-layouts  23.7 us (7%)
    ppermute x16, waiting for transfers between devices, xor_swap(): return lax.ppermute(value, axis, [(i, i ^ mask) for i in range(size)])  61 us
    convert_element_type x1, other arithmetic, local(): d_scores = (exponent_divisor * weights * (d_weights - row_dot)).astype(bf16)  22.7 us
    ppermute x2, waiting for transfers between devices, passed_along(): return lax.ppermute(value, axis, pairs)  19.8 us
    dot_general x1, matrix products, local(): jnp.einsum('hbqd,hbskd->hbqsk', d_attn, values, preferred_element_type=f32)  19.3 us
    ppermute x2, waiting for transfers between devices, padded(): after = lax.ppermute(first, axis, down)  18.1 us
    ppermute x16, starting transfers between devices, xor_swap(): return lax.ppermute(value, axis, [(i, i ^ mask) for i in range(size)])  17.4 us
    dot_general x1, matrix products, local(): jnp.einsum('hbqd,hbskd->hbqsk', q_heads, keys, preferred_element_type=f32)  14.5 us
    dot_general x1, matrix products, local(): jnp.einsum('hbqsk,hbskd->hbqd', weights_bf, values, preferred_element_typ...  13 us
  transfers between devices with their start and end apart: 25, of which 17 were waited for; matrix products, arithmetic and copies ran while one was open for 37% of the time, Pallas kernels for 0%

profile of v7, /device:TPU:89, one launch (start us, length us, event | category | flops | bytes accessed | tf_op | source)
XLA Modules:
  0.0 331.4 jit_solution(291475221342732764)
XLA Ops:
  7.8 16.5 %collective-permute-done.1 = bf16[1024,384]{1,0:T(8,128)(2,1)S(1)} collective-permute-done((bf16[1024,384]{1,0:T(8,128)(2,1)}, bf16[1024,384]{1,0:T(8,128)(2,1)S(1)}, u32[]{:S(2)}, u32[]{:S(2)}) %collective-permute-start.1) | collective-permute-done | bytes 786464 | tf_op jit(solution)/shard_map/ppermute | solution.py:70
  30.7 3.9 %collective-permute-start.3 = (bf16[3,16,128,32]{2,1,3,0:T(8,128)(2,1)S(1)}, bf16[3,16,128,32]{2,1,3,0:T(8,128)(2,1)S(1)}, u32[]{:S(2)}, u32[]{:S(2)}) collective-permute-start(bf16[3,16,128,32]{2,1,3,0:T(8,128)(2,1)S(1)} %bitcast.311), channel_id=1, source_target_pairs={{4,0},{8,4},{12,8},{16,12},{20,16},{24,20},{28,24},{32,28},{36,32}... | collective-permute-start | bytes 1179656 | tf_op jit(solution)/shard_map/ppermute | solution.py:25
  36.8 18.1 %collective-permute-done.3 = bf16[3,16,128,32]{2,1,3,0:T(8,128)(2,1)S(1)} collective-permute-done((bf16[3,16,128,32]{2,1,3,0:T(8,128)(2,1)S(1)}, bf16[3,16,128,32]{2,1,3,0:T(8,128)(2,1)S(1)}, u32[]{:S(2)}, u32[]{:S(2)}) %collective-permute-start.3) | collective-permute-done | bytes 393248 | tf_op jit(solution)/shard_map/ppermute | solution.py:25
  54.8 8.6 %collective-permute-done.2 = bf16[3,16,128,32]{2,1,3,0:T(8,128)(2,1)S(1)} collective-permute-done((bf16[3,16,128,32]{2,1,3,0:T(8,128)(2,1)S(1)}, bf16[3,16,128,32]{2,1,3,0:T(8,128)(2,1)S(1)}, u32[]{:S(2)}, u32[]{:S(2)}) %collective-permute-start.2) | collective-permute-done | bytes 393248 | tf_op jit(solution)/shard_map/ppermute | solution.py:24
  67.1 6.0 %all-to-all-start.1 = ((bf16[512,4,96]{0,2,1:T(8,128)(2,1)}), bf16[512,4,96]{0,2,1:T(8,128)(2,1)S(1)}, u32[]{:S(2)}, u32[]{:S(2)}) async-start(bf16[512,4,96]{0,2,1:T(8,128)(2,1)} %bitcast.34), calls=%async_computation.1 | async-start | bytes 786432 | tf_op jit(solution)/shard_map/all_to_all | solution.py:181
  73.2 14.5 %fusion.3 = (f32[3,16,128]{2,1,0:T(8,128)S(1)}, f32[3,16,128,8,128]{2,4,3,1,0:T(8,128)}) fusion(f32[16,8]{1,0:T(8,128)S(1)} %fusion.152, bf16[3,16,8,128,32]{3,1,2,4,0:T(8,128)(2,1)} %convert_bitcast_fusion.1, bf16[16,128,3,32]{1,0,3,2:T(8,128)(2,1)S(1)} %bitcast.295), kind=kOutput, calls=%fused_computation.6 | convolution fusion | flops 421521408 | bytes 28729856 | tf_op jit(solution)/shard_map/hbqd,hbskd->hbqsk/dot_general | solution.py:165
  88.7 13.0 %fusion.56 = bf16[16,128,3,32]{1,3,0,2:T(8,128)(2,1)S(1)} fusion(bf16[3,16,8,128,32]{3,1,2,4,0:T(8,128)(2,1)S(1)} %convert_bitcast_fusion, f32[3,16,128,8,128]{2,4,3,1,0:T(8,128)} %get-tuple-element.110, f32[3,16,128]{2,1,0:T(8,128)S(1)} %get-tuple-element.109, f32[16,8]{1,0:T(8,128)S(1)} %fusion.152), kind=kOutput, calls=%fused_computation.62 | convolution fusion | flops 428015616 | bytes 28729856 | tf_op jit(solution)/shard_map/hbqsk,hbskd->hbqd/dot_general | solution.py:171
  102.9 4.3 %all-to-all-start = ((bf16[4,512,96]{1,2,0:T(8,128)(2,1)}), bf16[4,512,96]{1,2,0:T(8,128)(2,1)}, u32[]{:S(2)}, u32[]{:S(2)}) async-start(bf16[4,512,96]{1,2,0:T(8,128)(2,1)} %copy.44), calls=%async_computation | async-start | bytes 786432 | tf_op jit(solution)/shard_map/all_to_all | solution.py:174
  107.7 12.5 %fusion.8 = f32[3,16,8,128,32]{3,4,2,1,0:T(8,128)} fusion(bf16[16,128,3,32]{1,0,3,2:T(8,128)(2,1)S(1)} %reshape.271, f32[3,16,128,8,128]{2,4,3,1,0:T(8,128)} %get-tuple-element.110, f32[3,16,128]{2,1,0:T(8,128)S(1)} %get-tuple-element.109, f32[16,8]{1,0:T(8,128)S(1)} %fusion.152), kind=kOutput, calls=%fused_computation.11 | convolution fusion | flops 427819008 | bytes 31875584 | tf_op jit(solution)/shard_map/hbqsk,hbqd->hbskd/dot_general | solution.py:188
  120.2 19.3 %multiply_reduce_fusion = (f32[3,16,128]{2,1,0:T(8,128)S(1)}, f32[3,16,128,8,128]{2,4,3,1,0:T(8,128)}) fusion(f32[3,16,128]{2,1,0:T(8,128)S(1)} %get-tuple-element.109, f32[16,8]{1,0:T(8,128)S(1)} %fusion.152, f32[3,16,128,8,128]{2,4,3,1,0:T(8,128)} %get-tuple-element.110, bf16[3,16,8,128,32]{3,1,2,4,0:T(8,128)(2,1)} %copy-done.13, ...), kind=kOutput, calls=%fused_computation.3 | convolution fusion | flops 434104320 | bytes 53920256 | tf_op jit(solution)/shard_map/hbqd,hbskd->hbqsk/dot_general | solution.py:182
  139.5 22.7 %multiply_convert_fusion = bf16[3,16,128,8,128]{2,4,3,1,0:T(8,128)(2,1)} fusion(f32[3,16,128,8,128]{2,4,3,1,0:T(8,128)} %get-tuple-element.112, f32[3,16,128]{2,1,0:T(8,128)S(1)} %get-tuple-element.111, f32[3,16,128]{2,1,0:T(8,128)S(1)} %get-tuple-element.109, f32[16,8]{1,0:T(8,128)S(1)} %fusion.152, f32[3,16,128,8,128]{2,4,3,1,0:T(8,128)} %get-tuple-element.110), kind=kLoop, calls=%fused_computation.2 | loop fusion | flops 44040192 | bytes 62964224 | tf_op jit(solution)/shard_map/convert_element_type | solution.py:184
  162.3 4.7 %fusion.28 = f32[1,3,48,128,32]{3,2,4,1,0:T(8,128)S(1)} fusion(f32[3,16,8,128,32]{3,4,2,1,0:T(8,128)S(1)} %copy-done.7, s32[16,8]{0,1:T(8,128)S(1)} %add_select_fusion), kind=kOutput, calls=%fused_computation.43 | convolution fusion | flops 452990976 | bytes 8651264 | tf_op jit(solution)/shard_map/bse,hbskd->hekd/dot_general | solution.py:189
  167.0 11.7 %fusion.96 = f32[3,16,8,128,32]{3,4,2,1,0:T(8,128)} fusion(bf16[3,16,128,8,128]{2,4,3,1,0:T(8,128)(2,1)} %multiply_convert_fusion, bf16[16,128,3,32]{1,0,3,2:T(8,128)(2,1)} %bitcast.296), kind=kOutput, calls=%fused_computation.118 | convolution fusion | flops 402653184 | bytes 19267584 | tf_op jit(solution)/shard_map/hbqsk,hbqd->hbskd/dot_general | solution.py:187
  178.6 7.4 %fusion.25 = f32[1,3,48,128,32]{3,2,4,1,0:T(8,128)S(1)} fusion(f32[3,16,8,128,32]{3,4,2,1,0:T(8,128)} %fusion.96, s32[16,8]{0,1:T(8,128)S(1)} %add_select_fusion), kind=kOutput, calls=%fused_computation.42 | convolution fusion | flops 452990976 | bytes 8651264 | tf_op jit(solution)/shard_map/bse,hbskd->hekd/dot_general | solution.py:189
  193.2 7.6 %fusion.53 = f32[3,16,128,32]{2,3,1,0:T(8,128)S(1)} fusion(bf16[3,16,128,8,128]{2,4,3,1,0:T(8,128)(2,1)} %multiply_convert_fusion, bf16[3,16,8,128,32]{3,1,2,4,0:T(8,128)(2,1)S(1)} %copy-done.1), kind=kOutput, calls=%fused_computation.60 | convolution fusion | flops 403046400 | bytes 16515072 | tf_op jit(solution)/shard_map/hbqsk,hbskd->hbqd/dot_general | solution.py:186
  211.2 18.8 %collective-permute-done.6 = bf16[2,3,16,128,32]{3,2,4,1,0:T(8,128)(2,1)} collective-permute-done((bf16[2,3,16,128,32]{3,2,4,1,0:T(8,128)(2,1)}, bf16[2,3,16,128,32]{3,2,4,1,0:T(8,128)(2,1)}, u32[]{:S(2)}, u32[]{:S(2)}) %collective-permute-start.6) | collective-permute-done | bytes 786464 | tf_op jit(solution)/shard_map/ppermute | solution.py:33
  241.8 4.2 %fusion.16 = (f32[384]{0:T(512)S(1)}, bf16[2048,384,1]{1,0,2:T(8,128)(2,1)}) fusion(f32[2048]{0:T(1024)S(1)} %copy-done.33, bf16[1024,384]{1,0:T(8,128)(2,1)S(1)} %copy-done.18, bf16[1024,384]{1,0:T(8,128)(2,1)S(1)} %copy-done.15, bf16[3,384,384]{2,1,0:T(8,128)(2,1)S(1)} %copy-done, s32[]{:T(128)S(6)} %select_n.147, ...), kind=kOutput, calls=%fused_computation.24 | convolution fusion | flops 460455552 | bytes 4630020 | tf_op jit(solution)/shard_map/crk,cdk->rd/dot_general | solution.py:210
  256.4 3.5 %collective-permute-done.10 = bf16[208,384]{1,0:T(8,128)(2,1)S(1)} collective-permute-done((bf16[208,384]{1,0:T(8,128)(2,1)S(1)}, bf16[208,384]{1,0:T(8,128)(2,1)S(1)}, u32[]{:S(2)}, u32[]{:S(2)}) %collective-permute-start.10) | collective-permute-done | bytes 159776 | tf_op jit(solution)/shard_map/ppermute | solution.py:70
  263.6 4.3 %collective-permute-done.12 = bf16[52,384]{1,0:T(8,128)(2,1)S(1)} collective-permute-done((bf16[52,384]{1,0:T(8,128)(2,1)S(1)}, bf16[52,384]{1,0:T(8,128)(2,1)S(1)}, u32[]{:S(2)}, u32[]{:S(2)}) %collective-permute-start.12) | collective-permute-done | bytes 39968 | tf_op jit(solution)/shard_map/ppermute | solution.py:70
  272.0 4.0 %collective-permute-done.14 = bf16[13,384]{1,0:T(8,128)(2,1)S(1)} collective-permute-done((bf16[13,384]{1,0:T(8,128)(2,1)S(1)}, bf16[13,384]{1,0:T(8,128)(2,1)S(1)}, u32[]{:S(2)}, u32[]{:S(2)}) %collective-permute-start.14) | collective-permute-done | bytes 10016 | tf_op jit(solution)/shard_map/ppermute | solution.py:70
  276.1 4.0 %collective-permute-done.15 = bf16[13,384]{1,0:T(8,128)(2,1)S(1)} collective-permute-done((bf16[13,384]{1,0:T(8,128)(2,1)S(1)}, bf16[13,384]{1,0:T(8,128)(2,1)S(1)}, u32[]{:S(2)}, u32[]{:S(2)}) %collective-permute-start.15) | collective-permute-done | bytes 10016 | tf_op jit(solution)/shard_map/ppermute | solution.py:70
  282.0 11.3 %all-to-all-start.2 = ((bf16[4,512,384]{2,1,0:T(8,128)(2,1)}), bf16[4,512,384]{2,1,0:T(8,128)(2,1)S(1)}, u32[]{:S(2)}, u32[]{:S(2)}) async-start(bf16[4,512,384]{2,1,0:T(8,128)(2,1)} %bitcast.306), calls=%async_computation.2 | async-start | bytes 3145728 | tf_op jit(solution)/shard_map/all_to_all | solution.py:219
  293.7 4.3 %collective-permute-done.17 = bf16[52,384]{1,0:T(8,128)(2,1)S(1)} collective-permute-done((bf16[52,384]{1,0:T(8,128)(2,1)S(1)}, bf16[52,384]{1,0:T(8,128)(2,1)S(1)}, u32[]{:S(2)}, u32[]{:S(2)}) %collective-permute-start.17) | collective-permute-done | bytes 39968 | tf_op jit(solution)/shard_map/ppermute | solution.py:70
  306.8 10.7 %collective-permute-done.19 = bf16[208,384]{1,0:T(8,128)(2,1)S(1)} collective-permute-done((bf16[208,384]{1,0:T(8,128)(2,1)S(1)}, bf16[208,384]{1,0:T(8,128)(2,1)S(1)}, u32[]{:S(2)}, u32[]{:S(2)}) %collective-permute-start.19) | collective-permute-done | bytes 159776 | tf_op jit(solution)/shard_map/ppermute | solution.py:70
  (206 shorter events, 93.3 us)
Async XLA Ops:
  0.7 2.3 collective-permute-start
  5.4 18.9 %collective-permute-start.1 = (bf16[1024,384]{1,0:T(8,128)(2,1)}, bf16[1024,384]{1,0:T(8,128)(2,1)S(1)}, u32[]{:S(2)}, u32[]{:S(2)}) collective-permute-start(bf16[1024,384]{1,0:T(8,128)(2,1)} %get-tuple-element.83), channel_id=1, source_target_pairs={{0,2},{1,3},{2,0},{3,1},{4,6},{5,7},{6,4},{7,5},{8,10},{9,11},{10,... | collective-permute-start | bytes 2359304 | tf_op jit(solution)/shard_map/ppermute | solution.py:70
  26.9 60.7 %collective-permute-start.5 = (bf16[3,16,128,32]{2,1,3,0:T(8,128)(2,1)S(1)}, bf16[3,16,128,32]{2,1,3,0:T(8,128)(2,1)S(1)}, u32[]{:S(2)}, u32[]{:S(2)}) collective-permute-start(bf16[3,16,128,32]{2,1,3,0:T(8,128)(2,1)S(1)} %bitcast.307), channel_id=1, source_target_pairs={{4,0},{8,4},{12,8},{16,12},{20,16},{24,20},{28,24},{32,28},{36,32}... | collective-permute-start | bytes 1179656 | tf_op jit(solution)/shard_map/ppermute | solution.py:25
  29.9 57.8 %collective-permute-start.4 = (bf16[3,16,128,32]{2,1,3,0:T(8,128)(2,1)S(1)}, bf16[3,16,128,32]{2,1,3,0:T(8,128)(2,1)S(1)}, u32[]{:S(2)}, u32[]{:S(2)}) collective-permute-start(bf16[3,16,128,32]{2,1,3,0:T(8,128)(2,1)S(1)} %bitcast.308), channel_id=1, source_target_pairs={{0,4},{4,8},{8,12},{12,16},{16,20},{20,24},{24,28},{28,32},{32,36}... | collective-permute-start | bytes 1179656 | tf_op jit(solution)/shard_map/ppermute | solution.py:24
  30.7 24.1 %collective-permute-start.3 = (bf16[3,16,128,32]{2,1,3,0:T(8,128)(2,1)S(1)}, bf16[3,16,128,32]{2,1,3,0:T(8,128)(2,1)S(1)}, u32[]{:S(2)}, u32[]{:S(2)}) collective-permute-start(bf16[3,16,128,32]{2,1,3,0:T(8,128)(2,1)S(1)} %bitcast.311), channel_id=1, source_target_pairs={{4,0},{8,4},{12,8},{16,12},{20,16},{24,20},{28,24},{32,28},{36,32}... | collective-permute-start | bytes 1179656 | tf_op jit(solution)/shard_map/ppermute | solution.py:25
  34.6 28.8 %collective-permute-start.2 = (bf16[3,16,128,32]{2,1,3,0:T(8,128)(2,1)S(1)}, bf16[3,16,128,32]{2,1,3,0:T(8,128)(2,1)S(1)}, u32[]{:S(2)}, u32[]{:S(2)}) collective-permute-start(bf16[3,16,128,32]{2,1,3,0:T(8,128)(2,1)S(1)} %bitcast.312), channel_id=1, source_target_pairs={{0,4},{4,8},{8,12},{12,16},{16,20},{20,24},{24,28},{28,32},{32,36}... | collective-permute-start | bytes 1179656 | tf_op jit(solution)/shard_map/ppermute | solution.py:24
  67.1 35.8 %all-to-all-start.1 = ((bf16[512,4,96]{0,2,1:T(8,128)(2,1)}), bf16[512,4,96]{0,2,1:T(8,128)(2,1)S(1)}, u32[]{:S(2)}, u32[]{:S(2)}) async-start(bf16[512,4,96]{0,2,1:T(8,128)(2,1)} %bitcast.34), calls=%async_computation.1 | async-start | bytes 786432 | tf_op jit(solution)/shard_map/all_to_all | solution.py:181
  102.9 64.0 %all-to-all-start = ((bf16[4,512,96]{1,2,0:T(8,128)(2,1)}), bf16[4,512,96]{1,2,0:T(8,128)(2,1)}, u32[]{:S(2)}, u32[]{:S(2)}) async-start(bf16[4,512,96]{1,2,0:T(8,128)(2,1)} %copy.44), calls=%async_computation | async-start | bytes 786432 | tf_op jit(solution)/shard_map/all_to_all | solution.py:174
  189.4 21.8 %collective-permute-start.7 = (bf16[2,3,16,128,32]{3,2,4,1,0:T(8,128)(2,1)}, bf16[2,3,16,128,32]{3,2,4,1,0:T(8,128)(2,1)}, u32[]{:S(2)}, u32[]{:S(2)}) collective-permute-start(bf16[2,3,16,128,32]{3,2,4,1,0:T(8,128)(2,1)} %get-tuple-element.74), channel_id=1, source_target_pairs={{0,4},{4,8},{8,12},{12,16},{16,20},{20,24},{24,28},{28,32},{32,36}... | collective-permute-start | bytes 2359304 | tf_op jit(solution)/shard_map/ppermute | solution.py:33
  192.1 37.8 %collective-permute-start.6 = (bf16[2,3,16,128,32]{3,2,4,1,0:T(8,128)(2,1)}, bf16[2,3,16,128,32]{3,2,4,1,0:T(8,128)(2,1)}, u32[]{:S(2)}, u32[]{:S(2)}) collective-permute-start(bf16[2,3,16,128,32]{3,2,4,1,0:T(8,128)(2,1)} %get-tuple-element.73), channel_id=1, source_target_pairs={{0,124},{4,0},{8,4},{12,8},{16,12},{20,16},{24,20},{28,24},{32,28}... | collective-permute-start | bytes 2359304 | tf_op jit(solution)/shard_map/ppermute | solution.py:33
  249.4 4.0 %collective-permute-start.9 = (bf16[104,384]{1,0:T(8,128)(2,1)S(1)}, bf16[104,384]{1,0:T(8,128)(2,1)S(1)}, u32[]{:S(2)}, u32[]{:S(2)}) collective-permute-start(bf16[104,384]{1,0:T(8,128)(2,1)S(1)} %fusion.115), channel_id=1, source_target_pairs={{0,2},{1,3},{2,0},{3,1},{4,6},{5,7},{6,4},{7,5},{8,10},{9,11},{10,... | collective-permute-start | bytes 239624 | tf_op jit(solution)/shard_map/ppermute | solution.py:70
  253.6 6.4 %collective-permute-start.10 = (bf16[208,384]{1,0:T(8,128)(2,1)S(1)}, bf16[208,384]{1,0:T(8,128)(2,1)S(1)}, u32[]{:S(2)}, u32[]{:S(2)}) collective-permute-start(bf16[208,384]{1,0:T(8,128)(2,1)S(1)} %fusion.107), channel_id=1, source_target_pairs={{0,4},{4,0},{8,12},{12,8},{16,20},{20,16},{24,28},{28,24},{32,36},... | collective-permute-start | bytes 479240 | tf_op jit(solution)/shard_map/ppermute | solution.py:70
  260.0 3.4 %collective-permute-start.11 = (bf16[104,384]{1,0:T(8,128)(2,1)S(1)}, bf16[104,384]{1,0:T(8,128)(2,1)S(1)}, u32[]{:S(2)}, u32[]{:S(2)}) collective-permute-start(bf16[104,384]{1,0:T(8,128)(2,1)S(1)} %fusion.116), channel_id=1, source_target_pairs={{0,8},{4,12},{8,0},{12,4},{16,24},{20,28},{24,16},{28,20},{32,40},... | collective-permute-start | bytes 239624 | tf_op jit(solution)/shard_map/ppermute | solution.py:70
  263.4 4.5 %collective-permute-start.12 = (bf16[52,384]{1,0:T(8,128)(2,1)S(1)}, bf16[52,384]{1,0:T(8,128)(2,1)S(1)}, u32[]{:S(2)}, u32[]{:S(2)}) collective-permute-start(bf16[52,384]{1,0:T(8,128)(2,1)S(1)} %fusion.130), channel_id=1, source_target_pairs={{0,16},{4,20},{8,24},{12,28},{16,0},{20,4},{24,8},{28,12},{32,48},... | collective-permute-start | bytes 119816 | tf_op jit(solution)/shard_map/ppermute | solution.py:70
  268.0 3.9 %collective-permute-start.13 = (bf16[26,384]{1,0:T(8,128)(2,1)S(1)}, bf16[26,384]{1,0:T(8,128)(2,1)S(1)}, u32[]{:S(2)}, u32[]{:S(2)}) collective-permute-start(bf16[26,384]{1,0:T(8,128)(2,1)S(1)} %fusion.139), channel_id=1, source_target_pairs={{0,32},{4,36},{8,40},{12,44},{16,48},{20,52},{24,56},{28,60},{32,0... | collective-permute-start | bytes 59912 | tf_op jit(solution)/shard_map/ppermute | solution.py:70
  271.9 4.1 %collective-permute-start.14 = (bf16[13,384]{1,0:T(8,128)(2,1)S(1)}, bf16[13,384]{1,0:T(8,128)(2,1)S(1)}, u32[]{:S(2)}, u32[]{:S(2)}) collective-permute-start(bf16[13,384]{1,0:T(8,128)(2,1)S(1)} %fusion.147), channel_id=1, source_target_pairs={{0,64},{4,68},{8,72},{12,76},{16,80},{20,84},{24,88},{28,92},{32,9... | collective-permute-start | bytes 29960 | tf_op jit(solution)/shard_map/ppermute | solution.py:70
  276.0 4.1 %collective-permute-start.15 = (bf16[13,384]{1,0:T(8,128)(2,1)S(1)}, bf16[13,384]{1,0:T(8,128)(2,1)S(1)}, u32[]{:S(2)}, u32[]{:S(2)}) collective-permute-start(bf16[13,384]{1,0:T(8,128)(2,1)S(1)} %fusion.144), channel_id=1, source_target_pairs={{0,64},{4,68},{8,72},{12,76},{16,80},{20,84},{24,88},{28,92},{32,9... | collective-permute-start | bytes 29960 | tf_op jit(solution)/shard_map/ppermute | solution.py:70
  280.2 13.2 %collective-permute-start.16 = (bf16[26,384]{1,0:T(8,128)(2,1)S(1)}, bf16[26,384]{1,0:T(8,128)(2,1)S(1)}, u32[]{:S(2)}, u32[]{:S(2)}) collective-permute-start(bf16[26,384]{1,0:T(8,128)(2,1)S(1)} %get-tuple-element.103), channel_id=1, source_target_pairs={{0,32},{4,36},{8,40},{12,44},{16,48},{20,52},{24,56},{28,60},{32,0... | collective-permute-start | bytes 59912 | tf_op jit(solution)/shard_map/ppermute | solution.py:70
  282.0 40.6 %all-to-all-start.2 = ((bf16[4,512,384]{2,1,0:T(8,128)(2,1)}), bf16[4,512,384]{2,1,0:T(8,128)(2,1)S(1)}, u32[]{:S(2)}, u32[]{:S(2)}) async-start(bf16[4,512,384]{2,1,0:T(8,128)(2,1)} %bitcast.306), calls=%async_computation.2 | async-start | bytes 3145728 | tf_op jit(solution)/shard_map/all_to_all | solution.py:219
  293.4 4.6 %collective-permute-start.17 = (bf16[52,384]{1,0:T(8,128)(2,1)S(1)}, bf16[52,384]{1,0:T(8,128)(2,1)S(1)}, u32[]{:S(2)}, u32[]{:S(2)}) collective-permute-start(bf16[52,384]{1,0:T(8,128)(2,1)S(1)} %pad_maximum_fusion.10), channel_id=1, source_target_pairs={{0,16},{4,20},{8,24},{12,28},{16,0},{20,4},{24,8},{28,12},{32,48},... | collective-permute-start | bytes 119816 | tf_op jit(solution)/shard_map/ppermute | solution.py:70
  298.1 3.6 %collective-permute-start.18 = (bf16[104,384]{1,0:T(8,128)(2,1)S(1)}, bf16[104,384]{1,0:T(8,128)(2,1)S(1)}, u32[]{:S(2)}, u32[]{:S(2)}) collective-permute-start(bf16[104,384]{1,0:T(8,128)(2,1)S(1)} %pad_maximum_fusion.9), channel_id=1, source_target_pairs={{0,8},{4,12},{8,0},{12,4},{16,24},{20,28},{24,16},{28,20},{32,40},... | collective-permute-start | bytes 239624 | tf_op jit(solution)/shard_map/ppermute | solution.py:70
  301.9 15.7 %collective-permute-start.19 = (bf16[208,384]{1,0:T(8,128)(2,1)S(1)}, bf16[208,384]{1,0:T(8,128)(2,1)S(1)}, u32[]{:S(2)}, u32[]{:S(2)}) collective-permute-start(bf16[208,384]{1,0:T(8,128)(2,1)S(1)} %get-tuple-element.95), channel_id=1, source_target_pairs={{0,4},{4,0},{8,12},{12,8},{16,20},{20,16},{24,28},{28,24},{32,36},... | collective-permute-start | bytes 479240 | tf_op jit(solution)/shard_map/ppermute | solution.py:70
  323.1 3.4 %collective-permute-start.20 = (bf16[104,384]{1,0:T(8,128)(2,1)S(1)}, bf16[104,384]{1,0:T(8,128)(2,1)S(1)}, u32[]{:S(2)}, u32[]{:S(2)}) collective-permute-start(bf16[104,384]{1,0:T(8,128)(2,1)S(1)} %slice_bitcast_fusion), channel_id=1, source_target_pairs={{0,2},{1,3},{2,0},{3,1},{4,6},{5,7},{6,4},{7,5},{8,10},{9,11},{10,... | collective-permute-start | bytes 239624 | tf_op jit(solution)/shard_map/ppermute | solution.py:70
  326.6 2.9 collective-permute-start.21
  (39 other events, 370.7 us)

commit v8 on v7

--- a/solution.py
+++ b/solution.py
@@ -78,14 +78,15 @@
 
 
 def butterfly_gather(value, axis):
-    size = lax.axis_size(axis)
+    masks = [mask for _, mask in xor_steps((axis,))][::-1]
     held = value
-    mask = 1
-    while mask < size:
+    for mask in masks:
         bit = (lax.axis_index(axis) // mask) % 2
         held = ordered_pair(held, xor_swap(held, axis, mask), bit)
-        mask *= 2
-    return held
+    depth = len(masks)
+    held = held.reshape((2,) * depth + value.shape)
+    held = jnp.transpose(held, tuple(range(depth))[::-1] + tuple(range(depth, held.ndim)))
+    return held.reshape((-1,) + value.shape[1:])
 
 
 def scatter_steps(held, steps, wire):
@@ -220,10 +221,10 @@
     narrow = d_qkv_part.reshape(-1, width)
     both = pad_rows(jnp.concatenate([narrow, wide_part], 0), n_slab)
     both_part, slab_bits = scatter_steps(both, slab_steps, bf16)
+    both_part, received = lax.optimization_barrier((both_part, received))
     both = gather_steps(both_part.astype(bf16), slab_steps, slab_bits)
     narrow_rows = narrow.shape[0]
     wide_part = both[narrow_rows : narrow_rows + wide_part.shape[0]]
-    wide_part, received = lax.optimization_barrier((wide_part, received))
     wide = gather_steps(wide_part, head_steps, head_bits).astype(f32)
     d_w_qkv = both[:narrow_rows].astype(f32).reshape(d_qkv_part.shape)
     d_w_out = wide[:width]

time: 338 us -> 347 us (1.027)
  the two profiles are of different devices: /device:TPU:89 before, /device:TPU:1 now
where the time goes in v8:
time: 347 us; the launch traced here: 340 us
  matrix products  109 us (31%)
  waiting for transfers between devices  81.2 us (23%)
  starting transfers between devices  71.8 us (21%)
  other arithmetic  41.9 us (12%)
  local copies, waits for them, and re-layouts  33.9 us (10%)
    ppermute x16, waiting for transfers between devices, xor_swap(): return lax.ppermute(value, axis, [(i, i ^ mask) for i in range(size)])  33.4 us
    ppermute x16, starting transfers between devices, xor_swap(): return lax.ppermute(value, axis, [(i, i ^ mask) for i in range(size)])  31.4 us
    convert_element_type x1, other arithmetic, local(): d_scores = (exponent_divisor * weights * (d_weights - row_dot)).astype(bf16)  22.8 us
    dot_general x1, matrix products, local(): jnp.einsum('hbqd,hbskd->hbqsk', d_attn, values, preferred_element_type=f32)  19.4 us
    ppermute x2, starting transfers between devices, padded(): after = lax.ppermute(first, axis, down)  16.2 us
    ppermute x2, waiting for transfers between devices, padded(): after = lax.ppermute(first, axis, down)  15.2 us
    dot_general x1, matrix products, local(): jnp.einsum('hbqd,hbskd->hbqsk', q_heads, keys, preferred_element_type=f32)  14.4 us
    ppermute x2, waiting for transfers between devices, passed_along(): return lax.ppermute(value, axis, pairs)  13.7 us
  transfers between devices with their start and end apart: 25, of which 18 were waited for; matrix products, arithmetic and copies ran while one was open for 38% of the time, Pallas kernels for 0%

profile of v8, /device:TPU:1, one launch (start us, length us, event | category | flops | bytes accessed | tf_op | source)
XLA Modules:
  0.0 339.7 jit_solution(6216448699124397278)
XLA Ops:
  2.8 8.6 %collective-permute-done = bf16[512,384]{1,0:T(8,128)(2,1)S(1)} collective-permute-done((bf16[512,384]{1,0:T(8,128)(2,1)}, bf16[512,384]{1,0:T(8,128)(2,1)S(1)}, u32[]{:S(2)}, u32[]{:S(2)}) %collective-permute-start) | collective-permute-done | bytes 393248 | tf_op jit(solution)/shard_map/ppermute | solution.py:70
  25.1 8.9 %collective-permute-start.5 = (bf16[3,16,128,32]{2,1,3,0:T(8,128)(2,1)}, bf16[3,16,128,32]{2,1,3,0:T(8,128)(2,1)}, u32[]{:S(2)}, u32[]{:S(2)}) collective-permute-start(bf16[3,16,128,32]{2,1,3,0:T(8,128)(2,1)} %bitcast.27), channel_id=1, source_target_pairs={{4,0},{8,4},{12,8},{16,12},{20,16},{24,20},{28,24},{32,28},{36,32}... | collective-permute-start | bytes 1179656 | tf_op jit(solution)/shard_map/ppermute | solution.py:25
  35.8 7.3 %collective-permute-start.3 = (bf16[3,16,128,32]{2,1,3,0:T(8,128)(2,1)S(1)}, bf16[3,16,128,32]{2,1,3,0:T(8,128)(2,1)S(1)}, u32[]{:S(2)}, u32[]{:S(2)}) collective-permute-start(bf16[3,16,128,32]{2,1,3,0:T(8,128)(2,1)S(1)} %bitcast.325), channel_id=1, source_target_pairs={{4,0},{8,4},{12,8},{16,12},{20,16},{24,20},{28,24},{32,28},{36,32}... | collective-permute-start | bytes 1179656 | tf_op jit(solution)/shard_map/ppermute | solution.py:25
  43.9 15.2 %collective-permute-done.3 = bf16[3,16,128,32]{2,1,3,0:T(8,128)(2,1)S(1)} collective-permute-done((bf16[3,16,128,32]{2,1,3,0:T(8,128)(2,1)S(1)}, bf16[3,16,128,32]{2,1,3,0:T(8,128)(2,1)S(1)}, u32[]{:S(2)}, u32[]{:S(2)}) %collective-permute-start.3) | collective-permute-done | bytes 393248 | tf_op jit(solution)/shard_map/ppermute | solution.py:25
  59.2 9.4 %collective-permute-done.2 = bf16[3,16,128,32]{2,1,3,0:T(8,128)(2,1)S(1)} collective-permute-done((bf16[3,16,128,32]{2,1,3,0:T(8,128)(2,1)S(1)}, bf16[3,16,128,32]{2,1,3,0:T(8,128)(2,1)S(1)}, u32[]{:S(2)}, u32[]{:S(2)}) %collective-permute-start.2) | collective-permute-done | bytes 393248 | tf_op jit(solution)/shard_map/ppermute | solution.py:24
  73.2 5.8 %all-to-all-start.1 = ((bf16[512,4,96]{0,2,1:T(8,128)(2,1)}), bf16[512,4,96]{0,2,1:T(8,128)(2,1)}, u32[]{:S(2)}, u32[]{:S(2)}) async-start(bf16[512,4,96]{0,2,1:T(8,128)(2,1)} %bitcast.324), calls=%async_computation.1 | async-start | bytes 786432 | tf_op jit(solution)/shard_map/all_to_all | solution.py:182
  79.0 14.4 %fusion.3 = (f32[3,16,128]{2,1,0:T(8,128)S(1)}, f32[3,16,128,8,128]{2,4,3,1,0:T(8,128)}) fusion(f32[16,8]{1,0:T(8,128)S(1)} %fusion.150, bf16[3,16,8,128,32]{3,1,2,4,0:T(8,128)(2,1)} %convert_bitcast_fusion.1, bf16[16,128,3,32]{1,0,3,2:T(8,128)(2,1)} %bitcast.312), kind=kOutput, calls=%fused_computation.6 | convolution fusion | flops 421521408 | bytes 28729856 | tf_op jit(solution)/shard_map/hbqd,hbskd->hbqsk/dot_general | solution.py:166
  95.7 13.0 %fusion.57 = bf16[16,128,3,32]{1,3,0,2:T(8,128)(2,1)S(1)} fusion(bf16[3,16,8,128,32]{3,1,2,4,0:T(8,128)(2,1)S(1)} %convert_bitcast_fusion, f32[3,16,128,8,128]{2,4,3,1,0:T(8,128)} %get-tuple-element.117, f32[3,16,128]{2,1,0:T(8,128)S(1)} %get-tuple-element.116, f32[16,8]{1,0:T(8,128)S(1)} %fusion.150), kind=kOutput, calls=%fused_computation.62 | convolution fusion | flops 428015616 | bytes 28729856 | tf_op jit(solution)/shard_map/hbqsk,hbskd->hbqd/dot_general | solution.py:172
  113.3 4.3 %all-to-all-start = ((bf16[4,512,96]{1,2,0:T(8,128)(2,1)}), bf16[4,512,96]{1,2,0:T(8,128)(2,1)}, u32[]{:S(2)}, u32[]{:S(2)}) async-start(bf16[4,512,96]{1,2,0:T(8,128)(2,1)} %copy.70), calls=%async_computation | async-start | bytes 786432 | tf_op jit(solution)/shard_map/all_to_all | solution.py:175
  121.5 12.9 %fusion.8 = f32[3,16,8,128,32]{3,4,2,1,0:T(8,128)} fusion(bf16[16,128,3,32]{1,0,3,2:T(8,128)(2,1)} %reshape.290, f32[3,16,128,8,128]{2,4,3,1,0:T(8,128)} %get-tuple-element.117, f32[3,16,128]{2,1,0:T(8,128)S(1)} %get-tuple-element.116, f32[16,8]{1,0:T(8,128)S(1)} %fusion.150), kind=kOutput, calls=%fused_computation.11 | convolution fusion | flops 427819008 | bytes 31875584 | tf_op jit(solution)/shard_map/hbqsk,hbqd->hbskd/dot_general | solution.py:189
  134.4 19.4 %multiply_reduce_fusion = (f32[3,16,128]{2,1,0:T(8,128)S(1)}, f32[3,16,128,8,128]{2,4,3,1,0:T(8,128)}) fusion(f32[3,16,128]{2,1,0:T(8,128)S(1)} %get-tuple-element.116, f32[16,8]{1,0:T(8,128)S(1)} %fusion.150, f32[3,16,128,8,128]{2,4,3,1,0:T(8,128)} %get-tuple-element.117, bf16[3,16,8,128,32]{3,1,2,4,0:T(8,128)(2,1)} %copy-done.14, ...), kind=kOutput, calls=%fused_computation.3 | convolution fusion | flops 434104320 | bytes 53920256 | tf_op jit(solution)/shard_map/hbqd,hbskd->hbqsk/dot_general | solution.py:183
  153.8 22.8 %multiply_convert_fusion = bf16[3,16,128,8,128]{2,4,3,1,0:T(8,128)(2,1)} fusion(f32[3,16,128,8,128]{2,4,3,1,0:T(8,128)} %get-tuple-element.119, f32[3,16,128]{2,1,0:T(8,128)S(1)} %get-tuple-element.118, f32[3,16,128]{2,1,0:T(8,128)S(1)} %get-tuple-element.116, f32[16,8]{1,0:T(8,128)S(1)} %fusion.150, f32[3,16,128,8,128]{2,4,3,1,0:T(8,128)} %get-tuple-element.117), kind=kLoop, calls=%fused_computation.2 | loop fusion | flops 44040192 | bytes 62964224 | tf_op jit(solution)/shard_map/convert_element_type | solution.py:185
  176.6 6.1 %fusion.24 = f32[1,3,48,128,32]{3,2,4,1,0:T(8,128)} fusion(f32[3,16,8,128,32]{3,4,2,1,0:T(8,128)S(1)} %copy-done.9, s32[16,8]{0,1:T(8,128)S(1)} %add_select_fusion), kind=kOutput, calls=%fused_computation.41 | convolution fusion | flops 452990976 | bytes 8651264 | tf_op jit(solution)/shard_map/bse,hbskd->hekd/dot_general | solution.py:190
  182.6 11.7 %fusion.95 = f32[3,16,8,128,32]{3,4,2,1,0:T(8,128)} fusion(bf16[3,16,128,8,128]{2,4,3,1,0:T(8,128)(2,1)} %multiply_convert_fusion, bf16[16,128,3,32]{1,0,3,2:T(8,128)(2,1)} %bitcast.313), kind=kOutput, calls=%fused_computation.118 | convolution fusion | flops 402653184 | bytes 19267584 | tf_op jit(solution)/shard_map/hbqsk,hbqd->hbskd/dot_general | solution.py:188
  194.3 7.6 %fusion.21 = f32[1,3,48,128,32]{3,2,4,1,0:T(8,128)S(1)} fusion(f32[3,16,8,128,32]{3,4,2,1,0:T(8,128)} %fusion.95, s32[16,8]{0,1:T(8,128)S(1)} %add_select_fusion), kind=kOutput, calls=%fused_computation.40 | convolution fusion | flops 452990976 | bytes 8651264 | tf_op jit(solution)/shard_map/bse,hbskd->hekd/dot_general | solution.py:190
  208.0 4.5 %collective-permute-start.6 = (bf16[2,3,16,128,32]{3,2,4,1,0:T(8,128)(2,1)}, bf16[2,3,16,128,32]{3,2,4,1,0:T(8,128)(2,1)}, u32[]{:S(2)}, u32[]{:S(2)}) collective-permute-start(bf16[2,3,16,128,32]{3,2,4,1,0:T(8,128)(2,1)} %get-tuple-element.78), channel_id=1, source_target_pairs={{0,124},{4,0},{8,4},{12,8},{16,12},{20,16},{24,20},{28,24},{32,28}... | collective-permute-start | bytes 2359304 | tf_op jit(solution)/shard_map/ppermute | solution.py:33
  212.4 7.6 %fusion.51 = f32[3,16,128,32]{2,3,1,0:T(8,128)S(1)} fusion(bf16[3,16,128,8,128]{2,4,3,1,0:T(8,128)(2,1)} %multiply_convert_fusion, bf16[3,16,8,128,32]{3,1,2,4,0:T(8,128)(2,1)S(1)} %copy-done.1), kind=kOutput, calls=%fused_computation.60 | convolution fusion | flops 403046400 | bytes 16515072 | tf_op jit(solution)/shard_map/hbqsk,hbskd->hbqd/dot_general | solution.py:187
  230.3 12.7 %collective-permute-done.6 = bf16[2,3,16,128,32]{3,2,4,1,0:T(8,128)(2,1)} collective-permute-done((bf16[2,3,16,128,32]{3,2,4,1,0:T(8,128)(2,1)}, bf16[2,3,16,128,32]{3,2,4,1,0:T(8,128)(2,1)}, u32[]{:S(2)}, u32[]{:S(2)}) %collective-permute-start.6) | collective-permute-done | bytes 786464 | tf_op jit(solution)/shard_map/ppermute | solution.py:33
  265.9 5.9 %collective-permute-done.10 = bf16[208,384]{1,0:T(8,128)(2,1)S(1)} collective-permute-done((bf16[208,384]{1,0:T(8,128)(2,1)S(1)}, bf16[208,384]{1,0:T(8,128)(2,1)S(1)}, u32[]{:S(2)}, u32[]{:S(2)}) %collective-permute-start.10) | collective-permute-done | bytes 159776 | tf_op jit(solution)/shard_map/ppermute | solution.py:70
  275.6 7.0 %all-to-all-start.2 = ((bf16[4,512,384]{2,1,0:T(8,128)(2,1)}), bf16[4,512,384]{2,1,0:T(8,128)(2,1)S(1)}, u32[]{:S(2)}, u32[]{:S(2)}) async-start(bf16[4,512,384]{2,1,0:T(8,128)(2,1)} %bitcast.323), calls=%async_computation.2 | async-start | bytes 3145728 | tf_op jit(solution)/shard_map/all_to_all | solution.py:220
  285.7 4.4 %collective-permute-start.14 = (bf16[13,384]{1,0:T(8,128)(2,1)S(1)}, bf16[13,384]{1,0:T(8,128)(2,1)S(1)}, u32[]{:S(2)}, u32[]{:S(2)}) collective-permute-start(bf16[13,384]{1,0:T(8,128)(2,1)S(1)} %fusion.145), channel_id=1, source_target_pairs={{0,64},{4,68},{8,72},{12,76},{16,80},{20,84},{24,88},{28,92},{32,9... | collective-permute-start | bytes 29960 | tf_op jit(solution)/shard_map/ppermute | solution.py:70
  292.3 9.3 %all-to-all-done.2 = bf16[4,512,384]{2,1,0:T(8,128)(2,1)S(1)} async-done(((bf16[4,512,384]{2,1,0:T(8,128)(2,1)}), bf16[4,512,384]{2,1,0:T(8,128)(2,1)S(1)}, u32[]{:S(2)}, u32[]{:S(2)}) %all-to-all-start.2) | async-done | bytes 1572896 | tf_op jit(solution)/shard_map/all_to_all | solution.py:220
  323.8 3.7 %collective-permute-done.20 = bf16[104,384]{1,0:T(8,128)(2,1)S(1)} collective-permute-done((bf16[104,384]{1,0:T(8,128)(2,1)S(1)}, bf16[104,384]{1,0:T(8,128)(2,1)S(1)}, u32[]{:S(2)}, u32[]{:S(2)}) %collective-permute-start.20) | collective-permute-done | bytes 79904 | tf_op jit(solution)/shard_map/ppermute | solution.py:70
  328.3 7.3 %collective-permute-start.21 = (bf16[208,384]{1,0:T(8,128)(2,1)}, bf16[208,384]{1,0:T(8,128)(2,1)S(1)}, u32[]{:S(2)}, u32[]{:S(2)}) collective-permute-start(bf16[208,384]{1,0:T(8,128)(2,1)} %get-tuple-element.96), channel_id=1, source_target_pairs={{0,1},{1,0},{2,3},{3,2},{4,5},{5,4},{6,7},{7,6},{8,9},{9,8},{10,11... | collective-permute-start | bytes 479240 | tf_op jit(solution)/shard_map/ppermute | solution.py:70
  (202 shorter events, 108.6 us)
Async XLA Ops:
  0.7 10.7 %collective-permute-start = (bf16[512,384]{1,0:T(8,128)(2,1)}, bf16[512,384]{1,0:T(8,128)(2,1)S(1)}, u32[]{:S(2)}, u32[]{:S(2)}) collective-permute-start(bf16[512,384]{1,0:T(8,128)(2,1)} %param.15), channel_id=1, source_target_pairs={{0,2},{1,3},{2,0},{3,1},{4,6},{5,7},{6,4},{7,5},{8,10},{9,11},{10,... | collective-permute-start | bytes 1179656 | tf_op jit(solution)/shard_map/ppermute | solution.py:70
  13.8 3.8 %collective-permute-start.1 = (bf16[1024,384]{1,0:T(8,128)(2,1)}, bf16[1024,384]{1,0:T(8,128)(2,1)S(1)}, u32[]{:S(2)}, u32[]{:S(2)}) collective-permute-start(bf16[1024,384]{1,0:T(8,128)(2,1)} %get-tuple-element.88), channel_id=1, source_target_pairs={{0,1},{1,0},{2,3},{3,2},{4,5},{5,4},{6,7},{7,6},{8,9},{9,8},{10,11... | collective-permute-start | bytes 2359304 | tf_op jit(solution)/shard_map/ppermute | solution.py:70
  25.1 68.3 %collective-permute-start.5 = (bf16[3,16,128,32]{2,1,3,0:T(8,128)(2,1)}, bf16[3,16,128,32]{2,1,3,0:T(8,128)(2,1)}, u32[]{:S(2)}, u32[]{:S(2)}) collective-permute-start(bf16[3,16,128,32]{2,1,3,0:T(8,128)(2,1)} %bitcast.27), channel_id=1, source_target_pairs={{4,0},{8,4},{12,8},{16,12},{20,16},{24,20},{28,24},{32,28},{36,32}... | collective-permute-start | bytes 1179656 | tf_op jit(solution)/shard_map/ppermute | solution.py:25
  34.0 59.4 %collective-permute-start.4 = (bf16[3,16,128,32]{2,1,3,0:T(8,128)(2,1)}, bf16[3,16,128,32]{2,1,3,0:T(8,128)(2,1)}, u32[]{:S(2)}, u32[]{:S(2)}) collective-permute-start(bf16[3,16,128,32]{2,1,3,0:T(8,128)(2,1)} %bitcast.27), channel_id=1, source_target_pairs={{0,4},{4,8},{8,12},{12,16},{16,20},{20,24},{24,28},{28,32},{32,36}... | collective-permute-start | bytes 1179656 | tf_op jit(solution)/shard_map/ppermute | solution.py:24
  35.8 23.4 %collective-permute-start.3 = (bf16[3,16,128,32]{2,1,3,0:T(8,128)(2,1)S(1)}, bf16[3,16,128,32]{2,1,3,0:T(8,128)(2,1)S(1)}, u32[]{:S(2)}, u32[]{:S(2)}) collective-permute-start(bf16[3,16,128,32]{2,1,3,0:T(8,128)(2,1)S(1)} %bitcast.325), channel_id=1, source_target_pairs={{4,0},{8,4},{12,8},{16,12},{20,16},{24,20},{28,24},{32,28},{36,32}... | collective-permute-start | bytes 1179656 | tf_op jit(solution)/shard_map/ppermute | solution.py:25
  43.0 25.5 %collective-permute-start.2 = (bf16[3,16,128,32]{2,1,3,0:T(8,128)(2,1)S(1)}, bf16[3,16,128,32]{2,1,3,0:T(8,128)(2,1)S(1)}, u32[]{:S(2)}, u32[]{:S(2)}) collective-permute-start(bf16[3,16,128,32]{2,1,3,0:T(8,128)(2,1)S(1)} %bitcast.326), channel_id=1, source_target_pairs={{0,4},{4,8},{8,12},{12,16},{16,20},{20,24},{24,28},{28,32},{32,36}... | collective-permute-start | bytes 1179656 | tf_op jit(solution)/shard_map/ppermute | solution.py:24
  73.2 40.1 %all-to-all-start.1 = ((bf16[512,4,96]{0,2,1:T(8,128)(2,1)}), bf16[512,4,96]{0,2,1:T(8,128)(2,1)}, u32[]{:S(2)}, u32[]{:S(2)}) async-start(bf16[512,4,96]{0,2,1:T(8,128)(2,1)} %bitcast.324), calls=%async_computation.1 | async-start | bytes 786432 | tf_op jit(solution)/shard_map/all_to_all | solution.py:182
  113.3 69.3 %all-to-all-start = ((bf16[4,512,96]{1,2,0:T(8,128)(2,1)}), bf16[4,512,96]{1,2,0:T(8,128)(2,1)}, u32[]{:S(2)}, u32[]{:S(2)}) async-start(bf16[4,512,96]{1,2,0:T(8,128)(2,1)} %copy.70), calls=%async_computation | async-start | bytes 786432 | tf_op jit(solution)/shard_map/all_to_all | solution.py:175
  205.2 25.1 %collective-permute-start.7 = (bf16[2,3,16,128,32]{3,2,4,1,0:T(8,128)(2,1)}, bf16[2,3,16,128,32]{3,2,4,1,0:T(8,128)(2,1)}, u32[]{:S(2)}, u32[]{:S(2)}) collective-permute-start(bf16[2,3,16,128,32]{3,2,4,1,0:T(8,128)(2,1)} %get-tuple-element.79), channel_id=1, source_target_pairs={{0,4},{4,8},{8,12},{12,16},{16,20},{20,24},{24,28},{28,32},{32,36}... | collective-permute-start | bytes 2359304 | tf_op jit(solution)/shard_map/ppermute | solution.py:33
  208.0 35.0 %collective-permute-start.6 = (bf16[2,3,16,128,32]{3,2,4,1,0:T(8,128)(2,1)}, bf16[2,3,16,128,32]{3,2,4,1,0:T(8,128)(2,1)}, u32[]{:S(2)}, u32[]{:S(2)}) collective-permute-start(bf16[2,3,16,128,32]{3,2,4,1,0:T(8,128)(2,1)} %get-tuple-element.78), channel_id=1, source_target_pairs={{0,124},{4,0},{8,4},{12,8},{16,12},{20,16},{24,20},{28,24},{32,28}... | collective-permute-start | bytes 2359304 | tf_op jit(solution)/shard_map/ppermute | solution.py:33
  261.9 3.7 %collective-permute-start.9 = (bf16[104,384]{1,0:T(8,128)(2,1)S(1)}, bf16[104,384]{1,0:T(8,128)(2,1)S(1)}, u32[]{:S(2)}, u32[]{:S(2)}) collective-permute-start(bf16[104,384]{1,0:T(8,128)(2,1)S(1)} %fusion.114), channel_id=1, source_target_pairs={{0,2},{1,3},{2,0},{3,1},{4,6},{5,7},{6,4},{7,5},{8,10},{9,11},{10,... | collective-permute-start | bytes 239624 | tf_op jit(solution)/shard_map/ppermute | solution.py:70
  265.8 6.0 %collective-permute-start.10 = (bf16[208,384]{1,0:T(8,128)(2,1)S(1)}, bf16[208,384]{1,0:T(8,128)(2,1)S(1)}, u32[]{:S(2)}, u32[]{:S(2)}) collective-permute-start(bf16[208,384]{1,0:T(8,128)(2,1)S(1)} %fusion.106), channel_id=1, source_target_pairs={{0,4},{4,0},{8,12},{12,8},{16,20},{20,16},{24,28},{28,24},{32,36},... | collective-permute-start | bytes 479240 | tf_op jit(solution)/shard_map/ppermute | solution.py:70
  271.9 3.3 collective-permute-start.11
  275.3 7.3 %collective-permute-start.12 = (bf16[52,384]{1,0:T(8,128)(2,1)S(1)}, bf16[52,384]{1,0:T(8,128)(2,1)S(1)}, u32[]{:S(2)}, u32[]{:S(2)}) collective-permute-start(bf16[52,384]{1,0:T(8,128)(2,1)S(1)} %fusion.129), channel_id=1, source_target_pairs={{0,16},{4,20},{8,24},{12,28},{16,0},{20,4},{24,8},{28,12},{32,48},... | collective-permute-start | bytes 119816 | tf_op jit(solution)/shard_map/ppermute | solution.py:70
  275.6 26.0 %all-to-all-start.2 = ((bf16[4,512,384]{2,1,0:T(8,128)(2,1)}), bf16[4,512,384]{2,1,0:T(8,128)(2,1)S(1)}, u32[]{:S(2)}, u32[]{:S(2)}) async-start(bf16[4,512,384]{2,1,0:T(8,128)(2,1)} %bitcast.323), calls=%async_computation.2 | async-start | bytes 3145728 | tf_op jit(solution)/shard_map/all_to_all | solution.py:220
  282.6 3.1 collective-permute-start.13
  285.7 6.6 %collective-permute-start.14 = (bf16[13,384]{1,0:T(8,128)(2,1)S(1)}, bf16[13,384]{1,0:T(8,128)(2,1)S(1)}, u32[]{:S(2)}, u32[]{:S(2)}) collective-permute-start(bf16[13,384]{1,0:T(8,128)(2,1)S(1)} %fusion.145), channel_id=1, source_target_pairs={{0,64},{4,68},{8,72},{12,76},{16,80},{20,84},{24,88},{28,92},{32,9... | collective-permute-start | bytes 29960 | tf_op jit(solution)/shard_map/ppermute | solution.py:70
  301.6 4.3 %collective-permute-start.15 = (bf16[13,384]{1,0:T(8,128)(2,1)S(1)}, bf16[13,384]{1,0:T(8,128)(2,1)S(1)}, u32[]{:S(2)}, u32[]{:S(2)}) collective-permute-start(bf16[13,384]{1,0:T(8,128)(2,1)S(1)} %bitcast_add_fusion.6), channel_id=1, source_target_pairs={{0,64},{4,68},{8,72},{12,76},{16,80},{20,84},{24,88},{28,92},{32,9... | collective-permute-start | bytes 29960 | tf_op jit(solution)/shard_map/ppermute | solution.py:70
  305.9 3.3 collective-permute-start.16
  309.3 4.6 %collective-permute-start.17 = (bf16[52,384]{1,0:T(8,128)(2,1)S(1)}, bf16[52,384]{1,0:T(8,128)(2,1)S(1)}, u32[]{:S(2)}, u32[]{:S(2)}) collective-permute-start(bf16[52,384]{1,0:T(8,128)(2,1)S(1)} %pad_maximum_fusion.9), channel_id=1, source_target_pairs={{0,16},{4,20},{8,24},{12,28},{16,0},{20,4},{24,8},{28,12},{32,48},... | collective-permute-start | bytes 119816 | tf_op jit(solution)/shard_map/ppermute | solution.py:70
  314.0 3.4 collective-permute-start.18
  317.5 5.7 %collective-permute-start.19 = (bf16[208,384]{1,0:T(8,128)(2,1)S(1)}, bf16[208,384]{1,0:T(8,128)(2,1)S(1)}, u32[]{:S(2)}, u32[]{:S(2)}) collective-permute-start(bf16[208,384]{1,0:T(8,128)(2,1)S(1)} %get-tuple-element.102), channel_id=1, source_target_pairs={{0,4},{4,0},{8,12},{12,8},{16,20},{20,16},{24,28},{28,24},{32,36},... | collective-permute-start | bytes 479240 | tf_op jit(solution)/shard_map/ppermute | solution.py:70
  323.3 4.2 %collective-permute-start.20 = (bf16[104,384]{1,0:T(8,128)(2,1)S(1)}, bf16[104,384]{1,0:T(8,128)(2,1)S(1)}, u32[]{:S(2)}, u32[]{:S(2)}) collective-permute-start(bf16[104,384]{1,0:T(8,128)(2,1)S(1)} %get-tuple-element.100), channel_id=1, source_target_pairs={{0,2},{1,3},{2,0},{3,1},{4,6},{5,7},{6,4},{7,5},{8,10},{9,11},{10,... | collective-permute-start | bytes 239624 | tf_op jit(solution)/shard_map/ppermute | solution.py:70
  328.3 9.6 %collective-permute-start.21 = (bf16[208,384]{1,0:T(8,128)(2,1)}, bf16[208,384]{1,0:T(8,128)(2,1)S(1)}, u32[]{:S(2)}, u32[]{:S(2)}) collective-permute-start(bf16[208,384]{1,0:T(8,128)(2,1)} %get-tuple-element.96), channel_id=1, source_target_pairs={{0,1},{1,0},{2,3},{3,2},{4,5},{5,4},{6,7},{7,6},{8,9},{9,8},{10,11... | collective-permute-start | bytes 479240 | tf_op jit(solution)/shard_map/ppermute | solution.py:70
  (34 other events, 347.4 us)

commit v9 on v8

--- a/solution.py
+++ b/solution.py
@@ -221,7 +221,6 @@
     narrow = d_qkv_part.reshape(-1, width)
     both = pad_rows(jnp.concatenate([narrow, wide_part], 0), n_slab)
     both_part, slab_bits = scatter_steps(both, slab_steps, bf16)
-    both_part, received = lax.optimization_barrier((both_part, received))
     both = gather_steps(both_part.astype(bf16), slab_steps, slab_bits)
     narrow_rows = narrow.shape[0]
     wide_part = both[narrow_rows : narrow_rows + wide_part.shape[0]]

time: 347 us -> 357 us (1.029)
  waiting for transfers between devices: 81.2 us -> 95.8 us
  starting transfers between devices: 71.8 us -> 64.2 us
    ppermute x16, waiting for transfers between devices: 33.4 us -> 57.4 us  [xor_swap(): return lax.ppermute(value, axis, [(i, i ^ mask) for i in range(size)])]
    ppermute x16, starting transfers between devices: 31.4 us -> 16.8 us  [xor_swap(): return lax.ppermute(value, axis, [(i, i ^ mask) for i in range(size)])]
    all_to_all x1, waiting for transfers between devices: 9.35 us -> 0.01 us  [local(): lax.all_to_all(shares, 'head', split_axis=0, concat_axis=0, tiled=True)]
    all_to_all x1, starting transfers between devices: 6.96 us -> 13.9 us  [local(): lax.all_to_all(shares, 'head', split_axis=0, concat_axis=0, tiled=True)]
where the time goes in v9:
time: 357 us; the launch traced here: 350 us
  matrix products  109 us (31%)
  waiting for transfers between devices  95.8 us (27%)
  starting transfers between devices  64.2 us (18%)
  other arithmetic  44.4 us (12%)
  local copies, waits for them, and re-layouts  34.9 us (10%)
    ppermute x16, waiting for transfers between devices, xor_swap(): return lax.ppermute(value, axis, [(i, i ^ mask) for i in range(size)])  57.4 us
    convert_element_type x1, other arithmetic, local(): d_scores = (exponent_divisor * weights * (d_weights - row_dot)).astype(bf16)  22.8 us
    dot_general x1, matrix products, local(): jnp.einsum('hbqd,hbskd->hbqsk', d_attn, values, preferred_element_type=f32)  19.4 us
    ppermute x16, starting transfers between devices, xor_swap(): return lax.ppermute(value, axis, [(i, i ^ mask) for i in range(size)])  16.8 us
    ppermute x2, starting transfers between devices, padded(): after = lax.ppermute(first, axis, down)  16.2 us
    ppermute x2, waiting for transfers between devices, padded(): after = lax.ppermute(first, axis, down)  15.2 us
    dot_general x1, matrix products, local(): jnp.einsum('hbqd,hbskd->hbqsk', q_heads, keys, preferred_element_type=f32)  14.4 us
    all_to_all x1, starting transfers between devices, local(): lax.all_to_all(shares, 'head', split_axis=0, concat_axis=0, tiled=True)  13.9 us
  transfers between devices with their start and end apart: 25, of which 18 were waited for; matrix products, arithmetic and copies ran while one was open for 38% of the time, Pallas kernels for 0%

profile of v9, /device:TPU:1, one launch (start us, length us, event | category | flops | bytes accessed | tf_op | source)
XLA Modules:
  0.0 350.4 jit_solution(16327404783492998627)
XLA Ops:
  2.8 8.6 %collective-permute-done = bf16[512,384]{1,0:T(8,128)(2,1)S(1)} collective-permute-done((bf16[512,384]{1,0:T(8,128)(2,1)}, bf16[512,384]{1,0:T(8,128)(2,1)S(1)}, u32[]{:S(2)}, u32[]{:S(2)}) %collective-permute-start) | collective-permute-done | bytes 393248 | tf_op jit(solution)/shard_map/ppermute | solution.py:70
  25.1 8.9 %collective-permute-start.5 = (bf16[3,16,128,32]{2,1,3,0:T(8,128)(2,1)}, bf16[3,16,128,32]{2,1,3,0:T(8,128)(2,1)}, u32[]{:S(2)}, u32[]{:S(2)}) collective-permute-start(bf16[3,16,128,32]{2,1,3,0:T(8,128)(2,1)} %bitcast.27), channel_id=1, source_target_pairs={{4,0},{8,4},{12,8},{16,12},{20,16},{24,20},{28,24},{32,28},{36,32}... | collective-permute-start | bytes 1179656 | tf_op jit(solution)/shard_map/ppermute | solution.py:25
  35.8 7.3 %collective-permute-start.3 = (bf16[3,16,128,32]{2,1,3,0:T(8,128)(2,1)S(1)}, bf16[3,16,128,32]{2,1,3,0:T(8,128)(2,1)S(1)}, u32[]{:S(2)}, u32[]{:S(2)}) collective-permute-start(bf16[3,16,128,32]{2,1,3,0:T(8,128)(2,1)S(1)} %bitcast.327), channel_id=1, source_target_pairs={{4,0},{8,4},{12,8},{16,12},{20,16},{24,20},{28,24},{32,28},{36,32}... | collective-permute-start | bytes 1179656 | tf_op jit(solution)/shard_map/ppermute | solution.py:25
  43.9 15.2 %collective-permute-done.3 = bf16[3,16,128,32]{2,1,3,0:T(8,128)(2,1)S(1)} collective-permute-done((bf16[3,16,128,32]{2,1,3,0:T(8,128)(2,1)S(1)}, bf16[3,16,128,32]{2,1,3,0:T(8,128)(2,1)S(1)}, u32[]{:S(2)}, u32[]{:S(2)}) %collective-permute-start.3) | collective-permute-done | bytes 393248 | tf_op jit(solution)/shard_map/ppermute | solution.py:25
  59.2 9.4 %collective-permute-done.2 = bf16[3,16,128,32]{2,1,3,0:T(8,128)(2,1)S(1)} collective-permute-done((bf16[3,16,128,32]{2,1,3,0:T(8,128)(2,1)S(1)}, bf16[3,16,128,32]{2,1,3,0:T(8,128)(2,1)S(1)}, u32[]{:S(2)}, u32[]{:S(2)}) %collective-permute-start.2) | collective-permute-done | bytes 393248 | tf_op jit(solution)/shard_map/ppermute | solution.py:24
  73.2 5.8 %all-to-all-start.1 = ((bf16[512,4,96]{0,2,1:T(8,128)(2,1)}), bf16[512,4,96]{0,2,1:T(8,128)(2,1)}, u32[]{:S(2)}, u32[]{:S(2)}) async-start(bf16[512,4,96]{0,2,1:T(8,128)(2,1)} %bitcast.326), calls=%async_computation.1 | async-start | bytes 786432 | tf_op jit(solution)/shard_map/all_to_all | solution.py:182
  79.0 14.4 %fusion.3 = (f32[3,16,128]{2,1,0:T(8,128)S(1)}, f32[3,16,128,8,128]{2,4,3,1,0:T(8,128)}) fusion(f32[16,8]{1,0:T(8,128)S(1)} %fusion.151, bf16[3,16,8,128,32]{3,1,2,4,0:T(8,128)(2,1)} %convert_bitcast_fusion.1, bf16[16,128,3,32]{1,0,3,2:T(8,128)(2,1)} %bitcast.314), kind=kOutput, calls=%fused_computation.6 | convolution fusion | flops 421521408 | bytes 28729856 | tf_op jit(solution)/shard_map/hbqd,hbskd->hbqsk/dot_general | solution.py:166
  95.7 13.0 %fusion.57 = bf16[16,128,3,32]{1,3,0,2:T(8,128)(2,1)S(1)} fusion(bf16[3,16,8,128,32]{3,1,2,4,0:T(8,128)(2,1)S(1)} %convert_bitcast_fusion, f32[3,16,128,8,128]{2,4,3,1,0:T(8,128)} %get-tuple-element.113, f32[3,16,128]{2,1,0:T(8,128)S(1)} %get-tuple-element.112, f32[16,8]{1,0:T(8,128)S(1)} %fusion.151), kind=kOutput, calls=%fused_computation.62 | convolution fusion | flops 428015616 | bytes 28729856 | tf_op jit(solution)/shard_map/hbqsk,hbskd->hbqd/dot_general | solution.py:172
  113.3 4.3 %all-to-all-start = ((bf16[4,512,96]{1,2,0:T(8,128)(2,1)}), bf16[4,512,96]{1,2,0:T(8,128)(2,1)}, u32[]{:S(2)}, u32[]{:S(2)}) async-start(bf16[4,512,96]{1,2,0:T(8,128)(2,1)} %copy.70), calls=%async_computation | async-start | bytes 786432 | tf_op jit(solution)/shard_map/all_to_all | solution.py:175
  121.5 12.9 %fusion.8 = f32[3,16,8,128,32]{3,4,2,1,0:T(8,128)} fusion(bf16[16,128,3,32]{1,0,3,2:T(8,128)(2,1)} %reshape.290, f32[3,16,128,8,128]{2,4,3,1,0:T(8,128)} %get-tuple-element.113, f32[3,16,128]{2,1,0:T(8,128)S(1)} %get-tuple-element.112, f32[16,8]{1,0:T(8,128)S(1)} %fusion.151), kind=kOutput, calls=%fused_computation.11 | convolution fusion | flops 427819008 | bytes 31875584 | tf_op jit(solution)/shard_map/hbqsk,hbqd->hbskd/dot_general | solution.py:189
  134.4 19.4 %multiply_reduce_fusion = (f32[3,16,128]{2,1,0:T(8,128)S(1)}, f32[3,16,128,8,128]{2,4,3,1,0:T(8,128)}) fusion(f32[3,16,128]{2,1,0:T(8,128)S(1)} %get-tuple-element.112, f32[16,8]{1,0:T(8,128)S(1)} %fusion.151, f32[3,16,128,8,128]{2,4,3,1,0:T(8,128)} %get-tuple-element.113, bf16[3,16,8,128,32]{3,1,2,4,0:T(8,128)(2,1)} %copy-done.14, ...), kind=kOutput, calls=%fused_computation.3 | convolution fusion | flops 434104320 | bytes 53920256 | tf_op jit(solution)/shard_map/hbqd,hbskd->hbqsk/dot_general | solution.py:183
  153.8 22.8 %multiply_convert_fusion = bf16[3,16,128,8,128]{2,4,3,1,0:T(8,128)(2,1)} fusion(f32[3,16,128,8,128]{2,4,3,1,0:T(8,128)} %get-tuple-element.115, f32[3,16,128]{2,1,0:T(8,128)S(1)} %get-tuple-element.114, f32[3,16,128]{2,1,0:T(8,128)S(1)} %get-tuple-element.112, f32[16,8]{1,0:T(8,128)S(1)} %fusion.151, f32[3,16,128,8,128]{2,4,3,1,0:T(8,128)} %get-tuple-element.113), kind=kLoop, calls=%fused_computation.2 | loop fusion | flops 44040192 | bytes 62964224 | tf_op jit(solution)/shard_map/convert_element_type | solution.py:185
  176.6 6.1 %fusion.24 = f32[1,3,48,128,32]{3,2,4,1,0:T(8,128)} fusion(f32[3,16,8,128,32]{3,4,2,1,0:T(8,128)S(1)} %copy-done.9, s32[16,8]{0,1:T(8,128)S(1)} %add_select_fusion), kind=kOutput, calls=%fused_computation.41 | convolution fusion | flops 452990976 | bytes 8651264 | tf_op jit(solution)/shard_map/bse,hbskd->hekd/dot_general | solution.py:190
  182.6 11.7 %fusion.95 = f32[3,16,8,128,32]{3,4,2,1,0:T(8,128)} fusion(bf16[3,16,128,8,128]{2,4,3,1,0:T(8,128)(2,1)} %multiply_convert_fusion, bf16[16,128,3,32]{1,0,3,2:T(8,128)(2,1)} %bitcast.315), kind=kOutput, calls=%fused_computation.118 | convolution fusion | flops 402653184 | bytes 19267584 | tf_op jit(solution)/shard_map/hbqsk,hbqd->hbskd/dot_general | solution.py:188
  194.3 7.6 %fusion.21 = f32[1,3,48,128,32]{3,2,4,1,0:T(8,128)S(1)} fusion(f32[3,16,8,128,32]{3,4,2,1,0:T(8,128)} %fusion.95, s32[16,8]{0,1:T(8,128)S(1)} %add_select_fusion), kind=kOutput, calls=%fused_computation.40 | convolution fusion | flops 452990976 | bytes 8651264 | tf_op jit(solution)/shard_map/bse,hbskd->hekd/dot_general | solution.py:190
  208.0 4.5 %collective-permute-start.6 = (bf16[2,3,16,128,32]{3,2,4,1,0:T(8,128)(2,1)}, bf16[2,3,16,128,32]{3,2,4,1,0:T(8,128)(2,1)}, u32[]{:S(2)}, u32[]{:S(2)}) collective-permute-start(bf16[2,3,16,128,32]{3,2,4,1,0:T(8,128)(2,1)} %get-tuple-element.74), channel_id=1, source_target_pairs={{0,124},{4,0},{8,4},{12,8},{16,12},{20,16},{24,20},{28,24},{32,28}... | collective-permute-start | bytes 2359304 | tf_op jit(solution)/shard_map/ppermute | solution.py:33
  212.4 7.6 %fusion.51 = f32[3,16,128,32]{2,3,1,0:T(8,128)S(1)} fusion(bf16[3,16,128,8,128]{2,4,3,1,0:T(8,128)(2,1)} %multiply_convert_fusion, bf16[3,16,8,128,32]{3,1,2,4,0:T(8,128)(2,1)S(1)} %copy-done.1), kind=kOutput, calls=%fused_computation.60 | convolution fusion | flops 403046400 | bytes 16515072 | tf_op jit(solution)/shard_map/hbqsk,hbskd->hbqd/dot_general | solution.py:187
  230.3 12.7 %collective-permute-done.6 = bf16[2,3,16,128,32]{3,2,4,1,0:T(8,128)(2,1)} collective-permute-done((bf16[2,3,16,128,32]{3,2,4,1,0:T(8,128)(2,1)}, bf16[2,3,16,128,32]{3,2,4,1,0:T(8,128)(2,1)}, u32[]{:S(2)}, u32[]{:S(2)}) %collective-permute-start.6) | collective-permute-done | bytes 786464 | tf_op jit(solution)/shard_map/ppermute | solution.py:33
  265.9 5.9 %collective-permute-done.10 = bf16[208,384]{1,0:T(8,128)(2,1)S(1)} collective-permute-done((bf16[208,384]{1,0:T(8,128)(2,1)S(1)}, bf16[208,384]{1,0:T(8,128)(2,1)S(1)}, u32[]{:S(2)}, u32[]{:S(2)}) %collective-permute-start.10) | collective-permute-done | bytes 159776 | tf_op jit(solution)/shard_map/ppermute | solution.py:70
  272.0 3.2 collective-permute-done.11
  275.6 4.2 %collective-permute-done.12 = bf16[52,384]{1,0:T(8,128)(2,1)S(1)} collective-permute-done((bf16[52,384]{1,0:T(8,128)(2,1)S(1)}, bf16[52,384]{1,0:T(8,128)(2,1)S(1)}, u32[]{:S(2)}, u32[]{:S(2)}) %collective-permute-start.12) | collective-permute-done | bytes 39968 | tf_op jit(solution)/shard_map/ppermute | solution.py:70
  298.4 3.2 collective-permute-done.18
  304.2 13.9 %all-to-all-start.2 = ((bf16[4,512,384]{2,1,0:T(8,128)(2,1)}), bf16[4,512,384]{2,1,0:T(8,128)(2,1)S(1)}, u32[]{:S(2)}, u32[]{:S(2)}) async-start(bf16[4,512,384]{2,1,0:T(8,128)(2,1)} %bitcast.325), calls=%async_computation.2 | async-start | bytes 3145728 | tf_op jit(solution)/shard_map/all_to_all | solution.py:220
  319.8 19.1 %collective-permute-done.20 = bf16[104,384]{1,0:T(8,128)(2,1)S(1)} collective-permute-done((bf16[104,384]{1,0:T(8,128)(2,1)S(1)}, bf16[104,384]{1,0:T(8,128)(2,1)S(1)}, u32[]{:S(2)}, u32[]{:S(2)}) %collective-permute-start.20) | collective-permute-done | bytes 79904 | tf_op jit(solution)/shard_map/ppermute | solution.py:70
  (202 shorter events, 107.0 us)
Async XLA Ops:
  0.7 10.7 %collective-permute-start = (bf16[512,384]{1,0:T(8,128)(2,1)}, bf16[512,384]{1,0:T(8,128)(2,1)S(1)}, u32[]{:S(2)}, u32[]{:S(2)}) collective-permute-start(bf16[512,384]{1,0:T(8,128)(2,1)} %param.15), channel_id=1, source_target_pairs={{0,2},{1,3},{2,0},{3,1},{4,6},{5,7},{6,4},{7,5},{8,10},{9,11},{10,... | collective-permute-start | bytes 1179656 | tf_op jit(solution)/shard_map/ppermute | solution.py:70
  13.8 3.8 %collective-permute-start.1 = (bf16[1024,384]{1,0:T(8,128)(2,1)}, bf16[1024,384]{1,0:T(8,128)(2,1)S(1)}, u32[]{:S(2)}, u32[]{:S(2)}) collective-permute-start(bf16[1024,384]{1,0:T(8,128)(2,1)} %get-tuple-element.84), channel_id=1, source_target_pairs={{0,1},{1,0},{2,3},{3,2},{4,5},{5,4},{6,7},{7,6},{8,9},{9,8},{10,11... | collective-permute-start | bytes 2359304 | tf_op jit(solution)/shard_map/ppermute | solution.py:70
  25.1 68.3 %collective-permute-start.5 = (bf16[3,16,128,32]{2,1,3,0:T(8,128)(2,1)}, bf16[3,16,128,32]{2,1,3,0:T(8,128)(2,1)}, u32[]{:S(2)}, u32[]{:S(2)}) collective-permute-start(bf16[3,16,128,32]{2,1,3,0:T(8,128)(2,1)} %bitcast.27), channel_id=1, source_target_pairs={{4,0},{8,4},{12,8},{16,12},{20,16},{24,20},{28,24},{32,28},{36,32}... | collective-permute-start | bytes 1179656 | tf_op jit(solution)/shard_map/ppermute | solution.py:25
  34.0 59.4 %collective-permute-start.4 = (bf16[3,16,128,32]{2,1,3,0:T(8,128)(2,1)}, bf16[3,16,128,32]{2,1,3,0:T(8,128)(2,1)}, u32[]{:S(2)}, u32[]{:S(2)}) collective-permute-start(bf16[3,16,128,32]{2,1,3,0:T(8,128)(2,1)} %bitcast.27), channel_id=1, source_target_pairs={{0,4},{4,8},{8,12},{12,16},{16,20},{20,24},{24,28},{28,32},{32,36}... | collective-permute-start | bytes 1179656 | tf_op jit(solution)/shard_map/ppermute | solution.py:24
  35.8 23.4 %collective-permute-start.3 = (bf16[3,16,128,32]{2,1,3,0:T(8,128)(2,1)S(1)}, bf16[3,16,128,32]{2,1,3,0:T(8,128)(2,1)S(1)}, u32[]{:S(2)}, u32[]{:S(2)}) collective-permute-start(bf16[3,16,128,32]{2,1,3,0:T(8,128)(2,1)S(1)} %bitcast.327), channel_id=1, source_target_pairs={{4,0},{8,4},{12,8},{16,12},{20,16},{24,20},{28,24},{32,28},{36,32}... | collective-permute-start | bytes 1179656 | tf_op jit(solution)/shard_map/ppermute | solution.py:25
  43.0 25.5 %collective-permute-start.2 = (bf16[3,16,128,32]{2,1,3,0:T(8,128)(2,1)S(1)}, bf16[3,16,128,32]{2,1,3,0:T(8,128)(2,1)S(1)}, u32[]{:S(2)}, u32[]{:S(2)}) collective-permute-start(bf16[3,16,128,32]{2,1,3,0:T(8,128)(2,1)S(1)} %bitcast.328), channel_id=1, source_target_pairs={{0,4},{4,8},{8,12},{12,16},{16,20},{20,24},{24,28},{28,32},{32,36}... | collective-permute-start | bytes 1179656 | tf_op jit(solution)/shard_map/ppermute | solution.py:24
  73.2 40.1 %all-to-all-start.1 = ((bf16[512,4,96]{0,2,1:T(8,128)(2,1)}), bf16[512,4,96]{0,2,1:T(8,128)(2,1)}, u32[]{:S(2)}, u32[]{:S(2)}) async-start(bf16[512,4,96]{0,2,1:T(8,128)(2,1)} %bitcast.326), calls=%async_computation.1 | async-start | bytes 786432 | tf_op jit(solution)/shard_map/all_to_all | solution.py:182
  113.3 69.3 %all-to-all-start = ((bf16[4,512,96]{1,2,0:T(8,128)(2,1)}), bf16[4,512,96]{1,2,0:T(8,128)(2,1)}, u32[]{:S(2)}, u32[]{:S(2)}) async-start(bf16[4,512,96]{1,2,0:T(8,128)(2,1)} %copy.70), calls=%async_computation | async-start | bytes 786432 | tf_op jit(solution)/shard_map/all_to_all | solution.py:175
  205.2 25.1 %collective-permute-start.7 = (bf16[2,3,16,128,32]{3,2,4,1,0:T(8,128)(2,1)}, bf16[2,3,16,128,32]{3,2,4,1,0:T(8,128)(2,1)}, u32[]{:S(2)}, u32[]{:S(2)}) collective-permute-start(bf16[2,3,16,128,32]{3,2,4,1,0:T(8,128)(2,1)} %get-tuple-element.75), channel_id=1, source_target_pairs={{0,4},{4,8},{8,12},{12,16},{16,20},{20,24},{24,28},{28,32},{32,36}... | collective-permute-start | bytes 2359304 | tf_op jit(solution)/shard_map/ppermute | solution.py:33
  208.0 35.0 %collective-permute-start.6 = (bf16[2,3,16,128,32]{3,2,4,1,0:T(8,128)(2,1)}, bf16[2,3,16,128,32]{3,2,4,1,0:T(8,128)(2,1)}, u32[]{:S(2)}, u32[]{:S(2)}) collective-permute-start(bf16[2,3,16,128,32]{3,2,4,1,0:T(8,128)(2,1)} %get-tuple-element.74), channel_id=1, source_target_pairs={{0,124},{4,0},{8,4},{12,8},{16,12},{20,16},{24,20},{28,24},{32,28}... | collective-permute-start | bytes 2359304 | tf_op jit(solution)/shard_map/ppermute | solution.py:33
  261.9 3.7 %collective-permute-start.9 = (bf16[104,384]{1,0:T(8,128)(2,1)S(1)}, bf16[104,384]{1,0:T(8,128)(2,1)S(1)}, u32[]{:S(2)}, u32[]{:S(2)}) collective-permute-start(bf16[104,384]{1,0:T(8,128)(2,1)S(1)} %fusion.114), channel_id=1, source_target_pairs={{0,2},{1,3},{2,0},{3,1},{4,6},{5,7},{6,4},{7,5},{8,10},{9,11},{10,... | collective-permute-start | bytes 239624 | tf_op jit(solution)/shard_map/ppermute | solution.py:70
  265.7 6.0 %collective-permute-start.10 = (bf16[208,384]{1,0:T(8,128)(2,1)S(1)}, bf16[208,384]{1,0:T(8,128)(2,1)S(1)}, u32[]{:S(2)}, u32[]{:S(2)}) collective-permute-start(bf16[208,384]{1,0:T(8,128)(2,1)S(1)} %fusion.106), channel_id=1, source_target_pairs={{0,4},{4,0},{8,12},{12,8},{16,20},{20,16},{24,28},{28,24},{32,36},... | collective-permute-start | bytes 479240 | tf_op jit(solution)/shard_map/ppermute | solution.py:70
  271.8 3.3 collective-permute-start.11
  275.3 4.5 %collective-permute-start.12 = (bf16[52,384]{1,0:T(8,128)(2,1)S(1)}, bf16[52,384]{1,0:T(8,128)(2,1)S(1)}, u32[]{:S(2)}, u32[]{:S(2)}) collective-permute-start(bf16[52,384]{1,0:T(8,128)(2,1)S(1)} %fusion.129), channel_id=1, source_target_pairs={{0,16},{4,20},{8,24},{12,28},{16,0},{20,4},{24,8},{28,12},{32,48},... | collective-permute-start | bytes 119816 | tf_op jit(solution)/shard_map/ppermute | solution.py:70
  279.8 2.8 collective-permute-start.13
  282.6 4.1 %collective-permute-start.14 = (bf16[13,384]{1,0:T(8,128)(2,1)S(1)}, bf16[13,384]{1,0:T(8,128)(2,1)S(1)}, u32[]{:S(2)}, u32[]{:S(2)}) collective-permute-start(bf16[13,384]{1,0:T(8,128)(2,1)S(1)} %fusion.146), channel_id=1, source_target_pairs={{0,64},{4,68},{8,72},{12,76},{16,80},{20,84},{24,88},{28,92},{32,9... | collective-permute-start | bytes 29960 | tf_op jit(solution)/shard_map/ppermute | solution.py:70
  286.7 4.1 %collective-permute-start.15 = (bf16[13,384]{1,0:T(8,128)(2,1)S(1)}, bf16[13,384]{1,0:T(8,128)(2,1)S(1)}, u32[]{:S(2)}, u32[]{:S(2)}) collective-permute-start(bf16[13,384]{1,0:T(8,128)(2,1)S(1)} %fusion.143), channel_id=1, source_target_pairs={{0,64},{4,68},{8,72},{12,76},{16,80},{20,84},{24,88},{28,92},{32,9... | collective-permute-start | bytes 29960 | tf_op jit(solution)/shard_map/ppermute | solution.py:70
  290.9 2.8 collective-permute-start.16
  293.7 4.5 %collective-permute-start.17 = (bf16[52,384]{1,0:T(8,128)(2,1)S(1)}, bf16[52,384]{1,0:T(8,128)(2,1)S(1)}, u32[]{:S(2)}, u32[]{:S(2)}) collective-permute-start(bf16[52,384]{1,0:T(8,128)(2,1)S(1)} %pad_maximum_fusion.9), channel_id=1, source_target_pairs={{0,16},{4,20},{8,24},{12,28},{16,0},{20,4},{24,8},{28,12},{32,48},... | collective-permute-start | bytes 119816 | tf_op jit(solution)/shard_map/ppermute | solution.py:70
  298.3 3.3 collective-permute-start.18
  302.4 15.7 %collective-permute-start.19 = (bf16[208,384]{1,0:T(8,128)(2,1)}, bf16[208,384]{1,0:T(8,128)(2,1)S(1)}, u32[]{:S(2)}, u32[]{:S(2)}) collective-permute-start(bf16[208,384]{1,0:T(8,128)(2,1)} %get-tuple-element.98), channel_id=1, source_target_pairs={{0,4},{4,0},{8,12},{12,8},{16,20},{20,16},{24,28},{28,24},{32,36},... | collective-permute-start | bytes 479240 | tf_op jit(solution)/shard_map/ppermute | solution.py:70
  304.2 44.3 %all-to-all-start.2 = ((bf16[4,512,384]{2,1,0:T(8,128)(2,1)}), bf16[4,512,384]{2,1,0:T(8,128)(2,1)S(1)}, u32[]{:S(2)}, u32[]{:S(2)}) async-start(bf16[4,512,384]{2,1,0:T(8,128)(2,1)} %bitcast.325), calls=%async_computation.2 | async-start | bytes 3145728 | tf_op jit(solution)/shard_map/all_to_all | solution.py:220
  318.3 20.6 %collective-permute-start.20 = (bf16[104,384]{1,0:T(8,128)(2,1)S(1)}, bf16[104,384]{1,0:T(8,128)(2,1)S(1)}, u32[]{:S(2)}, u32[]{:S(2)}) collective-permute-start(bf16[104,384]{1,0:T(8,128)(2,1)S(1)} %get-tuple-element.96), channel_id=1, source_target_pairs={{0,2},{1,3},{2,0},{3,1},{4,6},{5,7},{6,4},{7,5},{8,10},{9,11},{10,... | collective-permute-start | bytes 239624 | tf_op jit(solution)/shard_map/ppermute | solution.py:70
  339.7 6.2 %collective-permute-start.21 = (bf16[208,384]{1,0:T(8,128)(2,1)}, bf16[208,384]{1,0:T(8,128)(2,1)}, u32[]{:S(2)}, u32[]{:S(2)}) collective-permute-start(bf16[208,384]{1,0:T(8,128)(2,1)} %get-tuple-element.92), channel_id=1, source_target_pairs={{0,1},{1,0},{2,3},{3,2},{4,5},{5,4},{6,7},{7,6},{8,9},{9,8},{10,11... | collective-permute-start | bytes 479240 | tf_op jit(solution)/shard_map/ppermute | solution.py:70
  (34 other events, 329.8 us)

commit v10 on v7

--- a/solution.py
+++ b/solution.py
@@ -190,7 +190,7 @@
         "bse,hbskd->hekd",
         choose.astype(f32),
         grads,
-        precision=lax.Precision.HIGH,
+        precision=lax.Precision.DEFAULT,
         preferred_element_type=f32,
     )
     grad_ext = jnp.stack([scatter(d_keys), scatter(d_values)])

time: 338 us -> 330 us (0.976)
  matrix products: 107 us -> 99.8 us
    dot_general x2, matrix products: 12.1 us -> 6.11 us  [local(): jnp.einsum('bse,hbskd->hekd', choose.astype(f32), grads, precision=lax.Pr...]
where the time goes in v10:
time: 330 us; the launch traced here: 323 us
  waiting for transfers between devices  107 us (32%)
  matrix products  99.8 us (30%)
  starting transfers between devices  51.7 us (16%)
  other arithmetic  39.5 us (12%)
  local copies, waits for them, and re-layouts  23.3 us (7%)
    ppermute x16, waiting for transfers between devices, xor_swap(): return lax.ppermute(value, axis, [(i, i ^ mask) for i in range(size)])  61 us
    convert_element_type x1, other arithmetic, local(): d_scores = (exponent_divisor * weights * (d_weights - row_dot)).astype(bf16)  23 us
    ppermute x2, waiting for transfers between devices, passed_along(): return lax.ppermute(value, axis, pairs)  19.6 us
    dot_general x1, matrix products, local(): jnp.einsum('hbqd,hbskd->hbqsk', d_attn, values, preferred_element_type=f32)  19.3 us
    ppermute x2, waiting for transfers between devices, padded(): after = lax.ppermute(first, axis, down)  18 us
    ppermute x16, starting transfers between devices, xor_swap(): return lax.ppermute(value, axis, [(i, i ^ mask) for i in range(size)])  17.5 us
    dot_general x1, matrix products, local(): jnp.einsum('hbqd,hbskd->hbqsk', q_heads, keys, preferred_element_type=f32)  14.5 us
    dot_general x1, matrix products, local(): jnp.einsum('hbqsk,hbskd->hbqd', weights_bf, values, preferred_element_typ...  13 us
  transfers between devices with their start and end apart: 25, of which 17 were waited for; matrix products, arithmetic and copies ran while one was open for 37% of the time, Pallas kernels for 0%

profile of v10, /device:TPU:89, one launch (start us, length us, event | category | flops | bytes accessed | tf_op | source)
XLA Modules:
  0.0 323.3 jit_solution(11240145444899486756)
XLA Ops:
  7.8 16.6 %collective-permute-done.1 = bf16[1024,384]{1,0:T(8,128)(2,1)S(1)} collective-permute-done((bf16[1024,384]{1,0:T(8,128)(2,1)}, bf16[1024,384]{1,0:T(8,128)(2,1)S(1)}, u32[]{:S(2)}, u32[]{:S(2)}) %collective-permute-start.1) | collective-permute-done | bytes 786464 | tf_op jit(solution)/shard_map/ppermute | solution.py:70
  30.7 3.9 %collective-permute-start.3 = (bf16[3,16,128,32]{2,1,3,0:T(8,128)(2,1)S(1)}, bf16[3,16,128,32]{2,1,3,0:T(8,128)(2,1)S(1)}, u32[]{:S(2)}, u32[]{:S(2)}) collective-permute-start(bf16[3,16,128,32]{2,1,3,0:T(8,128)(2,1)S(1)} %bitcast.311), channel_id=1, source_target_pairs={{4,0},{8,4},{12,8},{16,12},{20,16},{24,20},{28,24},{32,28},{36,32}... | collective-permute-start | bytes 1179656 | tf_op jit(solution)/shard_map/ppermute | solution.py:25
  36.8 18.0 %collective-permute-done.3 = bf16[3,16,128,32]{2,1,3,0:T(8,128)(2,1)S(1)} collective-permute-done((bf16[3,16,128,32]{2,1,3,0:T(8,128)(2,1)S(1)}, bf16[3,16,128,32]{2,1,3,0:T(8,128)(2,1)S(1)}, u32[]{:S(2)}, u32[]{:S(2)}) %collective-permute-start.3) | collective-permute-done | bytes 393248 | tf_op jit(solution)/shard_map/ppermute | solution.py:25
  54.8 8.6 %collective-permute-done.2 = bf16[3,16,128,32]{2,1,3,0:T(8,128)(2,1)S(1)} collective-permute-done((bf16[3,16,128,32]{2,1,3,0:T(8,128)(2,1)S(1)}, bf16[3,16,128,32]{2,1,3,0:T(8,128)(2,1)S(1)}, u32[]{:S(2)}, u32[]{:S(2)}) %collective-permute-start.2) | collective-permute-done | bytes 393248 | tf_op jit(solution)/shard_map/ppermute | solution.py:24
  67.0 5.7 %all-to-all-start.1 = ((bf16[512,4,96]{0,2,1:T(8,128)(2,1)}), bf16[512,4,96]{0,2,1:T(8,128)(2,1)S(1)}, u32[]{:S(2)}, u32[]{:S(2)}) async-start(bf16[512,4,96]{0,2,1:T(8,128)(2,1)} %bitcast.34), calls=%async_computation.1 | async-start | bytes 786432 | tf_op jit(solution)/shard_map/all_to_all | solution.py:181
  72.8 14.5 %fusion.3 = (f32[3,16,128]{2,1,0:T(8,128)S(1)}, f32[3,16,128,8,128]{2,4,3,1,0:T(8,128)}) fusion(f32[16,8]{1,0:T(8,128)S(1)} %fusion.152, bf16[3,16,8,128,32]{3,1,2,4,0:T(8,128)(2,1)} %convert_bitcast_fusion.1, bf16[16,128,3,32]{1,0,3,2:T(8,128)(2,1)S(1)} %bitcast.295), kind=kOutput, calls=%fused_computation.6 | convolution fusion | flops 421521408 | bytes 28729856 | tf_op jit(solution)/shard_map/hbqd,hbskd->hbqsk/dot_general | solution.py:165
  88.3 13.0 %fusion.56 = bf16[16,128,3,32]{1,3,0,2:T(8,128)(2,1)S(1)} fusion(bf16[3,16,8,128,32]{3,1,2,4,0:T(8,128)(2,1)S(1)} %convert_bitcast_fusion, f32[3,16,128,8,128]{2,4,3,1,0:T(8,128)} %get-tuple-element.110, f32[3,16,128]{2,1,0:T(8,128)S(1)} %get-tuple-element.109, f32[16,8]{1,0:T(8,128)S(1)} %fusion.152), kind=kOutput, calls=%fused_computation.62 | convolution fusion | flops 428015616 | bytes 28729856 | tf_op jit(solution)/shard_map/hbqsk,hbskd->hbqd/dot_general | solution.py:171
  102.5 4.4 %all-to-all-start = ((bf16[4,512,96]{1,2,0:T(8,128)(2,1)}), bf16[4,512,96]{1,2,0:T(8,128)(2,1)}, u32[]{:S(2)}, u32[]{:S(2)}) async-start(bf16[4,512,96]{1,2,0:T(8,128)(2,1)} %copy.44), calls=%async_computation | async-start | bytes 786432 | tf_op jit(solution)/shard_map/all_to_all | solution.py:174
  107.4 11.9 %fusion.8 = bf16[3,16,8,128,32]{3,4,2,1,0:T(8,128)(2,1)} fusion(bf16[16,128,3,32]{1,0,3,2:T(8,128)(2,1)S(1)} %reshape.271, f32[3,16,128,8,128]{2,4,3,1,0:T(8,128)} %get-tuple-element.110, f32[3,16,128]{2,1,0:T(8,128)S(1)} %get-tuple-element.109, f32[16,8]{1,0:T(8,128)S(1)} %fusion.152), kind=kOutput, calls=%fused_computation.11 | convolution fusion | flops 427819008 | bytes 28729856 | tf_op jit(solution)/shard_map/hbqsk,hbqd->hbskd/dot_general | solution.py:188
  119.3 19.3 %multiply_reduce_fusion = (f32[3,16,128]{2,1,0:T(8,128)S(1)}, f32[3,16,128,8,128]{2,4,3,1,0:T(8,128)}) fusion(f32[3,16,128]{2,1,0:T(8,128)S(1)} %get-tuple-element.109, f32[16,8]{1,0:T(8,128)S(1)} %fusion.152, f32[3,16,128,8,128]{2,4,3,1,0:T(8,128)} %get-tuple-element.110, bf16[3,16,8,128,32]{3,1,2,4,0:T(8,128)(2,1)} %copy-done.13, ...), kind=kOutput, calls=%fused_computation.3 | convolution fusion | flops 434104320 | bytes 53920256 | tf_op jit(solution)/shard_map/hbqd,hbskd->hbqsk/dot_general | solution.py:182
  138.6 23.0 %multiply_convert_fusion = bf16[3,16,128,8,128]{2,4,3,1,0:T(8,128)(2,1)} fusion(f32[3,16,128,8,128]{2,4,3,1,0:T(8,128)} %get-tuple-element.112, f32[3,16,128]{2,1,0:T(8,128)S(1)} %get-tuple-element.111, f32[3,16,128]{2,1,0:T(8,128)S(1)} %get-tuple-element.109, f32[16,8]{1,0:T(8,128)S(1)} %fusion.152, f32[3,16,128,8,128]{2,4,3,1,0:T(8,128)} %get-tuple-element.110), kind=kLoop, calls=%fused_computation.2 | loop fusion | flops 44040192 | bytes 62964224 | tf_op jit(solution)/shard_map/convert_element_type | solution.py:184
  163.7 10.6 %fusion.96 = bf16[3,16,8,128,32]{3,4,2,1,0:T(8,128)(2,1)} fusion(bf16[3,16,128,8,128]{2,4,3,1,0:T(8,128)(2,1)} %multiply_convert_fusion, bf16[16,128,3,32]{1,0,3,2:T(8,128)(2,1)} %bitcast.296), kind=kOutput, calls=%fused_computation.118 | convolution fusion | flops 402653184 | bytes 16121856 | tf_op jit(solution)/shard_map/hbqsk,hbqd->hbskd/dot_general | solution.py:187
  174.4 4.0 %fusion.25 = f32[1,3,48,128,32]{3,2,4,1,0:T(8,128)S(1)} fusion(bf16[3,16,8,128,32]{3,4,2,1,0:T(8,128)(2,1)} %fusion.96, s32[16,8]{0,1:T(8,128)S(1)} %add_select_fusion), kind=kOutput, calls=%fused_computation.42 | convolution fusion | flops 151001088 | bytes 5505536 | tf_op jit(solution)/shard_map/bse,hbskd->hekd/dot_general | solution.py:189
  185.2 7.8 %fusion.53 = f32[3,16,128,32]{2,3,1,0:T(8,128)S(1)} fusion(bf16[3,16,128,8,128]{2,4,3,1,0:T(8,128)(2,1)} %multiply_convert_fusion, bf16[3,16,8,128,32]{3,1,2,4,0:T(8,128)(2,1)S(1)} %copy-done.1), kind=kOutput, calls=%fused_computation.60 | convolution fusion | flops 403046400 | bytes 16515072 | tf_op jit(solution)/shard_map/hbqsk,hbskd->hbqd/dot_general | solution.py:186
  203.1 18.8 %collective-permute-done.6 = bf16[2,3,16,128,32]{3,2,4,1,0:T(8,128)(2,1)} collective-permute-done((bf16[2,3,16,128,32]{3,2,4,1,0:T(8,128)(2,1)}, bf16[2,3,16,128,32]{3,2,4,1,0:T(8,128)(2,1)}, u32[]{:S(2)}, u32[]{:S(2)}) %collective-permute-start.6) | collective-permute-done | bytes 786464 | tf_op jit(solution)/shard_map/ppermute | solution.py:33
  233.8 4.2 %fusion.16 = (f32[384]{0:T(512)S(1)}, bf16[2048,384,1]{1,0,2:T(8,128)(2,1)}) fusion(f32[2048]{0:T(1024)S(1)} %copy-done.33, bf16[1024,384]{1,0:T(8,128)(2,1)S(1)} %copy-done.18, bf16[1024,384]{1,0:T(8,128)(2,1)S(1)} %copy-done.15, bf16[3,384,384]{2,1,0:T(8,128)(2,1)S(1)} %copy-done, s32[]{:T(128)S(6)} %select_n.147, ...), kind=kOutput, calls=%fused_computation.24 | convolution fusion | flops 460455552 | bytes 4630020 | tf_op jit(solution)/shard_map/crk,cdk->rd/dot_general | solution.py:210
  248.3 3.5 %collective-permute-done.10 = bf16[208,384]{1,0:T(8,128)(2,1)S(1)} collective-permute-done((bf16[208,384]{1,0:T(8,128)(2,1)S(1)}, bf16[208,384]{1,0:T(8,128)(2,1)S(1)}, u32[]{:S(2)}, u32[]{:S(2)}) %collective-permute-start.10) | collective-permute-done | bytes 159776 | tf_op jit(solution)/shard_map/ppermute | solution.py:70
  255.5 4.3 %collective-permute-done.12 = bf16[52,384]{1,0:T(8,128)(2,1)S(1)} collective-permute-done((bf16[52,384]{1,0:T(8,128)(2,1)S(1)}, bf16[52,384]{1,0:T(8,128)(2,1)S(1)}, u32[]{:S(2)}, u32[]{:S(2)}) %collective-permute-start.12) | collective-permute-done | bytes 39968 | tf_op jit(solution)/shard_map/ppermute | solution.py:70
  263.9 4.0 %collective-permute-done.14 = bf16[13,384]{1,0:T(8,128)(2,1)S(1)} collective-permute-done((bf16[13,384]{1,0:T(8,128)(2,1)S(1)}, bf16[13,384]{1,0:T(8,128)(2,1)S(1)}, u32[]{:S(2)}, u32[]{:S(2)}) %collective-permute-start.14) | collective-permute-done | bytes 10016 | tf_op jit(solution)/shard_map/ppermute | solution.py:70
  268.0 4.0 %collective-permute-done.15 = bf16[13,384]{1,0:T(8,128)(2,1)S(1)} collective-permute-done((bf16[13,384]{1,0:T(8,128)(2,1)S(1)}, bf16[13,384]{1,0:T(8,128)(2,1)S(1)}, u32[]{:S(2)}, u32[]{:S(2)}) %collective-permute-start.15) | collective-permute-done | bytes 10016 | tf_op jit(solution)/shard_map/ppermute | solution.py:70
  273.9 11.3 %all-to-all-start.2 = ((bf16[4,512,384]{2,1,0:T(8,128)(2,1)}), bf16[4,512,384]{2,1,0:T(8,128)(2,1)S(1)}, u32[]{:S(2)}, u32[]{:S(2)}) async-start(bf16[4,512,384]{2,1,0:T(8,128)(2,1)} %bitcast.306), calls=%async_computation.2 | async-start | bytes 3145728 | tf_op jit(solution)/shard_map/all_to_all | solution.py:219
  285.4 4.3 %collective-permute-done.17 = bf16[52,384]{1,0:T(8,128)(2,1)S(1)} collective-permute-done((bf16[52,384]{1,0:T(8,128)(2,1)S(1)}, bf16[52,384]{1,0:T(8,128)(2,1)S(1)}, u32[]{:S(2)}, u32[]{:S(2)}) %collective-permute-start.17) | collective-permute-done | bytes 39968 | tf_op jit(solution)/shard_map/ppermute | solution.py:70
  290.0 3.5 %collective-permute-done.18 = bf16[104,384]{1,0:T(8,128)(2,1)S(1)} collective-permute-done((bf16[104,384]{1,0:T(8,128)(2,1)S(1)}, bf16[104,384]{1,0:T(8,128)(2,1)S(1)}, u32[]{:S(2)}, u32[]{:S(2)}) %collective-permute-start.18) | collective-permute-done | bytes 79904 | tf_op jit(solution)/shard_map/ppermute | solution.py:70
  298.8 10.7 %collective-permute-done.19 = bf16[208,384]{1,0:T(8,128)(2,1)S(1)} collective-permute-done((bf16[208,384]{1,0:T(8,128)(2,1)S(1)}, bf16[208,384]{1,0:T(8,128)(2,1)S(1)}, u32[]{:S(2)}, u32[]{:S(2)}) %collective-permute-start.19) | collective-permute-done | bytes 159776 | tf_op jit(solution)/shard_map/ppermute | solution.py:70
  (206 shorter events, 91.3 us)
Async XLA Ops:
  0.7 2.3 collective-permute-start
  5.4 18.9 %collective-permute-start.1 = (bf16[1024,384]{1,0:T(8,128)(2,1)}, bf16[1024,384]{1,0:T(8,128)(2,1)S(1)}, u32[]{:S(2)}, u32[]{:S(2)}) collective-permute-start(bf16[1024,384]{1,0:T(8,128)(2,1)} %get-tuple-element.83), channel_id=1, source_target_pairs={{0,2},{1,3},{2,0},{3,1},{4,6},{5,7},{6,4},{7,5},{8,10},{9,11},{10,... | collective-permute-start | bytes 2359304 | tf_op jit(solution)/shard_map/ppermute | solution.py:70
  27.0 60.3 %collective-permute-start.5 = (bf16[3,16,128,32]{2,1,3,0:T(8,128)(2,1)S(1)}, bf16[3,16,128,32]{2,1,3,0:T(8,128)(2,1)S(1)}, u32[]{:S(2)}, u32[]{:S(2)}) collective-permute-start(bf16[3,16,128,32]{2,1,3,0:T(8,128)(2,1)S(1)} %bitcast.307), channel_id=1, source_target_pairs={{4,0},{8,4},{12,8},{16,12},{20,16},{24,20},{28,24},{32,28},{36,32}... | collective-permute-start | bytes 1179656 | tf_op jit(solution)/shard_map/ppermute | solution.py:25
  30.0 57.3 %collective-permute-start.4 = (bf16[3,16,128,32]{2,1,3,0:T(8,128)(2,1)S(1)}, bf16[3,16,128,32]{2,1,3,0:T(8,128)(2,1)S(1)}, u32[]{:S(2)}, u32[]{:S(2)}) collective-permute-start(bf16[3,16,128,32]{2,1,3,0:T(8,128)(2,1)S(1)} %bitcast.308), channel_id=1, source_target_pairs={{0,4},{4,8},{8,12},{12,16},{16,20},{20,24},{24,28},{28,32},{32,36}... | collective-permute-start | bytes 1179656 | tf_op jit(solution)/shard_map/ppermute | solution.py:24
  30.7 24.1 %collective-permute-start.3 = (bf16[3,16,128,32]{2,1,3,0:T(8,128)(2,1)S(1)}, bf16[3,16,128,32]{2,1,3,0:T(8,128)(2,1)S(1)}, u32[]{:S(2)}, u32[]{:S(2)}) collective-permute-start(bf16[3,16,128,32]{2,1,3,0:T(8,128)(2,1)S(1)} %bitcast.311), channel_id=1, source_target_pairs={{4,0},{8,4},{12,8},{16,12},{20,16},{24,20},{28,24},{32,28},{36,32}... | collective-permute-start | bytes 1179656 | tf_op jit(solution)/shard_map/ppermute | solution.py:25
  34.6 28.8 %collective-permute-start.2 = (bf16[3,16,128,32]{2,1,3,0:T(8,128)(2,1)S(1)}, bf16[3,16,128,32]{2,1,3,0:T(8,128)(2,1)S(1)}, u32[]{:S(2)}, u32[]{:S(2)}) collective-permute-start(bf16[3,16,128,32]{2,1,3,0:T(8,128)(2,1)S(1)} %bitcast.312), channel_id=1, source_target_pairs={{0,4},{4,8},{8,12},{12,16},{16,20},{20,24},{24,28},{28,32},{32,36}... | collective-permute-start | bytes 1179656 | tf_op jit(solution)/shard_map/ppermute | solution.py:24
  67.0 35.5 %all-to-all-start.1 = ((bf16[512,4,96]{0,2,1:T(8,128)(2,1)}), bf16[512,4,96]{0,2,1:T(8,128)(2,1)S(1)}, u32[]{:S(2)}, u32[]{:S(2)}) async-start(bf16[512,4,96]{0,2,1:T(8,128)(2,1)} %bitcast.34), calls=%async_computation.1 | async-start | bytes 786432 | tf_op jit(solution)/shard_map/all_to_all | solution.py:181
  102.5 61.2 %all-to-all-start = ((bf16[4,512,96]{1,2,0:T(8,128)(2,1)}), bf16[4,512,96]{1,2,0:T(8,128)(2,1)}, u32[]{:S(2)}, u32[]{:S(2)}) async-start(bf16[4,512,96]{1,2,0:T(8,128)(2,1)} %copy.44), calls=%async_computation | async-start | bytes 786432 | tf_op jit(solution)/shard_map/all_to_all | solution.py:174
  181.3 21.8 %collective-permute-start.7 = (bf16[2,3,16,128,32]{3,2,4,1,0:T(8,128)(2,1)}, bf16[2,3,16,128,32]{3,2,4,1,0:T(8,128)(2,1)}, u32[]{:S(2)}, u32[]{:S(2)}) collective-permute-start(bf16[2,3,16,128,32]{3,2,4,1,0:T(8,128)(2,1)} %get-tuple-element.74), channel_id=1, source_target_pairs={{0,4},{4,8},{8,12},{12,16},{16,20},{20,24},{24,28},{28,32},{32,36}... | collective-permute-start | bytes 2359304 | tf_op jit(solution)/shard_map/ppermute | solution.py:33
  184.1 37.8 %collective-permute-start.6 = (bf16[2,3,16,128,32]{3,2,4,1,0:T(8,128)(2,1)}, bf16[2,3,16,128,32]{3,2,4,1,0:T(8,128)(2,1)}, u32[]{:S(2)}, u32[]{:S(2)}) collective-permute-start(bf16[2,3,16,128,32]{3,2,4,1,0:T(8,128)(2,1)} %get-tuple-element.73), channel_id=1, source_target_pairs={{0,124},{4,0},{8,4},{12,8},{16,12},{20,16},{24,20},{28,24},{32,28}... | collective-permute-start | bytes 2359304 | tf_op jit(solution)/shard_map/ppermute | solution.py:33
  241.3 4.0 %collective-permute-start.9 = (bf16[104,384]{1,0:T(8,128)(2,1)S(1)}, bf16[104,384]{1,0:T(8,128)(2,1)S(1)}, u32[]{:S(2)}, u32[]{:S(2)}) collective-permute-start(bf16[104,384]{1,0:T(8,128)(2,1)S(1)} %fusion.115), channel_id=1, source_target_pairs={{0,2},{1,3},{2,0},{3,1},{4,6},{5,7},{6,4},{7,5},{8,10},{9,11},{10,... | collective-permute-start | bytes 239624 | tf_op jit(solution)/shard_map/ppermute | solution.py:70
  245.5 6.4 %collective-permute-start.10 = (bf16[208,384]{1,0:T(8,128)(2,1)S(1)}, bf16[208,384]{1,0:T(8,128)(2,1)S(1)}, u32[]{:S(2)}, u32[]{:S(2)}) collective-permute-start(bf16[208,384]{1,0:T(8,128)(2,1)S(1)} %fusion.107), channel_id=1, source_target_pairs={{0,4},{4,0},{8,12},{12,8},{16,20},{20,16},{24,28},{28,24},{32,36},... | collective-permute-start | bytes 479240 | tf_op jit(solution)/shard_map/ppermute | solution.py:70
  251.9 3.4 %collective-permute-start.11 = (bf16[104,384]{1,0:T(8,128)(2,1)S(1)}, bf16[104,384]{1,0:T(8,128)(2,1)S(1)}, u32[]{:S(2)}, u32[]{:S(2)}) collective-permute-start(bf16[104,384]{1,0:T(8,128)(2,1)S(1)} %fusion.116), channel_id=1, source_target_pairs={{0,8},{4,12},{8,0},{12,4},{16,24},{20,28},{24,16},{28,20},{32,40},... | collective-permute-start | bytes 239624 | tf_op jit(solution)/shard_map/ppermute | solution.py:70
  255.3 4.5 %collective-permute-start.12 = (bf16[52,384]{1,0:T(8,128)(2,1)S(1)}, bf16[52,384]{1,0:T(8,128)(2,1)S(1)}, u32[]{:S(2)}, u32[]{:S(2)}) collective-permute-start(bf16[52,384]{1,0:T(8,128)(2,1)S(1)} %fusion.130), channel_id=1, source_target_pairs={{0,16},{4,20},{8,24},{12,28},{16,0},{20,4},{24,8},{28,12},{32,48},... | collective-permute-start | bytes 119816 | tf_op jit(solution)/shard_map/ppermute | solution.py:70
  259.9 3.9 %collective-permute-start.13 = (bf16[26,384]{1,0:T(8,128)(2,1)S(1)}, bf16[26,384]{1,0:T(8,128)(2,1)S(1)}, u32[]{:S(2)}, u32[]{:S(2)}) collective-permute-start(bf16[26,384]{1,0:T(8,128)(2,1)S(1)} %fusion.139), channel_id=1, source_target_pairs={{0,32},{4,36},{8,40},{12,44},{16,48},{20,52},{24,56},{28,60},{32,0... | collective-permute-start | bytes 59912 | tf_op jit(solution)/shard_map/ppermute | solution.py:70
  263.8 4.1 %collective-permute-start.14 = (bf16[13,384]{1,0:T(8,128)(2,1)S(1)}, bf16[13,384]{1,0:T(8,128)(2,1)S(1)}, u32[]{:S(2)}, u32[]{:S(2)}) collective-permute-start(bf16[13,384]{1,0:T(8,128)(2,1)S(1)} %fusion.147), channel_id=1, source_target_pairs={{0,64},{4,68},{8,72},{12,76},{16,80},{20,84},{24,88},{28,92},{32,9... | collective-permute-start | bytes 29960 | tf_op jit(solution)/shard_map/ppermute | solution.py:70
  267.9 4.1 %collective-permute-start.15 = (bf16[13,384]{1,0:T(8,128)(2,1)S(1)}, bf16[13,384]{1,0:T(8,128)(2,1)S(1)}, u32[]{:S(2)}, u32[]{:S(2)}) collective-permute-start(bf16[13,384]{1,0:T(8,128)(2,1)S(1)} %fusion.144), channel_id=1, source_target_pairs={{0,64},{4,68},{8,72},{12,76},{16,80},{20,84},{24,88},{28,92},{32,9... | collective-permute-start | bytes 29960 | tf_op jit(solution)/shard_map/ppermute | solution.py:70
  272.1 13.2 %collective-permute-start.16 = (bf16[26,384]{1,0:T(8,128)(2,1)S(1)}, bf16[26,384]{1,0:T(8,128)(2,1)S(1)}, u32[]{:S(2)}, u32[]{:S(2)}) collective-permute-start(bf16[26,384]{1,0:T(8,128)(2,1)S(1)} %get-tuple-element.103), channel_id=1, source_target_pairs={{0,32},{4,36},{8,40},{12,44},{16,48},{20,52},{24,56},{28,60},{32,0... | collective-permute-start | bytes 59912 | tf_op jit(solution)/shard_map/ppermute | solution.py:70
  273.9 40.6 %all-to-all-start.2 = ((bf16[4,512,384]{2,1,0:T(8,128)(2,1)}), bf16[4,512,384]{2,1,0:T(8,128)(2,1)S(1)}, u32[]{:S(2)}, u32[]{:S(2)}) async-start(bf16[4,512,384]{2,1,0:T(8,128)(2,1)} %bitcast.306), calls=%async_computation.2 | async-start | bytes 3145728 | tf_op jit(solution)/shard_map/all_to_all | solution.py:219
  285.3 4.5 %collective-permute-start.17 = (bf16[52,384]{1,0:T(8,128)(2,1)S(1)}, bf16[52,384]{1,0:T(8,128)(2,1)S(1)}, u32[]{:S(2)}, u32[]{:S(2)}) collective-permute-start(bf16[52,384]{1,0:T(8,128)(2,1)S(1)} %pad_maximum_fusion.10), channel_id=1, source_target_pairs={{0,16},{4,20},{8,24},{12,28},{16,0},{20,4},{24,8},{28,12},{32,48},... | collective-permute-start | bytes 119816 | tf_op jit(solution)/shard_map/ppermute | solution.py:70
  289.8 3.6 %collective-permute-start.18 = (bf16[104,384]{1,0:T(8,128)(2,1)S(1)}, bf16[104,384]{1,0:T(8,128)(2,1)S(1)}, u32[]{:S(2)}, u32[]{:S(2)}) collective-permute-start(bf16[104,384]{1,0:T(8,128)(2,1)S(1)} %pad_maximum_fusion.9), channel_id=1, source_target_pairs={{0,8},{4,12},{8,0},{12,4},{16,24},{20,28},{24,16},{28,20},{32,40},... | collective-permute-start | bytes 239624 | tf_op jit(solution)/shard_map/ppermute | solution.py:70
  293.6 15.9 %collective-permute-start.19 = (bf16[208,384]{1,0:T(8,128)(2,1)S(1)}, bf16[208,384]{1,0:T(8,128)(2,1)S(1)}, u32[]{:S(2)}, u32[]{:S(2)}) collective-permute-start(bf16[208,384]{1,0:T(8,128)(2,1)S(1)} %get-tuple-element.95), channel_id=1, source_target_pairs={{0,4},{4,0},{8,12},{12,8},{16,20},{20,16},{24,28},{28,24},{32,36},... | collective-permute-start | bytes 479240 | tf_op jit(solution)/shard_map/ppermute | solution.py:70
  315.0 3.4 %collective-permute-start.20 = (bf16[104,384]{1,0:T(8,128)(2,1)S(1)}, bf16[104,384]{1,0:T(8,128)(2,1)S(1)}, u32[]{:S(2)}, u32[]{:S(2)}) collective-permute-start(bf16[104,384]{1,0:T(8,128)(2,1)S(1)} %slice_bitcast_fusion), channel_id=1, source_target_pairs={{0,2},{1,3},{2,0},{3,1},{4,6},{5,7},{6,4},{7,5},{8,10},{9,11},{10,... | collective-permute-start | bytes 239624 | tf_op jit(solution)/shard_map/ppermute | solution.py:70
  318.5 2.9 collective-permute-start.21
  (39 other events, 370.1 us)

commit v11 on v10

--- a/solution.py
+++ b/solution.py
@@ -166,7 +166,7 @@
         "hbqd,hbskd->hbqsk", q_heads, keys, preferred_element_type=f32
     )
     raised = jnp.exp(scores) * live[None, :, None, :, None]
-    weights = raised / jnp.sum(raised, (-2, -1), keepdims=True)
+    weights = raised * (1.0 / jnp.sum(raised, (-2, -1), keepdims=True))
     weights_bf = weights.astype(bf16)
     attended_heads = jnp.einsum(
         "hbqsk,hbskd->hbqd", weights_bf, values, preferred_element_type=f32

time: 330 us -> 333 us (level)
    unnamed x81 -> x97, local copies, waits for them, and re-layouts: 6.16 us -> 7.57 us
where the time goes in v11:
time: 333 us; the launch traced here: 326 us
  waiting for transfers between devices  106 us (32%)
  matrix products  99.8 us (30%)
  starting transfers between devices  51.6 us (15%)
  other arithmetic  41.2 us (12%)
  local copies, waits for them, and re-layouts  26 us (8%)
    ppermute x16, waiting for transfers between devices, xor_swap(): return lax.ppermute(value, axis, [(i, i ^ mask) for i in range(size)])  61 us
    convert_element_type x1, other arithmetic, local(): d_scores = (exponent_divisor * weights * (d_weights - row_dot)).astype(bf16)  23 us
    ppermute x2, waiting for transfers between devices, passed_along(): return lax.ppermute(value, axis, pairs)  19.5 us
    dot_general x1, matrix products, local(): jnp.einsum('hbqd,hbskd->hbqsk', d_attn, values, preferred_element_type=f32)  19.3 us
    ppermute x16, starting transfers between devices, xor_swap(): return lax.ppermute(value, axis, [(i, i ^ mask) for i in range(size)])  17.3 us
    ppermute x2, waiting for transfers between devices, padded(): after = lax.ppermute(first, axis, down)  16.7 us
    dot_general x1, matrix products, local(): jnp.einsum('hbqd,hbskd->hbqsk', q_heads, keys, preferred_element_type=f32)  14.6 us
    dot_general x1, matrix products, local(): jnp.einsum('hbqsk,hbskd->hbqd', weights_bf, values, preferred_element_typ...  13 us
  transfers between devices with their start and end apart: 25, of which 17 were waited for; matrix products, arithmetic and copies ran while one was open for 37% of the time, Pallas kernels for 0%

profile of v11, /device:TPU:89, one launch (start us, length us, event | category | flops | bytes accessed | tf_op | source)
XLA Modules:
  0.0 326.3 jit_solution(15989957499912618004)
XLA Ops:
  7.8 16.6 %collective-permute-done.1 = bf16[1024,384]{1,0:T(8,128)(2,1)S(1)} collective-permute-done((bf16[1024,384]{1,0:T(8,128)(2,1)}, bf16[1024,384]{1,0:T(8,128)(2,1)S(1)}, u32[]{:S(2)}, u32[]{:S(2)}) %collective-permute-start.1) | collective-permute-done | bytes 786464 | tf_op jit(solution)/shard_map/ppermute | solution.py:70
  31.4 3.9 %collective-permute-start.3 = (bf16[3,16,128,32]{2,1,3,0:T(8,128)(2,1)S(1)}, bf16[3,16,128,32]{2,1,3,0:T(8,128)(2,1)S(1)}, u32[]{:S(2)}, u32[]{:S(2)}) collective-permute-start(bf16[3,16,128,32]{2,1,3,0:T(8,128)(2,1)S(1)} %bitcast.311), channel_id=1, source_target_pairs={{4,0},{8,4},{12,8},{16,12},{20,16},{24,20},{28,24},{32,28},{36,32}... | collective-permute-start | bytes 1179656 | tf_op jit(solution)/shard_map/ppermute | solution.py:25
  38.1 16.7 %collective-permute-done.3 = bf16[3,16,128,32]{2,1,3,0:T(8,128)(2,1)S(1)} collective-permute-done((bf16[3,16,128,32]{2,1,3,0:T(8,128)(2,1)S(1)}, bf16[3,16,128,32]{2,1,3,0:T(8,128)(2,1)S(1)}, u32[]{:S(2)}, u32[]{:S(2)}) %collective-permute-start.3) | collective-permute-done | bytes 393248 | tf_op jit(solution)/shard_map/ppermute | solution.py:25
  54.9 8.6 %collective-permute-done.2 = bf16[3,16,128,32]{2,1,3,0:T(8,128)(2,1)S(1)} collective-permute-done((bf16[3,16,128,32]{2,1,3,0:T(8,128)(2,1)S(1)}, bf16[3,16,128,32]{2,1,3,0:T(8,128)(2,1)S(1)}, u32[]{:S(2)}, u32[]{:S(2)}) %collective-permute-start.2) | collective-permute-done | bytes 393248 | tf_op jit(solution)/shard_map/ppermute | solution.py:24
  67.0 5.7 %all-to-all-start.1 = ((bf16[512,4,96]{0,2,1:T(8,128)(2,1)}), bf16[512,4,96]{0,2,1:T(8,128)(2,1)S(1)}, u32[]{:S(2)}, u32[]{:S(2)}) async-start(bf16[512,4,96]{0,2,1:T(8,128)(2,1)} %bitcast.34), calls=%async_computation.1 | async-start | bytes 786432 | tf_op jit(solution)/shard_map/all_to_all | solution.py:181
  72.8 14.6 %fusion.2 = (f32[3,16,128]{2,1,0:T(8,128)S(1)}, f32[3,16,128,8,128]{2,4,3,1,0:T(8,128)}) fusion(f32[16,8]{1,0:T(8,128)S(1)} %fusion.143, bf16[3,16,8,128,32]{3,1,2,4,0:T(8,128)(2,1)} %convert_bitcast_fusion.1, bf16[16,128,3,32]{1,0,3,2:T(8,128)(2,1)S(1)} %bitcast.295), kind=kOutput, calls=%fused_computation.6 | convolution fusion | flops 421521408 | bytes 28729856 | tf_op jit(solution)/shard_map/hbqd,hbskd->hbqsk/dot_general | solution.py:165
  88.4 13.0 %fusion.48 = bf16[16,128,3,32]{1,3,0,2:T(8,128)(2,1)S(1)} fusion(bf16[3,16,8,128,32]{3,1,2,4,0:T(8,128)(2,1)S(1)} %convert_bitcast_fusion, f32[3,16,128]{2,1,0:T(8,128)S(1)} %broadcast_divide_fusion.2, f32[16,8]{1,0:T(8,128)S(1)} %fusion.143, f32[3,16,128,8,128]{2,4,3,1,0:T(8,128)} %get-tuple-element.110), kind=kOutput, calls=%fused_computation.59 | convolution fusion | flops 428015616 | bytes 28729856 | tf_op jit(solution)/shard_map/hbqsk,hbskd->hbqd/dot_general | solution.py:171
  102.6 4.4 %all-to-all-start = ((bf16[4,512,96]{1,2,0:T(8,128)(2,1)}), bf16[4,512,96]{1,2,0:T(8,128)(2,1)}, u32[]{:S(2)}, u32[]{:S(2)}) async-start(bf16[4,512,96]{1,2,0:T(8,128)(2,1)} %copy.44), calls=%async_computation | async-start | bytes 786432 | tf_op jit(solution)/shard_map/all_to_all | solution.py:174
  107.4 12.0 %fusion.84 = bf16[3,16,8,128,32]{3,4,2,1,0:T(8,128)(2,1)} fusion(bf16[16,128,3,32]{1,0,3,2:T(8,128)(2,1)S(1)} %reshape.274, f32[3,16,128]{2,1,0:T(8,128)S(1)} %broadcast_divide_fusion.2, f32[16,8]{1,0:T(8,128)S(1)} %fusion.143, f32[3,16,128,8,128]{2,4,3,1,0:T(8,128)} %get-tuple-element.110), kind=kOutput, calls=%fused_computation.113 | convolution fusion | flops 427819008 | bytes 28729856 | tf_op jit(solution)/shard_map/hbqsk,hbqd->hbskd/dot_general | solution.py:188
  119.4 19.3 %multiply_reduce_fusion = (f32[3,16,128]{2,1,0:T(8,128)S(1)}, f32[3,16,128,8,128]{2,4,3,1,0:T(8,128)}) fusion(f32[3,16,128]{2,1,0:T(8,128)S(1)} %broadcast_divide_fusion.2, f32[16,8]{1,0:T(8,128)S(1)} %fusion.143, f32[3,16,128,8,128]{2,4,3,1,0:T(8,128)} %get-tuple-element.110, bf16[3,16,8,128,32]{3,1,2,4,0:T(8,128)(2,1)} %copy-done.4, ...), kind=kOutput, calls=%fused_computation.3 | convolution fusion | flops 434104320 | bytes 53920256 | tf_op jit(solution)/shard_map/hbqd,hbskd->hbqsk/dot_general | solution.py:182
  138.7 23.0 %multiply_convert_fusion = bf16[3,16,128,8,128]{2,4,3,1,0:T(8,128)(2,1)} fusion(f32[3,16,128,8,128]{2,4,3,1,0:T(8,128)} %get-tuple-element.112, f32[3,16,128]{2,1,0:T(8,128)S(1)} %get-tuple-element.111, f32[3,16,128]{2,1,0:T(8,128)S(1)} %broadcast_divide_fusion.2, f32[16,8]{1,0:T(8,128)S(1)} %fusion.143, f32[3,16,128,8,128]{2,4,3,1,0:T(8,128)} %get-tuple-element.110), kind=kLoop, calls=%fused_computation.2 | loop fusion | flops 44040192 | bytes 62964224 | tf_op jit(solution)/shard_map/convert_element_type | solution.py:184
  163.9 10.6 %fusion.87 = bf16[3,16,8,128,32]{3,4,2,1,0:T(8,128)(2,1)} fusion(bf16[3,16,128,8,128]{2,4,3,1,0:T(8,128)(2,1)} %multiply_convert_fusion, bf16[16,128,3,32]{1,0,3,2:T(8,128)(2,1)} %bitcast.296), kind=kOutput, calls=%fused_computation.116 | convolution fusion | flops 402653184 | bytes 16121856 | tf_op jit(solution)/shard_map/hbqsk,hbqd->hbskd/dot_general | solution.py:187
  174.5 4.0 %fusion.21 = f32[1,3,48,128,32]{3,2,4,1,0:T(8,128)S(1)} fusion(bf16[3,16,8,128,32]{3,4,2,1,0:T(8,128)(2,1)} %fusion.87, s32[16,8]{0,1:T(8,128)S(1)} %add_select_fusion), kind=kOutput, calls=%fused_computation.39 | convolution fusion | flops 151001088 | bytes 5505536 | tf_op jit(solution)/shard_map/bse,hbskd->hekd/dot_general | solution.py:189
  185.3 7.8 %fusion.42 = f32[3,16,128,32]{2,3,1,0:T(8,128)S(1)} fusion(bf16[3,16,128,8,128]{2,4,3,1,0:T(8,128)(2,1)} %multiply_convert_fusion, bf16[3,16,8,128,32]{3,1,2,4,0:T(8,128)(2,1)S(1)} %copy-done.1), kind=kOutput, calls=%fused_computation.56 | convolution fusion | flops 403046400 | bytes 16515072 | tf_op jit(solution)/shard_map/hbqsk,hbskd->hbqd/dot_general | solution.py:186
  203.3 18.8 %collective-permute-done.6 = bf16[2,3,16,128,32]{3,2,4,1,0:T(8,128)(2,1)} collective-permute-done((bf16[2,3,16,128,32]{3,2,4,1,0:T(8,128)(2,1)}, bf16[2,3,16,128,32]{3,2,4,1,0:T(8,128)(2,1)}, u32[]{:S(2)}, u32[]{:S(2)}) %collective-permute-start.6) | collective-permute-done | bytes 786464 | tf_op jit(solution)/shard_map/ppermute | solution.py:33
  234.0 4.2 %fusion.11 = (f32[384]{0:T(512)S(1)}, bf16[2048,384,1]{1,0,2:T(8,128)(2,1)}) fusion(f32[2048]{0:T(1024)S(1)} %copy-done.40, bf16[1024,384]{1,0:T(8,128)(2,1)S(1)} %copy-done.18, bf16[1024,384]{1,0:T(8,128)(2,1)S(1)} %copy-done.15, bf16[3,384,384]{2,1,0:T(8,128)(2,1)S(1)} %copy-done, s32[]{:T(128)S(6)} %select_n.147, ...), kind=kOutput, calls=%fused_computation.20 | convolution fusion | flops 460455552 | bytes 4630020 | tf_op jit(solution)/shard_map/crk,cdk->rd/dot_general | solution.py:210
  251.5 3.2 collective-permute-done.10
  258.3 4.3 %collective-permute-done.12 = bf16[52,384]{1,0:T(8,128)(2,1)S(1)} collective-permute-done((bf16[52,384]{1,0:T(8,128)(2,1)S(1)}, bf16[52,384]{1,0:T(8,128)(2,1)S(1)}, u32[]{:S(2)}, u32[]{:S(2)}) %collective-permute-start.12) | collective-permute-done | bytes 39968 | tf_op jit(solution)/shard_map/ppermute | solution.py:70
  266.8 4.0 %collective-permute-done.14 = bf16[13,384]{1,0:T(8,128)(2,1)S(1)} collective-permute-done((bf16[13,384]{1,0:T(8,128)(2,1)S(1)}, bf16[13,384]{1,0:T(8,128)(2,1)S(1)}, u32[]{:S(2)}, u32[]{:S(2)}) %collective-permute-start.14) | collective-permute-done | bytes 10016 | tf_op jit(solution)/shard_map/ppermute | solution.py:70
  270.9 4.0 %collective-permute-done.15 = bf16[13,384]{1,0:T(8,128)(2,1)S(1)} collective-permute-done((bf16[13,384]{1,0:T(8,128)(2,1)S(1)}, bf16[13,384]{1,0:T(8,128)(2,1)S(1)}, u32[]{:S(2)}, u32[]{:S(2)}) %collective-permute-start.15) | collective-permute-done | bytes 10016 | tf_op jit(solution)/shard_map/ppermute | solution.py:70
  276.7 11.4 %all-to-all-start.2 = ((bf16[4,512,384]{2,1,0:T(8,128)(2,1)}), bf16[4,512,384]{2,1,0:T(8,128)(2,1)S(1)}, u32[]{:S(2)}, u32[]{:S(2)}) async-start(bf16[4,512,384]{2,1,0:T(8,128)(2,1)} %bitcast.306), calls=%async_computation.2 | async-start | bytes 3145728 | tf_op jit(solution)/shard_map/all_to_all | solution.py:219
  288.3 4.3 %collective-permute-done.17 = bf16[52,384]{1,0:T(8,128)(2,1)S(1)} collective-permute-done((bf16[52,384]{1,0:T(8,128)(2,1)S(1)}, bf16[52,384]{1,0:T(8,128)(2,1)S(1)}, u32[]{:S(2)}, u32[]{:S(2)}) %collective-permute-start.17) | collective-permute-done | bytes 39968 | tf_op jit(solution)/shard_map/ppermute | solution.py:70
  292.9 3.5 %collective-permute-done.18 = bf16[104,384]{1,0:T(8,128)(2,1)S(1)} collective-permute-done((bf16[104,384]{1,0:T(8,128)(2,1)S(1)}, bf16[104,384]{1,0:T(8,128)(2,1)S(1)}, u32[]{:S(2)}, u32[]{:S(2)}) %collective-permute-start.18) | collective-permute-done | bytes 79904 | tf_op jit(solution)/shard_map/ppermute | solution.py:70
  301.8 10.7 %collective-permute-done.19 = bf16[208,384]{1,0:T(8,128)(2,1)S(1)} collective-permute-done((bf16[208,384]{1,0:T(8,128)(2,1)S(1)}, bf16[208,384]{1,0:T(8,128)(2,1)S(1)}, u32[]{:S(2)}, u32[]{:S(2)}) %collective-permute-start.19) | collective-permute-done | bytes 159776 | tf_op jit(solution)/shard_map/ppermute | solution.py:70
  (223 shorter events, 95.6 us)
Async XLA Ops:
  0.7 2.3 collective-permute-start
  5.4 18.9 %collective-permute-start.1 = (bf16[1024,384]{1,0:T(8,128)(2,1)}, bf16[1024,384]{1,0:T(8,128)(2,1)S(1)}, u32[]{:S(2)}, u32[]{:S(2)}) collective-permute-start(bf16[1024,384]{1,0:T(8,128)(2,1)} %get-tuple-element.83), channel_id=1, source_target_pairs={{0,2},{1,3},{2,0},{3,1},{4,6},{5,7},{6,4},{7,5},{8,10},{9,11},{10,... | collective-permute-start | bytes 2359304 | tf_op jit(solution)/shard_map/ppermute | solution.py:70
  27.0 60.4 %collective-permute-start.5 = (bf16[3,16,128,32]{2,1,3,0:T(8,128)(2,1)S(1)}, bf16[3,16,128,32]{2,1,3,0:T(8,128)(2,1)S(1)}, u32[]{:S(2)}, u32[]{:S(2)}) collective-permute-start(bf16[3,16,128,32]{2,1,3,0:T(8,128)(2,1)S(1)} %bitcast.307), channel_id=1, source_target_pairs={{4,0},{8,4},{12,8},{16,12},{20,16},{24,20},{28,24},{32,28},{36,32}... | collective-permute-start | bytes 1179656 | tf_op jit(solution)/shard_map/ppermute | solution.py:25
  30.0 57.4 %collective-permute-start.4 = (bf16[3,16,128,32]{2,1,3,0:T(8,128)(2,1)S(1)}, bf16[3,16,128,32]{2,1,3,0:T(8,128)(2,1)S(1)}, u32[]{:S(2)}, u32[]{:S(2)}) collective-permute-start(bf16[3,16,128,32]{2,1,3,0:T(8,128)(2,1)S(1)} %bitcast.308), channel_id=1, source_target_pairs={{0,4},{4,8},{8,12},{12,16},{16,20},{20,24},{24,28},{28,32},{32,36}... | collective-permute-start | bytes 1179656 | tf_op jit(solution)/shard_map/ppermute | solution.py:24
  31.4 23.4 %collective-permute-start.3 = (bf16[3,16,128,32]{2,1,3,0:T(8,128)(2,1)S(1)}, bf16[3,16,128,32]{2,1,3,0:T(8,128)(2,1)S(1)}, u32[]{:S(2)}, u32[]{:S(2)}) collective-permute-start(bf16[3,16,128,32]{2,1,3,0:T(8,128)(2,1)S(1)} %bitcast.311), channel_id=1, source_target_pairs={{4,0},{8,4},{12,8},{16,12},{20,16},{24,20},{28,24},{32,28},{36,32}... | collective-permute-start | bytes 1179656 | tf_op jit(solution)/shard_map/ppermute | solution.py:25
  35.3 28.2 %collective-permute-start.2 = (bf16[3,16,128,32]{2,1,3,0:T(8,128)(2,1)S(1)}, bf16[3,16,128,32]{2,1,3,0:T(8,128)(2,1)S(1)}, u32[]{:S(2)}, u32[]{:S(2)}) collective-permute-start(bf16[3,16,128,32]{2,1,3,0:T(8,128)(2,1)S(1)} %bitcast.312), channel_id=1, source_target_pairs={{0,4},{4,8},{8,12},{12,16},{16,20},{20,24},{24,28},{28,32},{32,36}... | collective-permute-start | bytes 1179656 | tf_op jit(solution)/shard_map/ppermute | solution.py:24
  67.0 35.5 %all-to-all-start.1 = ((bf16[512,4,96]{0,2,1:T(8,128)(2,1)}), bf16[512,4,96]{0,2,1:T(8,128)(2,1)S(1)}, u32[]{:S(2)}, u32[]{:S(2)}) async-start(bf16[512,4,96]{0,2,1:T(8,128)(2,1)} %bitcast.34), calls=%async_computation.1 | async-start | bytes 786432 | tf_op jit(solution)/shard_map/all_to_all | solution.py:181
  102.6 61.3 %all-to-all-start = ((bf16[4,512,96]{1,2,0:T(8,128)(2,1)}), bf16[4,512,96]{1,2,0:T(8,128)(2,1)}, u32[]{:S(2)}, u32[]{:S(2)}) async-start(bf16[4,512,96]{1,2,0:T(8,128)(2,1)} %copy.44), calls=%async_computation | async-start | bytes 786432 | tf_op jit(solution)/shard_map/all_to_all | solution.py:174
  181.5 21.8 %collective-permute-start.7 = (bf16[2,3,16,128,32]{3,2,4,1,0:T(8,128)(2,1)}, bf16[2,3,16,128,32]{3,2,4,1,0:T(8,128)(2,1)}, u32[]{:S(2)}, u32[]{:S(2)}) collective-permute-start(bf16[2,3,16,128,32]{3,2,4,1,0:T(8,128)(2,1)} %get-tuple-element.74), channel_id=1, source_target_pairs={{0,4},{4,8},{8,12},{12,16},{16,20},{20,24},{24,28},{28,32},{32,36}... | collective-permute-start | bytes 2359304 | tf_op jit(solution)/shard_map/ppermute | solution.py:33
  184.2 37.8 %collective-permute-start.6 = (bf16[2,3,16,128,32]{3,2,4,1,0:T(8,128)(2,1)}, bf16[2,3,16,128,32]{3,2,4,1,0:T(8,128)(2,1)}, u32[]{:S(2)}, u32[]{:S(2)}) collective-permute-start(bf16[2,3,16,128,32]{3,2,4,1,0:T(8,128)(2,1)} %get-tuple-element.73), channel_id=1, source_target_pairs={{0,124},{4,0},{8,4},{12,8},{16,12},{20,16},{24,20},{28,24},{32,28}... | collective-permute-start | bytes 2359304 | tf_op jit(solution)/shard_map/ppermute | solution.py:33
  243.6 3.9 %collective-permute-start.9 = (bf16[104,384]{1,0:T(8,128)(2,1)}, bf16[104,384]{1,0:T(8,128)(2,1)}, u32[]{:S(2)}, u32[]{:S(2)}) collective-permute-start(bf16[104,384]{1,0:T(8,128)(2,1)} %fusion.106), channel_id=1, source_target_pairs={{0,2},{1,3},{2,0},{3,1},{4,6},{5,7},{6,4},{7,5},{8,10},{9,11},{10,... | collective-permute-start | bytes 239624 | tf_op jit(solution)/shard_map/ppermute | solution.py:70
  248.6 6.1 %collective-permute-start.10 = (bf16[208,384]{1,0:T(8,128)(2,1)S(1)}, bf16[208,384]{1,0:T(8,128)(2,1)S(1)}, u32[]{:S(2)}, u32[]{:S(2)}) collective-permute-start(bf16[208,384]{1,0:T(8,128)(2,1)S(1)} %fusion.98), channel_id=1, source_target_pairs={{0,4},{4,0},{8,12},{12,8},{16,20},{20,16},{24,28},{28,24},{32,36},... | collective-permute-start | bytes 479240 | tf_op jit(solution)/shard_map/ppermute | solution.py:70
  254.8 3.4 %collective-permute-start.11 = (bf16[104,384]{1,0:T(8,128)(2,1)S(1)}, bf16[104,384]{1,0:T(8,128)(2,1)S(1)}, u32[]{:S(2)}, u32[]{:S(2)}) collective-permute-start(bf16[104,384]{1,0:T(8,128)(2,1)S(1)} %fusion.107), channel_id=1, source_target_pairs={{0,8},{4,12},{8,0},{12,4},{16,24},{20,28},{24,16},{28,20},{32,40},... | collective-permute-start | bytes 239624 | tf_op jit(solution)/shard_map/ppermute | solution.py:70
  258.2 4.5 %collective-permute-start.12 = (bf16[52,384]{1,0:T(8,128)(2,1)S(1)}, bf16[52,384]{1,0:T(8,128)(2,1)S(1)}, u32[]{:S(2)}, u32[]{:S(2)}) collective-permute-start(bf16[52,384]{1,0:T(8,128)(2,1)S(1)} %fusion.121), channel_id=1, source_target_pairs={{0,16},{4,20},{8,24},{12,28},{16,0},{20,4},{24,8},{28,12},{32,48},... | collective-permute-start | bytes 119816 | tf_op jit(solution)/shard_map/ppermute | solution.py:70
  262.7 3.9 %collective-permute-start.13 = (bf16[26,384]{1,0:T(8,128)(2,1)S(1)}, bf16[26,384]{1,0:T(8,128)(2,1)S(1)}, u32[]{:S(2)}, u32[]{:S(2)}) collective-permute-start(bf16[26,384]{1,0:T(8,128)(2,1)S(1)} %fusion.130), channel_id=1, source_target_pairs={{0,32},{4,36},{8,40},{12,44},{16,48},{20,52},{24,56},{28,60},{32,0... | collective-permute-start | bytes 59912 | tf_op jit(solution)/shard_map/ppermute | solution.py:70
  266.7 4.1 %collective-permute-start.14 = (bf16[13,384]{1,0:T(8,128)(2,1)S(1)}, bf16[13,384]{1,0:T(8,128)(2,1)S(1)}, u32[]{:S(2)}, u32[]{:S(2)}) collective-permute-start(bf16[13,384]{1,0:T(8,128)(2,1)S(1)} %fusion.138), channel_id=1, source_target_pairs={{0,64},{4,68},{8,72},{12,76},{16,80},{20,84},{24,88},{28,92},{32,9... | collective-permute-start | bytes 29960 | tf_op jit(solution)/shard_map/ppermute | solution.py:70
  270.8 4.1 %collective-permute-start.15 = (bf16[13,384]{1,0:T(8,128)(2,1)S(1)}, bf16[13,384]{1,0:T(8,128)(2,1)S(1)}, u32[]{:S(2)}, u32[]{:S(2)}) collective-permute-start(bf16[13,384]{1,0:T(8,128)(2,1)S(1)} %fusion.135), channel_id=1, source_target_pairs={{0,64},{4,68},{8,72},{12,76},{16,80},{20,84},{24,88},{28,92},{32,9... | collective-permute-start | bytes 29960 | tf_op jit(solution)/shard_map/ppermute | solution.py:70
  275.0 13.2 %collective-permute-start.16 = (bf16[26,384]{1,0:T(8,128)(2,1)S(1)}, bf16[26,384]{1,0:T(8,128)(2,1)S(1)}, u32[]{:S(2)}, u32[]{:S(2)}) collective-permute-start(bf16[26,384]{1,0:T(8,128)(2,1)S(1)} %get-tuple-element.103), channel_id=1, source_target_pairs={{0,32},{4,36},{8,40},{12,44},{16,48},{20,52},{24,56},{28,60},{32,0... | collective-permute-start | bytes 59912 | tf_op jit(solution)/shard_map/ppermute | solution.py:70
  276.7 40.8 %all-to-all-start.2 = ((bf16[4,512,384]{2,1,0:T(8,128)(2,1)}), bf16[4,512,384]{2,1,0:T(8,128)(2,1)S(1)}, u32[]{:S(2)}, u32[]{:S(2)}) async-start(bf16[4,512,384]{2,1,0:T(8,128)(2,1)} %bitcast.306), calls=%async_computation.2 | async-start | bytes 3145728 | tf_op jit(solution)/shard_map/all_to_all | solution.py:219
  288.2 4.5 %collective-permute-start.17 = (bf16[52,384]{1,0:T(8,128)(2,1)S(1)}, bf16[52,384]{1,0:T(8,128)(2,1)S(1)}, u32[]{:S(2)}, u32[]{:S(2)}) collective-permute-start(bf16[52,384]{1,0:T(8,128)(2,1)S(1)} %pad_maximum_fusion.10), channel_id=1, source_target_pairs={{0,16},{4,20},{8,24},{12,28},{16,0},{20,4},{24,8},{28,12},{32,48},... | collective-permute-start | bytes 119816 | tf_op jit(solution)/shard_map/ppermute | solution.py:70
  292.7 3.6 %collective-permute-start.18 = (bf16[104,384]{1,0:T(8,128)(2,1)S(1)}, bf16[104,384]{1,0:T(8,128)(2,1)S(1)}, u32[]{:S(2)}, u32[]{:S(2)}) collective-permute-start(bf16[104,384]{1,0:T(8,128)(2,1)S(1)} %pad_maximum_fusion.9), channel_id=1, source_target_pairs={{0,8},{4,12},{8,0},{12,4},{16,24},{20,28},{24,16},{28,20},{32,40},... | collective-permute-start | bytes 239624 | tf_op jit(solution)/shard_map/ppermute | solution.py:70
  296.5 15.9 %collective-permute-start.19 = (bf16[208,384]{1,0:T(8,128)(2,1)S(1)}, bf16[208,384]{1,0:T(8,128)(2,1)S(1)}, u32[]{:S(2)}, u32[]{:S(2)}) collective-permute-start(bf16[208,384]{1,0:T(8,128)(2,1)S(1)} %get-tuple-element.95), channel_id=1, source_target_pairs={{0,4},{4,0},{8,12},{12,8},{16,20},{20,16},{24,28},{28,24},{32,36},... | collective-permute-start | bytes 479240 | tf_op jit(solution)/shard_map/ppermute | solution.py:70
  318.0 3.4 %collective-permute-start.20 = (bf16[104,384]{1,0:T(8,128)(2,1)S(1)}, bf16[104,384]{1,0:T(8,128)(2,1)S(1)}, u32[]{:S(2)}, u32[]{:S(2)}) collective-permute-start(bf16[104,384]{1,0:T(8,128)(2,1)S(1)} %slice_bitcast_fusion), channel_id=1, source_target_pairs={{0,2},{1,3},{2,0},{3,1},{4,6},{5,7},{6,4},{7,5},{8,10},{9,11},{10,... | collective-permute-start | bytes 239624 | tf_op jit(solution)/shard_map/ppermute | solution.py:70
  321.5 2.9 collective-permute-start.21
  (47 other events, 369.8 us)
